TPU v7x, 512 devices: a whole 4x8x8 slice. The times are simulated.
512 devices in a mesh: lat: 64 (over y, x, core), row: 8 (over z).
Axes of the slice: x: 4, y: 8, z: 8, core: 2. Of those that a mesh axis runs over, the one named last changes fastest.
Arguments:
- activations: float32 [12288, 8192], P('lat', 'row'), may hold values from -15 to 15
- center_bias: float32 [8192], P('row'), may hold values from -3 to 3
- encoder_weight: bfloat16 [8192, 16384], P('row', 'lat'), may hold values from -0.0625 to 0.0625
- encoder_bias: float32 [16384], P('lat'), may hold values from -3 to 3
- decoder_weight: bfloat16 [16384, 8192], P('lat', 'row'), may hold values from -1 to 1
- row_blocks: int32 [12288, 4], P('lat'), may hold values from 0 to 127, all different within a row; in each aligned block of 192 rows (0 to 191, 192 to 383, ...) at most 12 rows name the same one
- pick_offsets: int32 [12288, 4, 8], P('lat'), may hold values from 0 to 127
Outputs:
- encoder_grad: bfloat16 [8192, 16384], P('row', 'lat')
- decoder_grad: bfloat16 [16384, 8192], P('lat', 'row')
- bias_grad: float32 [16384], P('lat')
- row_loss: float32 [12288], P('lat')
Inputs may be any that keep to these rules, and one draw needn't show every extreme that they name: `row_blocks`: the 4 blocks of a row differ. Within each group of 192 rows (the rows of one lat index), at most 12 rows name the same block, and in some groups one block is named by exactly 12 rows.
All inputs are finite; a program needn't handle non-finite values.
Results may differ from a plain program's by a relative error of at most 0.006.
Values may be sent and summed in bfloat16 or wider, within the bound.
No kernel may reach another device: no remote copies, remote signals or barrier semaphores. Data moves between devices by JAX's collectives and lax.ppermute only.
A program may use at most 64 MiB of HBM per device.

v0:
```python
import jax
import jax.numpy as jnp
from jax import lax
from jax.sharding import PartitionSpec as P

D = 8192
BLK = 128
KB = 4
PER = 8


def slot_targets(row_blocks, total_blocks, capacity):
    pair_blocks = row_blocks.reshape(-1)
    onehot = (pair_blocks[:, None] == jnp.arange(total_blocks, dtype=jnp.int32)[None, :]).astype(
        jnp.int32
    )
    before = jnp.cumsum(onehot, axis=0) - onehot
    ranking = jnp.sum(before * onehot, axis=1)
    return pair_blocks * capacity + ranking


def per_device(
    activations, center_bias, encoder_weight, encoder_bias, decoder_weight, row_blocks, pick_offsets
):
    group_rows, feature_width = activations.shape
    owners = lax.axis_size("lat")
    owned_blocks = encoder_bias.shape[0] // BLK
    total_blocks = owned_blocks * owners
    capacity = 2 * group_rows * KB // total_blocks
    slot_count = total_blocks * capacity
    target = slot_targets(row_blocks, total_blocks, capacity)
    centered = (activations - center_bias[None, :]).astype(jnp.bfloat16)
    outgoing = (
        jnp.zeros((slot_count, feature_width), jnp.bfloat16)
        .at[target]
        .set(jnp.repeat(centered, KB, axis=0))
    )
    out_offsets = (
        jnp.full((slot_count, PER), -1, jnp.int32).at[target].set(pick_offsets.reshape(-1, PER))
    )
    got_rows, got_offsets = (
        lax.all_to_all(
            outgoing.reshape(owners, -1, feature_width),
            "lat",
            split_axis=0,
            concat_axis=0,
            tiled=True,
        ),
        lax.all_to_all(
            out_offsets.reshape(owners, -1, PER), "lat", split_axis=0, concat_axis=0, tiled=True
        ),
    )
    slot_shape = (owners, owned_blocks, capacity)
    got_rows = got_rows.reshape(slot_shape + (feature_width,))
    got_offsets = got_offsets.reshape(slot_shape + (PER,))
    latent_ids = jnp.arange(BLK, dtype=jnp.int32)
    chosen = jnp.any(got_offsets[..., None] == latent_ids, axis=-2).astype(jnp.float32)
    enc_blocks = encoder_weight.reshape(feature_width, owned_blocks, BLK)
    dec_blocks = decoder_weight.reshape(owned_blocks, BLK, feature_width)
    bias_blocks = encoder_bias.reshape(owned_blocks, BLK)
    partial_pre = jnp.einsum(
        "gcsf,fcl->gcsl", got_rows, enc_blocks, preferred_element_type=jnp.float32
    )
    summed = lax.psum(partial_pre, "row")
    latent = ((summed + bias_blocks[None, :, None, :]) * chosen).astype(jnp.bfloat16)
    decoded = jnp.einsum(
        "gcsl,clf->gcsf", latent, dec_blocks, preferred_element_type=jnp.float32
    ).astype(jnp.bfloat16)
    returned = lax.all_to_all(
        decoded.reshape(owners, -1, feature_width), "lat", split_axis=0, concat_axis=0, tiled=True
    )
    picked = returned.reshape(slot_count, feature_width)[target].astype(jnp.float32)
    rebuilt = center_bias[None, :] + jnp.sum(picked.reshape(group_rows, KB, feature_width), axis=1)
    recon_error = rebuilt - activations
    loss_part = jnp.sum(recon_error * recon_error, axis=1)
    error_b = recon_error.astype(jnp.bfloat16)
    out_error = (
        jnp.zeros((slot_count, feature_width), jnp.bfloat16)
        .at[target]
        .set(jnp.repeat(error_b, KB, axis=0))
    )
    got_error = lax.all_to_all(
        out_error.reshape(owners, -1, feature_width), "lat", split_axis=0, concat_axis=0, tiled=True
    )
    got_error = got_error.reshape(slot_shape + (feature_width,))
    decoder_grad = jnp.einsum(
        "gcsl,gcsf->clf", latent, got_error, preferred_element_type=jnp.float32
    )
    decoder_grad = decoder_grad.astype(jnp.bfloat16).reshape(owned_blocks * BLK, feature_width)
    dlatent_part = jnp.einsum(
        "gcsf,clf->gcsl", got_error, dec_blocks, preferred_element_type=jnp.float32
    )
    dlatent, loss_total = lax.psum((dlatent_part, loss_part), "row")
    grad_pre = (dlatent * chosen).astype(jnp.bfloat16)
    encoder_grad = jnp.einsum(
        "gcsf,gcsl->fcl", got_rows, grad_pre, preferred_element_type=jnp.float32
    )
    encoder_grad = encoder_grad.astype(jnp.bfloat16).reshape(feature_width, owned_blocks * BLK)
    bias_grad = jnp.sum(grad_pre.astype(jnp.float32), axis=(0, 2)).reshape(owned_blocks * BLK)
    row_loss = loss_total / D
    return (encoder_grad, decoder_grad, bias_grad, row_loss)


def solution(mesh):
    return jax.shard_map(
        per_device,
        mesh=mesh,
        in_specs=(
            P("lat", "row"),
            P("row"),
            P("row", "lat"),
            P("lat"),
            P("lat", "row"),
            P("lat", None),
            P("lat", None, None),
        ),
        out_specs=(P("row", "lat"), P("lat", "row"), P("lat"), P("lat")),
        check_vma=False,
    )
```

profile of v0, /device:TPU:6, one launch (start us, length us, event | category | flops | bytes accessed | tf_op | source)
XLA Modules:
  0.0 441.3 jit_solution(8325516000080497305)
XLA Ops:
  10.3 1.8 reshape.143
  12.5 8.5 %scatter_custom_fusion.1 = bf16[1536,1024]{1,0:T(8,128)(2,1)} fusion(s32[768]{0:T(1024)S(1)} %fusion.16, bf16[768,1024]{1,0:T(8,128)(2,1)} %reshape.143, bf16[]{:T(256)} %constant.21.clone.1), kind=kCustom, calls=%fused_computation.9 | custom fusion | bytes 3146240 | tf_op jit(solution)/shard_map/scatter | solution.py:36
  21.0 10.9 %all-to-all-start.1 = ((bf16[64,24,1024]{2,1,0:T(8,128)(2,1)}), bf16[64,24,1024]{2,1,0:T(8,128)(2,1)}, u32[]{:S(2)}, u32[]{:S(2)}) async-start(bf16[64,24,1024]{2,1,0:T(8,128)(2,1)} %bitcast.62), calls=%async_computation.1 | async-start | bytes 6291456 | tf_op jit(solution)/shard_map/all_to_all | solution.py:42
  32.1 73.6 %all-to-all-done.1 = bf16[64,24,1024]{2,1,0:T(8,128)(2,1)} async-done(((bf16[64,24,1024]{2,1,0:T(8,128)(2,1)}), bf16[64,24,1024]{2,1,0:T(8,128)(2,1)}, u32[]{:S(2)}, u32[]{:S(2)}) %all-to-all-start.1) | async-done | bytes 3145760 | tf_op jit(solution)/shard_map/all_to_all | solution.py:42
  105.7 3.6 copy.78
  111.0 1.9 convolution_bitcast_fusion.3
  113.1 4.5 %scatter_custom_fusion = s32[1536,8]{1,0:T(8,128)S(1)} fusion(s32[768]{0:T(1024)S(1)} %fusion.16, s32[768,8]{1,0:T(8,128)S(1)} %bitcast.72, s32[]{:T(128)} %constant.8.clone.1), kind=kCustom, calls=%fused_computation.31 | custom fusion | bytes 49156 | tf_op jit(solution)/shard_map/scatter | solution.py:39
  118.1 13.2 %all_to_all.20 = s32[64,1,192]{2,1,0:T(1,128)S(1)} all-to-all(s32[64,1,192]{2,1,0:T(1,128)S(1)} %reshape.166), channel_id=1, replica_groups=mesh['lat'=64,'row'=8] {'lat'}, dimensions={0} | all-to-all | bytes 98304 | tf_op jit(solution)/shard_map/all_to_all | solution.py:49
  133.9 2.6 fusion
  136.5 56.7 %all-reduce.4.cloned.1.call-done = f32[64,2,12,128]{3,0,2,1:T(8,128)} async-done(((f32[64,2,12,128]{3,0,2,1:T(8,128)}), f32[64,2,12,128]{3,0,2,1:T(8,128)}) %all-reduce.4.cloned.1.call-update) | async-done | bytes 786448 | tf_op jit(solution)/shard_map/psum | solution.py:64
  193.2 2.1 convolution_convert_fusion
  195.3 3.4 copy.81
  198.8 10.4 %all-to-all-start.2 = ((bf16[64,24,1024]{2,1,0:T(8,128)(2,1)}), bf16[64,24,1024]{2,1,0:T(8,128)(2,1)}, u32[]{:S(2)}, u32[]{:S(2)}) async-start(bf16[64,24,1024]{2,1,0:T(8,128)(2,1)} %copy.81), calls=%async_computation.2 | async-start | bytes 6291456 | tf_op jit(solution)/shard_map/all_to_all | solution.py:69
  209.2 73.7 %all-to-all-done.2 = bf16[64,24,1024]{2,1,0:T(8,128)(2,1)} async-done(((bf16[64,24,1024]{2,1,0:T(8,128)(2,1)}), bf16[64,24,1024]{2,1,0:T(8,128)(2,1)}, u32[]{:S(2)}, u32[]{:S(2)}) %all-to-all-start.2) | async-done | bytes 3145760 | tf_op jit(solution)/shard_map/all_to_all | solution.py:69
  282.9 6.1 %gather_fusion = bf16[768,1024]{1,0:T(8,128)(2,1)S(1)} fusion(bf16[1536,1024]{1,0:T(8,128)(2,1)} %bitcast.16, s32[1024]{0:T(1024)S(1)} %pad_clamp_fusion), kind=kCustom, calls=%fused_computation | custom fusion | bytes 3148800 | tf_op jit(solution)/shard_map/gather | solution.py:72
  289.0 2.7 reshape.122
  291.7 3.8 reduce_sum.40
  296.2 1.9 reshape.151
  298.0 8.6 %scatter_custom_fusion.2 = bf16[1536,1024]{1,0:T(8,128)(2,1)} fusion(s32[768]{0:T(1024)S(1)} %fusion.16, bf16[768,1024]{1,0:T(8,128)(2,1)} %reshape.151, bf16[]{:T(256)} %constant.21.clone.1), kind=kCustom, calls=%fused_computation.7 | custom fusion | bytes 3146240 | tf_op jit(solution)/shard_map/scatter | solution.py:80
  306.6 79.1 %all_to_all.21 = bf16[64,24,1024]{2,1,0:T(8,128)(2,1)S(1)} all-to-all(bf16[64,24,1024]{2,1,0:T(8,128)(2,1)} %bitcast.63), channel_id=1, replica_groups=mesh['lat'=64,'row'=8] {'lat'}, dimensions={0} | all-to-all | bytes 6291456 | tf_op jit(solution)/shard_map/all_to_all | solution.py:82
  385.7 1.7 copy.82
  390.1 36.1 %all-reduce.5 = (bf16[64,2,12,128]{3,0,2,1:T(8,128)(2,1)S(1)}, f32[192]{0:T(256)S(1)}) all-reduce(f32[64,2,12,128]{3,0,2,1:T(8,128)S(1)} %convolution_bitcast_fusion.2, f32[192]{0:T(256)S(1)} %get-tuple-element.30), channel_id=1, replica_groups=mesh['lat'=64,'row'=8] {'row'}, use_global_device_ids=true, to_apply=%region_9.10 | all-reduce | flops 196800 | bytes 1181184 | tf_op jit(solution)/shard_map/psum | solution.py:93
  426.2 2.6 fusion.5
  431.1 3.3 fusion.6
  (52 shorter events, 14.0 us)
Async XLA Ops:
  7.2 186.1 %copy-start = (bf16[256,1024]{1,0:T(8,128)(2,1)S(1)}, bf16[256,1024]{1,0:T(8,128)(2,1)}, u32[]{:S(2)}) copy-start(bf16[256,1024]{1,0:T(8,128)(2,1)} %param.11) | copy-start | bytes 1572868
  7.2 2.6 copy-start.3
  7.2 2.6 copy-start.7
  21.0 11.0 %copy-start.5 = (bf16[1024,256]{1,0:T(8,128)(2,1)S(1)}, bf16[1024,256]{1,0:T(8,128)(2,1)}, u32[]{:S(2)}) copy-start(bf16[1024,256]{1,0:T(8,128)(2,1)} %param.9) | copy-start | bytes 1572868
  21.0 84.7 %all-to-all-start.1 = ((bf16[64,24,1024]{2,1,0:T(8,128)(2,1)}), bf16[64,24,1024]{2,1,0:T(8,128)(2,1)}, u32[]{:S(2)}, u32[]{:S(2)}) async-start(bf16[64,24,1024]{2,1,0:T(8,128)(2,1)} %bitcast.62), calls=%async_computation.1 | async-start | bytes 6291456 | tf_op jit(solution)/shard_map/all_to_all | solution.py:42
  31.9 161.3 %all-reduce.4.cloned.1.call-start = ((), (), s32[]{:S(2)}) async-start(), calls=%async_computation.4 | async-start | bytes 1572864 | tf_op jit(solution)/shard_map/psum | solution.py:64
  109.3 1.7 copy-start.1
  109.3 3.6 copy-start.6
  112.9 80.3 %copy-start.8 = (f32[256]{0:T(256)S(1)}, f32[256]{0:T(256)}, u32[]{:S(2)}) copy-start(f32[256]{0:T(256)} %param.10) | copy-start | bytes 3076
  198.8 84.1 %all-to-all-start.2 = ((bf16[64,24,1024]{2,1,0:T(8,128)(2,1)}), bf16[64,24,1024]{2,1,0:T(8,128)(2,1)}, u32[]{:S(2)}, u32[]{:S(2)}) async-start(bf16[64,24,1024]{2,1,0:T(8,128)(2,1)} %copy.81), calls=%async_computation.2 | async-start | bytes 6291456 | tf_op jit(solution)/shard_map/all_to_all | solution.py:69
  387.4 1.7 copy-start.2
  426.2 4.9 %copy-start.4 = (f32[64,2,12,128]{3,0,2,1:T(8,128)S(1)}, f32[64,2,12,128]{3,0,2,1:T(8,128)}, u32[]{:S(2)}) copy-start(f32[64,2,12,128]{3,0,2,1:T(8,128)} %all-reduce.4.cloned.1.call-done) | copy-start | bytes 2359300
Sparse Core Ops, SparseCore 0:
  113.0 80.1 all-reduce.3
where the time goes:
time: 443 us; the launch traced here: 441 us
  waiting for transfers between devices  204 us (46%)
  blocking collectives  128 us (29%)
  local copies, waits for them, and re-layouts  52.2 us (12%)
  starting transfers between devices  21.4 us (5%)
  between operations  14.4 us (3%)
  matrix products  10.9 us (2%)
  other arithmetic  10 us (2%)
    all_to_all x1, blocking collectives, per_device(): lax.all_to_all(out_error.reshape(owners, -1, feature_width), 'lat', split...  79.1 us
    all_to_all x1, waiting for transfers between devices, per_device(): lax.all_to_all(decoded.reshape(owners, -1, feature_width), 'lat', split_a...  73.7 us
    all_to_all x1, waiting for transfers between devices, per_device(): lax.all_to_all(outgoing.reshape(owners, -1, feature_width), 'lat', split_...  73.6 us
    psum x1, waiting for transfers between devices, per_device(): summed = lax.psum(partial_pre, 'row')  56.7 us
    psum x1, blocking collectives, per_device(): dlatent, loss_total = lax.psum((dlatent_part, loss_part), 'row')  36.1 us
    all_to_all x1, blocking collectives, per_device(): lax.all_to_all(out_offsets.reshape(owners, -1, PER), 'lat', split_axis=0,...  13.2 us
    all_to_all x1, starting transfers between devices, per_device(): lax.all_to_all(outgoing.reshape(owners, -1, feature_width), 'lat', split_...  10.9 us
    all_to_all x1, starting transfers between devices, per_device(): lax.all_to_all(decoded.reshape(owners, -1, feature_width), 'lat', split_a...  10.4 us
  transfers between devices with their start and end apart: 3, of which 3 were waited for; matrix products, arithmetic and copies ran while one was open for 2% of the time, Pallas kernels for 0%

commit v1 on v0

v1 whole, which is shorter than its diff:
```python
import jax
import jax.numpy as jnp
from jax import lax
from jax.sharding import PartitionSpec as P

D = 8192
BLK = 128
KB = 4
PER = 8


def slot_targets(row_blocks, total_blocks, capacity):
    pair_blocks = row_blocks.reshape(-1)
    onehot = (pair_blocks[:, None] == jnp.arange(total_blocks, dtype=jnp.int32)[None, :]).astype(
        jnp.int32
    )
    before = jnp.cumsum(onehot, axis=0) - onehot
    ranking = jnp.sum(before * onehot, axis=1)
    return pair_blocks * capacity + ranking


def pick_columns(values, offsets):
    lanes = jnp.arange(BLK, dtype=jnp.int32)
    hit = offsets[:, :, None] == lanes[None, None, :]
    return jnp.sum(jnp.where(hit, values[:, None, :], 0.0), axis=2)


def spread_columns(picked, offsets):
    lanes = jnp.arange(BLK, dtype=jnp.int32)[None, :]
    out = jnp.zeros((picked.shape[0], BLK), picked.dtype)
    for j in range(PER):
        out = jnp.where(offsets[:, j : j + 1] == lanes, picked[:, j : j + 1], out)
    return out


def per_device(
    activations, center_bias, encoder_weight, encoder_bias, decoder_weight, row_blocks, pick_offsets
):
    group_rows, feature_width = activations.shape
    owners = lax.axis_size("lat")
    owned_blocks = encoder_bias.shape[0] // BLK
    total_blocks = owned_blocks * owners
    capacity = 2 * group_rows * KB // total_blocks
    slot_count = total_blocks * capacity
    per_owner = owned_blocks * capacity
    target = slot_targets(row_blocks, total_blocks, capacity)
    slots = jnp.arange(slot_count, dtype=jnp.int32)

    pair_hot = target[None, :] == slots[:, None]
    row_hot = jnp.any(pair_hot.reshape(slot_count, group_rows, KB), axis=2).astype(jnp.bfloat16)
    pair_hot = pair_hot.astype(jnp.bfloat16)

    centered = (activations - center_bias[None, :]).astype(jnp.bfloat16)
    outgoing = jnp.dot(row_hot, centered, preferred_element_type=jnp.float32).astype(jnp.bfloat16)
    offs_plus = (pick_offsets.reshape(-1, PER) + 1).astype(jnp.bfloat16)
    out_offs = jnp.dot(pair_hot, offs_plus, preferred_element_type=jnp.float32).astype(jnp.int32)

    got_offs = lax.all_to_all(
        out_offs.reshape(owners, per_owner, PER), "lat", split_axis=0, concat_axis=0, tiled=True
    )
    got_rows = lax.all_to_all(
        outgoing.reshape(owners, per_owner, feature_width),
        "lat",
        split_axis=0,
        concat_axis=0,
        tiled=True,
    )
    got_rows = got_rows.reshape(slot_count, feature_width)
    offs = got_offs.reshape(slot_count, PER) - 1

    slot_block = (slots // capacity) % owned_blocks
    col_block = jnp.arange(owned_blocks * BLK, dtype=jnp.int32) // BLK
    own_col = slot_block[:, None] == col_block[None, :]

    def own_half(full):
        parts = full.reshape(slot_count, owned_blocks, BLK)
        sel = slot_block[:, None, None] == jnp.arange(owned_blocks, dtype=jnp.int32)[None, :, None]
        return jnp.sum(jnp.where(sel, parts, 0.0), axis=1)

    def widen(narrow):
        tiled = jnp.tile(narrow, (1, owned_blocks))
        return jnp.where(own_col, tiled, jnp.zeros_like(tiled))

    partial_full = jnp.dot(got_rows, encoder_weight, preferred_element_type=jnp.float32)
    partial = pick_columns(own_half(partial_full), offs)
    summed = lax.psum(partial, "row")
    bias_rows = own_half(jnp.broadcast_to(encoder_bias[None, :], (slot_count, owned_blocks * BLK)))
    pre_picked = summed + pick_columns(bias_rows, offs)
    latent = spread_columns(pre_picked, offs).astype(jnp.bfloat16)
    latent_wide = widen(latent)
    decoded = jnp.dot(latent_wide, decoder_weight, preferred_element_type=jnp.float32).astype(
        jnp.bfloat16
    )
    returned = lax.all_to_all(
        decoded.reshape(owners, per_owner, feature_width),
        "lat",
        split_axis=0,
        concat_axis=0,
        tiled=True,
    ).reshape(slot_count, feature_width)
    rebuilt = lax.dot_general(
        row_hot, returned, (((0,), (0,)), ((), ())), preferred_element_type=jnp.float32
    )
    recon_error = (center_bias[None, :] + rebuilt) - activations
    loss_part = jnp.sum(recon_error * recon_error, axis=1)
    error_b = recon_error.astype(jnp.bfloat16)
    out_error = jnp.dot(row_hot, error_b, preferred_element_type=jnp.float32).astype(jnp.bfloat16)
    got_error = lax.all_to_all(
        out_error.reshape(owners, per_owner, feature_width),
        "lat",
        split_axis=0,
        concat_axis=0,
        tiled=True,
    ).reshape(slot_count, feature_width)
    decoder_grad = lax.dot_general(
        latent_wide, got_error, (((0,), (0,)), ((), ())), preferred_element_type=jnp.float32
    ).astype(jnp.bfloat16)
    dlatent_full = lax.dot_general(
        got_error, decoder_weight, (((1,), (1,)), ((), ())), preferred_element_type=jnp.float32
    )
    dlatent_part = pick_columns(own_half(dlatent_full), offs)
    dlatent, loss_total = lax.psum((dlatent_part, loss_part), "row")
    grad_pre = spread_columns(dlatent, offs).astype(jnp.bfloat16)
    grad_wide = widen(grad_pre)
    encoder_grad = lax.dot_general(
        got_rows, grad_wide, (((0,), (0,)), ((), ())), preferred_element_type=jnp.float32
    ).astype(jnp.bfloat16)
    bias_grad = jnp.sum(grad_wide.astype(jnp.float32), axis=0)
    row_loss = loss_total / D
    return (encoder_grad, decoder_grad, bias_grad, row_loss)


def solution(mesh):
    return jax.shard_map(
        per_device,
        mesh=mesh,
        in_specs=(
            P("lat", "row"),
            P("row"),
            P("row", "lat"),
            P("lat"),
            P("lat", "row"),
            P("lat", None),
            P("lat", None, None),
        ),
        out_specs=(P("row", "lat"), P("lat", "row"), P("lat"), P("lat")),
        check_vma=False,
    )
```

time: 443 us -> 399 us (0.901)
  waiting for transfers between devices: 204 us -> 148 us
  local copies, waits for them, and re-layouts: 52.2 us -> 11.3 us
  blocking collectives: 128 us -> 159 us
  other arithmetic: 10 us -> 31.3 us
  between operations: 14.4 us -> 1.03 us
  matrix products: 10.9 us -> 23.9 us
    psum x1 -> x0, waiting for transfers between devices: 56.7 us -> none  [per_device(): summed = lax.psum(partial_pre, 'row')]
    psum x0 -> x1, blocking collectives: none -> 42.3 us  [per_device(): summed = lax.psum(partial, 'row')]
    scatter x3 -> x0, local copies, waits for them, and re-layouts: 21.6 us -> none  [the longest x1 8.55 us: per_device(): out_error = jnp.zeros((slot_count, feature_width), jnp.bfloat16).at[targe...]
    dot_general x5 -> x9, matrix products: 10.9 us -> 23.9 us  [the longest x1 3.98 us: per_device(): lax.dot_general(got_error, decoder_weight, (((1,), (1,)), ((), ())), pref...]
    all_to_all x2 -> x1, blocking collectives: 92.4 us -> 80.9 us  [per_device(): lax.all_to_all(decoded.reshape(owners, per_owner, feature_width), 'lat',...]
    reduce_sum x3 -> x4, other arithmetic: 4.73 us -> 14.8 us  [the longest x2 13.3 us: pick_columns(): return jnp.sum(jnp.where(hit, values[:, None, :], 0.0), axis=2)]
    convert_element_type x1 -> x3, other arithmetic: 0.06 us -> 7.52 us  [the longest x1 3.76 us: per_device(): latent = spread_columns(pre_picked, offs).astype(jnp.bfloat16)]
    reshape x5 -> x2, local copies, waits for them, and re-layouts: 7.49 us -> 0.33 us  [per_device(): out_offs.reshape(owners, per_owner, PER)]
where the time goes in v1:
time: 399 us; the launch traced here: 398 us
  blocking collectives  159 us (40%)
  waiting for transfers between devices  148 us (37%)
  other arithmetic  31.3 us (8%)
  starting transfers between devices  24 us (6%)
  matrix products  23.9 us (6%)
  local copies, waits for them, and re-layouts  11.3 us (3%)
    all_to_all x1, blocking collectives, per_device(): lax.all_to_all(decoded.reshape(owners, per_owner, feature_width), 'lat',...  80.9 us
    all_to_all x1, waiting for transfers between devices, per_device(): lax.all_to_all(out_error.reshape(owners, per_owner, feature_width), 'lat'...  73.7 us
    all_to_all x1, waiting for transfers between devices, per_device(): lax.all_to_all(outgoing.reshape(owners, per_owner, feature_width), 'lat',...  70.5 us
    psum x1, blocking collectives, per_device(): summed = lax.psum(partial, 'row')  42.3 us
    psum x1, blocking collectives, per_device(): dlatent, loss_total = lax.psum((dlatent_part, loss_part), 'row')  35.4 us
    reduce_sum x2, other arithmetic, pick_columns(): return jnp.sum(jnp.where(hit, values[:, None, :], 0.0), axis=2)  13.3 us
    all_to_all x1, starting transfers between devices, per_device(): lax.all_to_all(out_offs.reshape(owners, per_owner, PER), 'lat', split_axi...  10.6 us
  transfers between devices with their start and end apart: 3, of which 3 were waited for; matrix products, arithmetic and copies ran while one was open for 2% of the time, Pallas kernels for 0%

profile of v1, /device:TPU:6, one launch (start us, length us, event | category | flops | bytes accessed | tf_op | source)
XLA Modules:
  0.0 398.1 jit_solution(482381687215918004)
XLA Ops:
  4.9 10.6 %all-to-all-start.1 = ((s32[64,1,192]{2,1,0:T(1,128)}), s32[64,1,192]{2,1,0:T(1,128)S(1)}, u32[]{:S(2)}, u32[]{:S(2)}) async-start(s32[64,1,192]{2,1,0:T(1,128)} %reshape.842), calls=%async_computation.1 | async-start | bytes 131072 | tf_op jit(solution)/shard_map/all_to_all | solution.py:58
  16.7 2.8 convolution_convert_fusion.2
  19.5 4.0 all-to-all-done.1
  23.5 7.6 %all-to-all-start = ((bf16[64,24,1024]{2,1,0:T(8,128)(2,1)}), bf16[64,24,1024]{2,1,0:T(8,128)(2,1)}, u32[]{:S(2)}, u32[]{:S(2)}) async-start(bf16[64,24,1024]{2,1,0:T(8,128)(2,1)} %bitcast.63), calls=%async_computation | async-start | bytes 6291456 | tf_op jit(solution)/shard_map/all_to_all | solution.py:61
  34.4 70.5 %all-to-all-done = bf16[64,24,1024]{2,1,0:T(8,128)(2,1)} async-done(((bf16[64,24,1024]{2,1,0:T(8,128)(2,1)}), bf16[64,24,1024]{2,1,0:T(8,128)(2,1)}, u32[]{:S(2)}, u32[]{:S(2)}) %all-to-all-start) | async-done | bytes 3145760 | tf_op jit(solution)/shard_map/all_to_all | solution.py:61
  104.9 4.0 fusion.4
  108.8 8.5 %select_reduce_fusion.1 = (f32[1536,8]{1,0:T(8,128)}, f32[1536,8]{1,0:T(8,128)S(1)}) fusion(f32[1536,128]{1,0:T(8,128)S(1)} %select_reduce_fusion.3, s32[1536,8]{1,0:T(8,128)S(1)} %copy.55, f32[1536,128]{1,0:T(8,128)S(1)} %fusion.4), kind=kLoop, calls=%fused_computation.1 | loop fusion | flops 7839744 | bytes 1720320 | tf_op jit(solution)/shard_map/reduce_sum | solution.py:25
  117.3 42.3 %psum.21 = f32[1536,8]{1,0:T(8,128)S(1)} all-reduce(f32[1536,8]{1,0:T(8,128)S(1)} %get-tuple-element.21), channel_id=1, replica_groups=mesh['lat'=64,'row'=8] {'row'}, use_global_device_ids=true, to_apply=%region_6.7 | all-reduce | flops 12288 | bytes 98304 | tf_op jit(solution)/shard_map/psum | solution.py:86
  159.6 1.2 add.87
  160.8 3.1 slice_reduce_fusion.15
  163.9 3.8 select_convert_fusion.1
  168.2 1.0 convolution_convert_fusion.1
  169.2 80.9 %all_to_all.20 = bf16[64,24,1024]{2,1,0:T(8,128)(2,1)S(1)} all-to-all(bf16[64,24,1024]{2,1,0:T(8,128)(2,1)S(1)} %bitcast.66), channel_id=1, replica_groups=mesh['lat'=64,'row'=8] {'lat'}, dimensions={0} | all-to-all | bytes 6291456 | tf_op jit(solution)/shard_map/all_to_all | solution.py:94
  251.1 2.8 convolution_convert_fusion
  253.9 5.8 %all-to-all-start.3 = ((bf16[64,24,1024]{2,1,0:T(8,128)(2,1)}), bf16[64,24,1024]{2,1,0:T(8,128)(2,1)}, u32[]{:S(2)}, u32[]{:S(2)}) async-start(bf16[64,24,1024]{2,1,0:T(8,128)(2,1)} %bitcast.64), calls=%async_computation.3 | async-start | bytes 6291456 | tf_op jit(solution)/shard_map/all_to_all | solution.py:108
  259.7 73.7 %all-to-all-done.3 = bf16[64,24,1024]{2,1,0:T(8,128)(2,1)} async-done(((bf16[64,24,1024]{2,1,0:T(8,128)(2,1)}), bf16[64,24,1024]{2,1,0:T(8,128)(2,1)}, u32[]{:S(2)}, u32[]{:S(2)}) %all-to-all-start.3) | async-done | bytes 3145760 | tf_op jit(solution)/shard_map/all_to_all | solution.py:108
  333.4 4.0 fusion.5
  337.3 4.8 %select_reduce_fusion = f32[1536,8]{1,0:T(8,128)S(1)} fusion(f32[1536,128]{1,0:T(8,128)S(1)} %fusion.5, s32[1536,8]{1,0:T(8,128)S(1)} %copy.55), kind=kLoop, calls=%fused_computation | loop fusion | flops 4706304 | bytes 884736 | tf_op jit(solution)/shard_map/reduce_sum | solution.py:25
  342.2 35.4 %all-reduce = (f32[1536,8]{1,0:T(8,128)S(1)}, f32[192]{0:T(256)S(1)}) all-reduce(f32[1536,8]{1,0:T(8,128)S(1)} %select_reduce_fusion, f32[192]{0:T(256)S(1)} %get-tuple-element.34), channel_id=1, replica_groups=mesh['lat'=64,'row'=8] {'row'}, use_global_device_ids=true, to_apply=%region_11.12 | all-reduce | flops 12480 | bytes 99840 | tf_op jit(solution)/shard_map/psum | solution.py:122
  377.6 3.1 slice_reduce_fusion.7
  380.7 3.8 select_convert_fusion
  384.5 4.8 %compare_select_fusion = (bf16[1536,2,128]{2,1,0:T(2,128)(2,1)S(1)}, bf16[1536,2,128]{2,1,0:T(2,128)(2,1)S(1)}) fusion(s32[2,128]{1,0:T(2,128)S(1)} %and_select_fusion.1, s32[1536]{0:T(1024)S(1)} %add_select_fusion, bf16[1536,128]{1,0:T(8,128)(2,1)S(1)} %select_convert_fusion.1, bf16[1536,128]{1,0:T(8,128)(2,1)S(1)} %select_convert_fusion), kind=kLoop, calls=%fused_computation.11 | loop fusion | flops 1179648 | bytes 2366464 | tf_op jit(solution)/shard_map/jit(_where)/select_n | solution.py:82
  390.7 3.7 convolution_convert_fusion.3
  394.4 3.7 convolution_convert_fusion.4
  (56 shorter events, 11.3 us)
Async XLA Ops:
  0.6 167.5 %copy-start = (bf16[256,1024]{1,0:T(8,128)(2,1)S(1)}, bf16[256,1024]{1,0:T(8,128)(2,1)}, u32[]{:S(2)}) copy-start(bf16[256,1024]{1,0:T(8,128)(2,1)} %param.11) | copy-start | bytes 1572868
  0.6 1.9 copy-start.4
  1.5 14.2 %copy-start.5 = (s32[192,4]{0,1:T(4,128)S(1)}, s32[192,4]{0,1:T(4,128)}, u32[]{:S(2)}) copy-start(s32[192,4]{0,1:T(4,128)} %param.12) | copy-start | bytes 9220
  1.9 14.9 %copy-start.1 = (f32[192,1024]{1,0:T(8,128)S(1)}, f32[192,1024]{1,0:T(8,128)}, u32[]{:S(2)}) copy-start(f32[192,1024]{1,0:T(8,128)} %param.7) | copy-start | bytes 2359300
  1.9 14.9 %copy-start.6 = (f32[1024]{0:T(1024)S(1)}, f32[1024]{0:T(1024)}, u32[]{:S(2)}) copy-start(f32[1024]{0:T(1024)} %param.8) | copy-start | bytes 12292
  4.9 18.6 %all-to-all-start.1 = ((s32[64,1,192]{2,1,0:T(1,128)}), s32[64,1,192]{2,1,0:T(1,128)S(1)}, u32[]{:S(2)}, u32[]{:S(2)}) async-start(s32[64,1,192]{2,1,0:T(1,128)} %reshape.842), calls=%async_computation.1 | async-start | bytes 131072 | tf_op jit(solution)/shard_map/all_to_all | solution.py:58
  23.5 7.6 %copy-start.3 = (bf16[1024,256]{1,0:T(8,128)(2,1)S(1)}, bf16[1024,256]{1,0:T(8,128)(2,1)}, u32[]{:S(2)}) copy-start(bf16[1024,256]{1,0:T(8,128)(2,1)} %param.9) | copy-start | bytes 1572868
  23.5 7.9 %copy-start.7 = (f32[256]{0:T(256)S(1)}, f32[256]{0:T(256)}, u32[]{:S(2)}) copy-start(f32[256]{0:T(256)} %param.10) | copy-start | bytes 3076
  23.5 81.3 %all-to-all-start = ((bf16[64,24,1024]{2,1,0:T(8,128)(2,1)}), bf16[64,24,1024]{2,1,0:T(8,128)(2,1)}, u32[]{:S(2)}, u32[]{:S(2)}) async-start(bf16[64,24,1024]{2,1,0:T(8,128)(2,1)} %bitcast.63), calls=%async_computation | async-start | bytes 6291456 | tf_op jit(solution)/shard_map/all_to_all | solution.py:61
  169.2 80.9 %copy-start.2 = (f32[192,1024]{1,0:T(8,128)S(1)}, f32[192,1024]{1,0:T(8,128)}, u32[]{:S(2)}) copy-start(f32[192,1024]{1,0:T(8,128)} %param.7) | copy-start | bytes 2359300
  253.9 79.5 %all-to-all-start.3 = ((bf16[64,24,1024]{2,1,0:T(8,128)(2,1)}), bf16[64,24,1024]{2,1,0:T(8,128)(2,1)}, u32[]{:S(2)}, u32[]{:S(2)}) async-start(bf16[64,24,1024]{2,1,0:T(8,128)(2,1)} %bitcast.64), calls=%async_computation.3 | async-start | bytes 6291456 | tf_op jit(solution)/shard_map/all_to_all | solution.py:108

commit v2 on v1

v2 whole, which is shorter than its diff:
```python
import jax
import jax.numpy as jnp
from jax import lax
from jax.sharding import PartitionSpec as P

D = 8192
BLK = 128
KB = 4
PER = 8


def slot_targets(row_blocks, total_blocks, capacity):
    pair_blocks = row_blocks.reshape(-1)
    onehot = (pair_blocks[:, None] == jnp.arange(total_blocks, dtype=jnp.int32)[None, :]).astype(
        jnp.int32
    )
    before = jnp.cumsum(onehot, axis=0) - onehot
    ranking = jnp.sum(before * onehot, axis=1)
    return pair_blocks * capacity + ranking


def pick_rows(values_t, offsets_t):
    lanes = jnp.arange(BLK, dtype=jnp.int32)
    hit = offsets_t[:, None, :] == lanes[None, :, None]
    return jnp.sum(jnp.where(hit, values_t[None, :, :], 0.0), axis=1)


def spread_rows(picked_t, offsets_t):
    lanes = jnp.arange(BLK, dtype=jnp.int32)[:, None]
    out = jnp.zeros((BLK, picked_t.shape[1]), picked_t.dtype)
    for j in range(PER):
        out = jnp.where(offsets_t[j : j + 1, :] == lanes, picked_t[j : j + 1, :], out)
    return out


def per_device(
    activations, center_bias, encoder_weight, encoder_bias, decoder_weight, row_blocks, pick_offsets
):
    group_rows, feature_width = activations.shape
    owners = lax.axis_size("lat")
    owned_blocks = encoder_bias.shape[0] // BLK
    owned_cols = owned_blocks * BLK
    total_blocks = owned_blocks * owners
    capacity = 2 * group_rows * KB // total_blocks
    slot_count = total_blocks * capacity
    per_owner = owned_blocks * capacity
    target = slot_targets(row_blocks, total_blocks, capacity)
    slots = jnp.arange(slot_count, dtype=jnp.int32)

    pair_hot = target[None, :] == slots[:, None]
    row_hot = jnp.any(pair_hot.reshape(slot_count, group_rows, KB), axis=2).astype(jnp.bfloat16)
    pair_hot = pair_hot.astype(jnp.bfloat16)

    centered = (activations - center_bias[None, :]).astype(jnp.bfloat16)
    outgoing = jnp.dot(row_hot, centered, preferred_element_type=jnp.float32).astype(jnp.bfloat16)
    offs_plus = (pick_offsets.reshape(-1, PER) + 1).astype(jnp.bfloat16)
    out_offs_t = lax.dot_general(
        offs_plus, pair_hot, (((0,), (1,)), ((), ())), preferred_element_type=jnp.float32
    ).astype(jnp.int32)
    out_offs = out_offs_t.reshape(PER, owners, per_owner).transpose(1, 0, 2)

    got_offs = lax.all_to_all(out_offs, "lat", split_axis=0, concat_axis=0, tiled=True)
    got_rows = lax.all_to_all(
        outgoing.reshape(owners, per_owner, feature_width),
        "lat",
        split_axis=0,
        concat_axis=0,
        tiled=True,
    )
    got_rows = got_rows.reshape(slot_count, feature_width)
    offs_t = got_offs.transpose(1, 0, 2).reshape(PER, slot_count) - 1

    slot_block = (slots // capacity) % owned_blocks
    col_block = jnp.arange(owned_cols, dtype=jnp.int32) // BLK
    own_col = col_block[:, None] == slot_block[None, :]

    def own_half(full_t):
        parts = full_t.reshape(owned_blocks, BLK, slot_count)
        sel = jnp.arange(owned_blocks, dtype=jnp.int32)[:, None, None] == slot_block[None, None, :]
        return jnp.sum(jnp.where(sel, parts, 0.0), axis=0)

    def widen(narrow_t):
        tiled = jnp.tile(narrow_t, (owned_blocks, 1))
        return jnp.where(own_col, tiled, jnp.zeros_like(tiled))

    partial_t = lax.dot_general(
        encoder_weight, got_rows, (((0,), (1,)), ((), ())), preferred_element_type=jnp.float32
    )
    partial = pick_rows(own_half(partial_t), offs_t)
    summed = lax.psum(partial, "row")
    bias_t = own_half(jnp.broadcast_to(encoder_bias[:, None], (owned_cols, slot_count)))
    pre_picked = summed + pick_rows(bias_t, offs_t)
    latent_t = spread_rows(pre_picked, offs_t).astype(jnp.bfloat16)
    latent_wide_t = widen(latent_t)
    decoded = lax.dot_general(
        latent_wide_t, decoder_weight, (((0,), (0,)), ((), ())), preferred_element_type=jnp.float32
    ).astype(jnp.bfloat16)
    returned = lax.all_to_all(
        decoded.reshape(owners, per_owner, feature_width),
        "lat",
        split_axis=0,
        concat_axis=0,
        tiled=True,
    ).reshape(slot_count, feature_width)
    rebuilt = lax.dot_general(
        row_hot, returned, (((0,), (0,)), ((), ())), preferred_element_type=jnp.float32
    )
    recon_error = (center_bias[None, :] + rebuilt) - activations
    loss_part = jnp.sum(recon_error * recon_error, axis=1)
    error_b = recon_error.astype(jnp.bfloat16)
    out_error = jnp.dot(row_hot, error_b, preferred_element_type=jnp.float32).astype(jnp.bfloat16)
    got_error = lax.all_to_all(
        out_error.reshape(owners, per_owner, feature_width),
        "lat",
        split_axis=0,
        concat_axis=0,
        tiled=True,
    ).reshape(slot_count, feature_width)
    decoder_grad = lax.dot_general(
        latent_wide_t, got_error, (((1,), (0,)), ((), ())), preferred_element_type=jnp.float32
    ).astype(jnp.bfloat16)
    dlatent_t = lax.dot_general(
        decoder_weight, got_error, (((1,), (1,)), ((), ())), preferred_element_type=jnp.float32
    )
    dlatent_part = pick_rows(own_half(dlatent_t), offs_t)
    dlatent, loss_total = lax.psum((dlatent_part, loss_part), "row")
    grad_t = spread_rows(dlatent, offs_t).astype(jnp.bfloat16)
    grad_wide_t = widen(grad_t)
    encoder_grad = lax.dot_general(
        got_rows, grad_wide_t, (((0,), (1,)), ((), ())), preferred_element_type=jnp.float32
    ).astype(jnp.bfloat16)
    bias_grad = jnp.sum(grad_wide_t.astype(jnp.float32), axis=1)
    row_loss = loss_total / D
    return (encoder_grad, decoder_grad, bias_grad, row_loss)


def solution(mesh):
    return jax.shard_map(
        per_device,
        mesh=mesh,
        in_specs=(
            P("lat", "row"),
            P("row"),
            P("row", "lat"),
            P("lat"),
            P("lat", "row"),
            P("lat", None),
            P("lat", None, None),
        ),
        out_specs=(P("row", "lat"), P("lat", "row"), P("lat"), P("lat")),
        check_vma=False,
    )
```

time: 399 us -> 352 us (0.88)
  other arithmetic: 31.3 us -> 8.07 us
  blocking collectives: 159 us -> 143 us
  local copies, waits for them, and re-layouts: 11.3 us -> 5.42 us
    reduce_sum x4 -> x5, other arithmetic: 14.8 us -> 3.88 us  [the longest x2 2.44 us: pick_rows(): return jnp.sum(jnp.where(hit, values_t[None, :, :], 0.0), axis=1)]
    psum x1, blocking collectives: 35.4 us -> 27.5 us  [per_device(): dlatent, loss_total = lax.psum((dlatent_part, loss_part), 'row')]
    convert_element_type x2, other arithmetic: 7.51 us -> 0.89 us  [the longest x1 0.44 us: per_device(): latent_t = spread_rows(pre_picked, offs_t).astype(jnp.bfloat16)]
    psum x1, blocking collectives: 42.3 us -> 36.4 us  [per_device(): summed = lax.psum(partial, 'row')]
    slice x3, local copies, waits for them, and re-layouts: 6.42 us -> 1.01 us  [spread_rows(): out = jnp.where(offsets_t[j:j + 1, :] == lanes, picked_t[j:j + 1, :], out)]
    select_n x1, other arithmetic: 4.76 us -> 0.28 us  [widen(): return jnp.where(own_col, tiled, jnp.zeros_like(tiled))]
where the time goes in v2:
time: 352 us; the launch traced here: 351 us
  waiting for transfers between devices  148 us (42%)
  blocking collectives  143 us (41%)
  starting transfers between devices  24 us (7%)
  matrix products  21.9 us (6%)
  other arithmetic  8.07 us (2%)
  local copies, waits for them, and re-layouts  5.42 us (2%)
    all_to_all x1, blocking collectives, per_device(): lax.all_to_all(decoded.reshape(owners, per_owner, feature_width), 'lat',...  78.9 us
    all_to_all x1, waiting for transfers between devices, per_device(): lax.all_to_all(out_error.reshape(owners, per_owner, feature_width), 'lat'...  73.7 us
    all_to_all x1, waiting for transfers between devices, per_device(): lax.all_to_all(outgoing.reshape(owners, per_owner, feature_width), 'lat',...  70.6 us
    psum x1, blocking collectives, per_device(): summed = lax.psum(partial, 'row')  36.4 us
    psum x1, blocking collectives, per_device(): dlatent, loss_total = lax.psum((dlatent_part, loss_part), 'row')  27.5 us
    all_to_all x1, starting transfers between devices, per_device(): lax.all_to_all(out_offs, 'lat', split_axis=0, concat_axis=0, tiled=True)  10.6 us
    all_to_all x1, starting transfers between devices, per_device(): lax.all_to_all(outgoing.reshape(owners, per_owner, feature_width), 'lat',...  7.57 us
  transfers between devices with their start and end apart: 3, of which 3 were waited for; matrix products, arithmetic and copies ran while one was open for 2% of the time, Pallas kernels for 0%

profile of v2, /device:TPU:6, one launch (start us, length us, event | category | flops | bytes accessed | tf_op | source)
XLA Modules:
  0.0 351.4 jit_solution(15194727655224638866)
XLA Ops:
  0.7 0.9 copy.38
  2.8 0.9 fusion.3
  4.0 0.9 reshape.972
  4.9 10.6 %all-to-all-start.1 = ((s32[64,1,192]{2,1,0:T(1,128)}), s32[64,1,192]{2,1,0:T(1,128)S(1)}, u32[]{:S(2)}, u32[]{:S(2)}) async-start(s32[64,1,192]{2,1,0:T(1,128)} %reshape.972), calls=%async_computation.1 | async-start | bytes 131072 | tf_op jit(solution)/shard_map/all_to_all | solution.py:62
  15.7 1.0 fusion
  16.8 2.8 convolution_convert_fusion.2
  19.5 4.0 %all-to-all-done.1 = s32[64,1,192]{2,1,0:T(1,128)S(1)} async-done(((s32[64,1,192]{2,1,0:T(1,128)}), s32[64,1,192]{2,1,0:T(1,128)S(1)}, u32[]{:S(2)}, u32[]{:S(2)}) %all-to-all-start.1) | async-done | bytes 49184 | tf_op jit(solution)/shard_map/all_to_all | solution.py:62
  23.5 7.6 %all-to-all-start = ((bf16[64,24,1024]{2,1,0:T(8,128)(2,1)}), bf16[64,24,1024]{2,1,0:T(8,128)(2,1)}, u32[]{:S(2)}, u32[]{:S(2)}) async-start(bf16[64,24,1024]{2,1,0:T(8,128)(2,1)} %bitcast.47), calls=%async_computation | async-start | bytes 6291456 | tf_op jit(solution)/shard_map/all_to_all | solution.py:63
  34.3 70.6 %all-to-all-done = bf16[64,24,1024]{2,1,0:T(8,128)(2,1)} async-done(((bf16[64,24,1024]{2,1,0:T(8,128)(2,1)}), bf16[64,24,1024]{2,1,0:T(8,128)(2,1)}, u32[]{:S(2)}, u32[]{:S(2)}) %all-to-all-start) | async-done | bytes 3145760 | tf_op jit(solution)/shard_map/all_to_all | solution.py:63
  104.9 2.9 fusion.20
  108.2 1.5 select_reduce_fusion.1
  109.7 36.4 %psum.21 = f32[8,1536]{1,0:T(8,128)S(1)} all-reduce(f32[8,1536]{1,0:T(8,128)S(1)} %get-tuple-element.29), channel_id=1, replica_groups=mesh['lat'=64,'row'=8] {'row'}, use_global_device_ids=true, to_apply=%region_6.7 | all-reduce | flops 12288 | bytes 98304 | tf_op jit(solution)/shard_map/psum | solution.py:90
  146.8 1.1 convolution_convert_fusion.1
  148.0 78.9 %all_to_all.20 = bf16[64,24,1024]{2,1,0:T(8,128)(2,1)S(1)} all-to-all(bf16[64,24,1024]{2,1,0:T(8,128)(2,1)S(1)} %bitcast.50), channel_id=1, replica_groups=mesh['lat'=64,'row'=8] {'lat'}, dimensions={0} | all-to-all | bytes 6291456 | tf_op jit(solution)/shard_map/all_to_all | solution.py:98
  226.9 0.9 multiply_reduce_fusion
  227.8 2.8 convolution_convert_fusion
  230.6 5.8 %all-to-all-start.3 = ((bf16[64,24,1024]{2,1,0:T(8,128)(2,1)}), bf16[64,24,1024]{2,1,0:T(8,128)(2,1)}, u32[]{:S(2)}, u32[]{:S(2)}) async-start(bf16[64,24,1024]{2,1,0:T(8,128)(2,1)} %bitcast.48), calls=%async_computation.3 | async-start | bytes 6291456 | tf_op jit(solution)/shard_map/all_to_all | solution.py:112
  236.4 73.7 %all-to-all-done.3 = bf16[64,24,1024]{2,1,0:T(8,128)(2,1)} async-done(((bf16[64,24,1024]{2,1,0:T(8,128)(2,1)}), bf16[64,24,1024]{2,1,0:T(8,128)(2,1)}, u32[]{:S(2)}, u32[]{:S(2)}) %all-to-all-start.3) | async-done | bytes 3145760 | tf_op jit(solution)/shard_map/all_to_all | solution.py:112
  310.1 2.9 fusion.21
  313.2 0.9 select_reduce_fusion
  314.1 27.5 %all-reduce = (f32[8,1536]{1,0:T(8,128)S(1)}, f32[192]{0:T(256)S(1)}) all-reduce(f32[8,1536]{1,0:T(8,128)S(1)} %select_reduce_fusion, f32[192]{0:T(256)S(1)} %get-tuple-element.36), channel_id=1, replica_groups=mesh['lat'=64,'row'=8] {'row'}, use_global_device_ids=true, to_apply=%region_11.12 | all-reduce | flops 12480 | bytes 99840 | tf_op jit(solution)/shard_map/psum | solution.py:126
  342.5 0.9 convert_reduce_fusion
  343.4 3.7 %convolution_convert_fusion.3 = bf16[256,1024]{1,0:T(8,128)(2,1)} fusion(bf16[256,1536]{1,0:T(8,128)(2,1)S(1)} %bitcast.56, bf16[1536,1024]{1,0:T(8,128)(2,1)} %bitcast.15), kind=kOutput, calls=%fused_computation.21 | convolution fusion | flops 805568512 | bytes 4456448 | tf_op jit(solution)/shard_map/dot_general | solution.py:119
  347.1 3.7 %convolution_convert_fusion.4 = bf16[1024,256]{1,0:T(8,128)(2,1)} fusion(bf16[1536,1024]{1,0:T(8,128)(2,1)} %bitcast.4, bf16[256,1536]{1,0:T(8,128)(2,1)S(1)} %bitcast.55), kind=kOutput, calls=%fused_computation.22 | convolution fusion | flops 805568512 | bytes 4456448 | tf_op jit(solution)/shard_map/dot_general | solution.py:129
  (60 shorter events, 7.4 us)
Async XLA Ops:
  0.6 146.2 %copy-start = (bf16[256,1024]{1,0:T(8,128)(2,1)S(1)}, bf16[256,1024]{1,0:T(8,128)(2,1)}, u32[]{:S(2)}) copy-start(bf16[256,1024]{1,0:T(8,128)(2,1)} %param.11) | copy-start | bytes 1572868
  0.6 1.9 copy-start.2
  1.5 14.2 %copy-start.3 = (s32[192,4]{0,1:T(4,128)S(1)}, s32[192,4]{0,1:T(4,128)}, u32[]{:S(2)}) copy-start(s32[192,4]{0,1:T(4,128)} %param.12) | copy-start | bytes 9220
  1.9 14.9 %copy-start.1 = (f32[192,1024]{1,0:T(8,128)S(1)}, f32[192,1024]{1,0:T(8,128)}, u32[]{:S(2)}) copy-start(f32[192,1024]{1,0:T(8,128)} %param.7) | copy-start | bytes 2359300
  1.9 14.9 %copy-start.4 = (f32[1024]{0:T(1024)S(1)}, f32[1024]{0:T(1024)}, u32[]{:S(2)}) copy-start(f32[1024]{0:T(1024)} %param.8) | copy-start | bytes 12292
  4.9 18.6 %all-to-all-start.1 = ((s32[64,1,192]{2,1,0:T(1,128)}), s32[64,1,192]{2,1,0:T(1,128)S(1)}, u32[]{:S(2)}, u32[]{:S(2)}) async-start(s32[64,1,192]{2,1,0:T(1,128)} %reshape.972), calls=%async_computation.1 | async-start | bytes 131072 | tf_op jit(solution)/shard_map/all_to_all | solution.py:62
  23.5 81.3 %copy-start.6 = (bf16[1024,256]{1,0:T(8,128)(2,1)S(1)}, bf16[1024,256]{1,0:T(8,128)(2,1)}, u32[]{:S(2)}) copy-start(bf16[1024,256]{1,0:T(8,128)(2,1)} %param.9) | copy-start | bytes 1572868
  23.5 81.3 %all-to-all-start = ((bf16[64,24,1024]{2,1,0:T(8,128)(2,1)}), bf16[64,24,1024]{2,1,0:T(8,128)(2,1)}, u32[]{:S(2)}, u32[]{:S(2)}) async-start(bf16[64,24,1024]{2,1,0:T(8,128)(2,1)} %bitcast.47), calls=%async_computation | async-start | bytes 6291456 | tf_op jit(solution)/shard_map/all_to_all | solution.py:63
  104.9 2.9 copy-start.5
  230.6 79.5 %all-to-all-start.3 = ((bf16[64,24,1024]{2,1,0:T(8,128)(2,1)}), bf16[64,24,1024]{2,1,0:T(8,128)(2,1)}, u32[]{:S(2)}, u32[]{:S(2)}) async-start(bf16[64,24,1024]{2,1,0:T(8,128)(2,1)} %bitcast.48), calls=%async_computation.3 | async-start | bytes 6291456 | tf_op jit(solution)/shard_map/all_to_all | solution.py:112

commit v3 on v2

--- a/solution.py
+++ b/solution.py
@@ -31,6 +31,16 @@
     for j in range(PER):
         out = jnp.where(offsets_t[j : j + 1, :] == lanes, picked_t[j : j + 1, :], out)
     return out
+
+
+def butterfly_sum(x, axis):
+    size = lax.axis_size(axis)
+    step = 1
+    while step < size:
+        other = lax.ppermute(x, axis, perm=[(i, i ^ step) for i in range(size)])
+        x = x + other
+        step *= 2
+    return x
 
 
 def per_device(
@@ -87,7 +97,7 @@
         encoder_weight, got_rows, (((0,), (1,)), ((), ())), preferred_element_type=jnp.float32
     )
     partial = pick_rows(own_half(partial_t), offs_t)
-    summed = lax.psum(partial, "row")
+    summed = butterfly_sum(partial, "row")
     bias_t = own_half(jnp.broadcast_to(encoder_bias[:, None], (owned_cols, slot_count)))
     pre_picked = summed + pick_rows(bias_t, offs_t)
     latent_t = spread_rows(pre_picked, offs_t).astype(jnp.bfloat16)
@@ -123,7 +133,10 @@
         decoder_weight, got_error, (((1,), (1,)), ((), ())), preferred_element_type=jnp.float32
     )
     dlatent_part = pick_rows(own_half(dlatent_t), offs_t)
-    dlatent, loss_total = lax.psum((dlatent_part, loss_part), "row")
+    loss_row = jnp.zeros((1, slot_count), jnp.float32).at[0, :group_rows].set(loss_part)
+    reduced = butterfly_sum(jnp.concatenate([dlatent_part, loss_row], axis=0), "row")
+    dlatent = reduced[:PER]
+    loss_total = reduced[PER, :group_rows]
     grad_t = spread_rows(dlatent, offs_t).astype(jnp.bfloat16)
     grad_wide_t = widen(grad_t)
     encoder_grad = lax.dot_general(

time: 352 us -> 341 us (0.969)
  blocking collectives: 143 us -> 78.9 us
  starting transfers between devices: 24 us -> 59.2 us
  waiting for transfers between devices: 148 us -> 164 us
    psum x2 -> x0, blocking collectives: 63.9 us -> none  [the longest x1 36.4 us: per_device(): summed = lax.psum(partial, 'row')]
    ppermute x0 -> x6, starting transfers between devices: none -> 35.2 us  [butterfly_sum(): other = lax.ppermute(x, axis, perm=[(i, i ^ step) for i in range(size)])]
    ppermute x0 -> x6, waiting for transfers between devices: none -> 15.7 us  [butterfly_sum(): other = lax.ppermute(x, axis, perm=[(i, i ^ step) for i in range(size)])]
  transfers between devices with their start and end apart: 3 -> 9, of which waited for: 3 -> 9; matrix products, arithmetic and copies ran while one was open for 2% -> 2% of each run, Pallas kernels for 0% -> 0%
where the time goes in v3:
time: 341 us; the launch traced here: 340 us
  waiting for transfers between devices  164 us (48%)
  blocking collectives  78.9 us (23%)
  starting transfers between devices  59.2 us (17%)
  matrix products  21.9 us (6%)
  other arithmetic  9.42 us (3%)
  local copies, waits for them, and re-layouts  5.42 us (2%)
    all_to_all x1, blocking collectives, per_device(): lax.all_to_all(decoded.reshape(owners, per_owner, feature_width), 'lat',...  78.9 us
    all_to_all x1, waiting for transfers between devices, per_device(): lax.all_to_all(out_error.reshape(owners, per_owner, feature_width), 'lat'...  72.4 us
    all_to_all x1, waiting for transfers between devices, per_device(): lax.all_to_all(outgoing.reshape(owners, per_owner, feature_width), 'lat',...  72 us
    ppermute x6, starting transfers between devices, butterfly_sum(): other = lax.ppermute(x, axis, perm=[(i, i ^ step) for i in range(size)])  35.2 us
    ppermute x6, waiting for transfers between devices, butterfly_sum(): other = lax.ppermute(x, axis, perm=[(i, i ^ step) for i in range(size)])  15.7 us
    all_to_all x1, starting transfers between devices, per_device(): lax.all_to_all(out_offs, 'lat', split_axis=0, concat_axis=0, tiled=True)  10.6 us
    all_to_all x1, starting transfers between devices, per_device(): lax.all_to_all(outgoing.reshape(owners, per_owner, feature_width), 'lat',...  7.57 us
  transfers between devices with their start and end apart: 9, of which 9 were waited for; matrix products, arithmetic and copies ran while one was open for 2% of the time, Pallas kernels for 0%

profile of v3, /device:TPU:6, one launch (start us, length us, event | category | flops | bytes accessed | tf_op | source)
XLA Modules:
  0.0 340.0 jit_solution(6969288830426775263)
XLA Ops:
  4.9 10.6 %all-to-all-start.1 = ((s32[64,1,192]{2,1,0:T(1,128)}), s32[64,1,192]{2,1,0:T(1,128)S(1)}, u32[]{:S(2)}, u32[]{:S(2)}) async-start(s32[64,1,192]{2,1,0:T(1,128)} %reshape.1013), calls=%async_computation.1 | async-start | bytes 131072 | tf_op jit(solution)/shard_map/all_to_all | solution.py:72
  16.8 2.8 convolution_convert_fusion.2
  19.5 4.0 %all-to-all-done.1 = s32[64,1,192]{2,1,0:T(1,128)S(1)} async-done(((s32[64,1,192]{2,1,0:T(1,128)}), s32[64,1,192]{2,1,0:T(1,128)S(1)}, u32[]{:S(2)}, u32[]{:S(2)}) %all-to-all-start.1) | async-done | bytes 49184 | tf_op jit(solution)/shard_map/all_to_all | solution.py:72
  23.5 7.6 %all-to-all-start = ((bf16[64,24,1024]{2,1,0:T(8,128)(2,1)}), bf16[64,24,1024]{2,1,0:T(8,128)(2,1)}, u32[]{:S(2)}, u32[]{:S(2)}) async-start(bf16[64,24,1024]{2,1,0:T(8,128)(2,1)} %bitcast.49), calls=%async_computation | async-start | bytes 6291456 | tf_op jit(solution)/shard_map/all_to_all | solution.py:73
  32.9 72.0 %all-to-all-done = bf16[64,24,1024]{2,1,0:T(8,128)(2,1)} async-done(((bf16[64,24,1024]{2,1,0:T(8,128)(2,1)}), bf16[64,24,1024]{2,1,0:T(8,128)(2,1)}, u32[]{:S(2)}, u32[]{:S(2)}) %all-to-all-start) | async-done | bytes 3145760 | tf_op jit(solution)/shard_map/all_to_all | solution.py:73
  104.9 2.9 fusion.21
  109.7 4.3 %collective-permute-start = (f32[8,1536]{1,0:T(8,128)S(1)}, f32[8,1536]{1,0:T(8,128)S(1)}, u32[]{:S(2)}, u32[]{:S(2)}) collective-permute-start(f32[8,1536]{1,0:T(8,128)S(1)} %get-tuple-element.40), channel_id=1, source_target_pairs={{0,1},{1,0},{2,3},{3,2},{4,5},{5,4},{6,7},{7,6},{8,9},{9,8},{10,11... | collective-permute-start | bytes 147464 | tf_op jit(solution)/shard_map/ppermute | solution.py:40
  114.0 2.1 collective-permute-done
  116.1 6.1 %collective-permute-start.1 = (f32[8,1536]{1,0:T(8,128)S(1)}, f32[8,1536]{1,0:T(8,128)S(1)}, u32[]{:S(2)}, u32[]{:S(2)}) collective-permute-start(f32[8,1536]{1,0:T(8,128)S(1)} %add.104), channel_id=1, source_target_pairs={{0,2},{1,3},{2,0},{3,1},{4,6},{5,7},{6,4},{7,5},{8,10},{9,11},{10,... | collective-permute-start | bytes 147464 | tf_op jit(solution)/shard_map/ppermute | solution.py:40
  122.2 2.0 collective-permute-done.1
  124.2 9.5 %collective-permute-start.2 = (f32[8,1536]{1,0:T(8,128)S(1)}, f32[8,1536]{1,0:T(8,128)S(1)}, u32[]{:S(2)}, u32[]{:S(2)}) collective-permute-start(f32[8,1536]{1,0:T(8,128)S(1)} %add.105), channel_id=1, source_target_pairs={{0,4},{1,5},{2,6},{3,7},{4,0},{5,1},{6,2},{7,3},{8,12},{9,13},{10,... | collective-permute-start | bytes 147464 | tf_op jit(solution)/shard_map/ppermute | solution.py:40
  137.8 78.9 %all_to_all.20 = bf16[64,24,1024]{2,1,0:T(8,128)(2,1)S(1)} all-to-all(bf16[64,24,1024]{2,1,0:T(8,128)(2,1)S(1)} %bitcast.52), channel_id=1, replica_groups=mesh['lat'=64,'row'=8] {'lat'}, dimensions={0} | all-to-all | bytes 6291456 | tf_op jit(solution)/shard_map/all_to_all | solution.py:108
  217.7 2.8 convolution_convert_fusion
  220.5 5.8 %all-to-all-start.3 = ((bf16[64,24,1024]{2,1,0:T(8,128)(2,1)}), bf16[64,24,1024]{2,1,0:T(8,128)(2,1)}, u32[]{:S(2)}, u32[]{:S(2)}) async-start(bf16[64,24,1024]{2,1,0:T(8,128)(2,1)} %bitcast.50), calls=%async_computation.3 | async-start | bytes 6291456 | tf_op jit(solution)/shard_map/all_to_all | solution.py:122
  227.6 72.4 %all-to-all-done.3 = bf16[64,24,1024]{2,1,0:T(8,128)(2,1)} async-done(((bf16[64,24,1024]{2,1,0:T(8,128)(2,1)}), bf16[64,24,1024]{2,1,0:T(8,128)(2,1)}, u32[]{:S(2)}, u32[]{:S(2)}) %all-to-all-start.3) | async-done | bytes 3145760 | tf_op jit(solution)/shard_map/all_to_all | solution.py:122
  300.0 2.9 fusion.22
  304.1 2.9 collective-permute-start.3
  307.0 3.6 %collective-permute-done.3 = f32[9,1536]{1,0:T(8,128)S(1)} collective-permute-done((f32[9,1536]{1,0:T(8,128)S(1)}, f32[9,1536]{1,0:T(8,128)S(1)}, u32[]{:S(2)}, u32[]{:S(2)}) %collective-permute-start.3) | collective-permute-done | bytes 55328 | tf_op jit(solution)/shard_map/ppermute | solution.py:40
  310.6 4.4 %collective-permute-start.4 = (f32[9,1536]{1,0:T(8,128)S(1)}, f32[9,1536]{1,0:T(8,128)S(1)}, u32[]{:S(2)}, u32[]{:S(2)}) collective-permute-start(f32[9,1536]{1,0:T(8,128)S(1)} %fusion.20), channel_id=1, source_target_pairs={{0,2},{1,3},{2,0},{3,1},{4,6},{5,7},{6,4},{7,5},{8,10},{9,11},{10,... | collective-permute-start | bytes 165896 | tf_op jit(solution)/shard_map/ppermute | solution.py:40
  315.0 4.0 %collective-permute-done.4 = f32[9,1536]{1,0:T(8,128)S(1)} collective-permute-done((f32[9,1536]{1,0:T(8,128)S(1)}, f32[9,1536]{1,0:T(8,128)S(1)}, u32[]{:S(2)}, u32[]{:S(2)}) %collective-permute-start.4) | collective-permute-done | bytes 55328 | tf_op jit(solution)/shard_map/ppermute | solution.py:40
  319.1 8.0 %collective-permute-start.5 = (f32[9,1536]{1,0:T(8,128)S(1)}, f32[9,1536]{1,0:T(8,128)S(1)}, u32[]{:S(2)}, u32[]{:S(2)}) collective-permute-start(f32[9,1536]{1,0:T(8,128)S(1)} %add.110), channel_id=1, source_target_pairs={{0,4},{1,5},{2,6},{3,7},{4,0},{5,1},{6,2},{7,3},{8,12},{9,13},{10,... | collective-permute-start | bytes 165896 | tf_op jit(solution)/shard_map/ppermute | solution.py:40
  327.1 3.1 collective-permute-done.5
  332.5 3.7 %convolution_convert_fusion.3 = bf16[256,1024]{1,0:T(8,128)(2,1)} fusion(bf16[256,1536]{1,0:T(8,128)(2,1)S(1)} %bitcast.58, bf16[1536,1024]{1,0:T(8,128)(2,1)} %bitcast.15), kind=kOutput, calls=%fused_computation.21 | convolution fusion | flops 805568512 | bytes 4456448 | tf_op jit(solution)/shard_map/dot_general | solution.py:129
  336.2 3.7 %convolution_convert_fusion.4 = bf16[1024,256]{1,0:T(8,128)(2,1)} fusion(bf16[1536,1024]{1,0:T(8,128)(2,1)} %bitcast.4, bf16[256,1536]{1,0:T(8,128)(2,1)S(1)} %bitcast.57), kind=kOutput, calls=%fused_computation.22 | convolution fusion | flops 805568512 | bytes 4456448 | tf_op jit(solution)/shard_map/dot_general | solution.py:142
  (78 shorter events, 18.7 us)
Async XLA Ops:
  0.6 136.1 %copy-start = (bf16[256,1024]{1,0:T(8,128)(2,1)S(1)}, bf16[256,1024]{1,0:T(8,128)(2,1)}, u32[]{:S(2)}) copy-start(bf16[256,1024]{1,0:T(8,128)(2,1)} %param.13) | copy-start | bytes 1572868
  0.6 1.9 copy-start.2
  1.5 14.2 %copy-start.3 = (s32[192,4]{0,1:T(4,128)S(1)}, s32[192,4]{0,1:T(4,128)}, u32[]{:S(2)}) copy-start(s32[192,4]{0,1:T(4,128)} %param.14) | copy-start | bytes 9220
  1.9 14.9 %copy-start.1 = (f32[192,1024]{1,0:T(8,128)S(1)}, f32[192,1024]{1,0:T(8,128)}, u32[]{:S(2)}) copy-start(f32[192,1024]{1,0:T(8,128)} %param.9) | copy-start | bytes 2359300
  1.9 14.9 %copy-start.4 = (f32[1024]{0:T(1024)S(1)}, f32[1024]{0:T(1024)}, u32[]{:S(2)}) copy-start(f32[1024]{0:T(1024)} %param.10) | copy-start | bytes 12292
  4.9 18.6 %all-to-all-start.1 = ((s32[64,1,192]{2,1,0:T(1,128)}), s32[64,1,192]{2,1,0:T(1,128)S(1)}, u32[]{:S(2)}, u32[]{:S(2)}) async-start(s32[64,1,192]{2,1,0:T(1,128)} %reshape.1013), calls=%async_computation.1 | async-start | bytes 131072 | tf_op jit(solution)/shard_map/all_to_all | solution.py:72
  23.5 81.3 %copy-start.6 = (bf16[1024,256]{1,0:T(8,128)(2,1)S(1)}, bf16[1024,256]{1,0:T(8,128)(2,1)}, u32[]{:S(2)}) copy-start(bf16[1024,256]{1,0:T(8,128)(2,1)} %param.11) | copy-start | bytes 1572868
  23.5 81.3 %all-to-all-start = ((bf16[64,24,1024]{2,1,0:T(8,128)(2,1)}), bf16[64,24,1024]{2,1,0:T(8,128)(2,1)}, u32[]{:S(2)}, u32[]{:S(2)}) async-start(bf16[64,24,1024]{2,1,0:T(8,128)(2,1)} %bitcast.49), calls=%async_computation | async-start | bytes 6291456 | tf_op jit(solution)/shard_map/all_to_all | solution.py:73
  104.9 2.9 copy-start.5
  109.7 6.3 %collective-permute-start = (f32[8,1536]{1,0:T(8,128)S(1)}, f32[8,1536]{1,0:T(8,128)S(1)}, u32[]{:S(2)}, u32[]{:S(2)}) collective-permute-start(f32[8,1536]{1,0:T(8,128)S(1)} %get-tuple-element.40), channel_id=1, source_target_pairs={{0,1},{1,0},{2,3},{3,2},{4,5},{5,4},{6,7},{7,6},{8,9},{9,8},{10,11... | collective-permute-start | bytes 147464 | tf_op jit(solution)/shard_map/ppermute | solution.py:40
  116.1 8.1 %collective-permute-start.1 = (f32[8,1536]{1,0:T(8,128)S(1)}, f32[8,1536]{1,0:T(8,128)S(1)}, u32[]{:S(2)}, u32[]{:S(2)}) collective-permute-start(f32[8,1536]{1,0:T(8,128)S(1)} %add.104), channel_id=1, source_target_pairs={{0,2},{1,3},{2,0},{3,1},{4,6},{5,7},{6,4},{7,5},{8,10},{9,11},{10,... | collective-permute-start | bytes 147464 | tf_op jit(solution)/shard_map/ppermute | solution.py:40
  124.2 11.8 %collective-permute-start.2 = (f32[8,1536]{1,0:T(8,128)S(1)}, f32[8,1536]{1,0:T(8,128)S(1)}, u32[]{:S(2)}, u32[]{:S(2)}) collective-permute-start(f32[8,1536]{1,0:T(8,128)S(1)} %add.105), channel_id=1, source_target_pairs={{0,4},{1,5},{2,6},{3,7},{4,0},{5,1},{6,2},{7,3},{8,12},{9,13},{10,... | collective-permute-start | bytes 147464 | tf_op jit(solution)/shard_map/ppermute | solution.py:40
  220.5 79.5 %all-to-all-start.3 = ((bf16[64,24,1024]{2,1,0:T(8,128)(2,1)}), bf16[64,24,1024]{2,1,0:T(8,128)(2,1)}, u32[]{:S(2)}, u32[]{:S(2)}) async-start(bf16[64,24,1024]{2,1,0:T(8,128)(2,1)} %bitcast.50), calls=%async_computation.3 | async-start | bytes 6291456 | tf_op jit(solution)/shard_map/all_to_all | solution.py:122
  304.1 6.5 %collective-permute-start.3 = (f32[9,1536]{1,0:T(8,128)S(1)}, f32[9,1536]{1,0:T(8,128)S(1)}, u32[]{:S(2)}, u32[]{:S(2)}) collective-permute-start(f32[9,1536]{1,0:T(8,128)S(1)} %select_maximum_fusion), channel_id=1, source_target_pairs={{0,1},{1,0},{2,3},{3,2},{4,5},{5,4},{6,7},{7,6},{8,9},{9,8},{10,11... | collective-permute-start | bytes 165896 | tf_op jit(solution)/shard_map/ppermute | solution.py:40
  310.6 8.5 %collective-permute-start.4 = (f32[9,1536]{1,0:T(8,128)S(1)}, f32[9,1536]{1,0:T(8,128)S(1)}, u32[]{:S(2)}, u32[]{:S(2)}) collective-permute-start(f32[9,1536]{1,0:T(8,128)S(1)} %fusion.20), channel_id=1, source_target_pairs={{0,2},{1,3},{2,0},{3,1},{4,6},{5,7},{6,4},{7,5},{8,10},{9,11},{10,... | collective-permute-start | bytes 165896 | tf_op jit(solution)/shard_map/ppermute | solution.py:40
  319.1 11.1 %collective-permute-start.5 = (f32[9,1536]{1,0:T(8,128)S(1)}, f32[9,1536]{1,0:T(8,128)S(1)}, u32[]{:S(2)}, u32[]{:S(2)}) collective-permute-start(f32[9,1536]{1,0:T(8,128)S(1)} %add.110), channel_id=1, source_target_pairs={{0,4},{1,5},{2,6},{3,7},{4,0},{5,1},{6,2},{7,3},{8,12},{9,13},{10,... | collective-permute-start | bytes 165896 | tf_op jit(solution)/shard_map/ppermute | solution.py:40

commit v4 on v2

--- a/solution.py
+++ b/solution.py
@@ -31,6 +31,10 @@
     for j in range(PER):
         out = jnp.where(offsets_t[j : j + 1, :] == lanes, picked_t[j : j + 1, :], out)
     return out
+
+
+def gathered_sum(x, axis):
+    return jnp.sum(lax.all_gather(x, axis, axis=0), axis=0)
 
 
 def per_device(
@@ -87,7 +91,7 @@
         encoder_weight, got_rows, (((0,), (1,)), ((), ())), preferred_element_type=jnp.float32
     )
     partial = pick_rows(own_half(partial_t), offs_t)
-    summed = lax.psum(partial, "row")
+    summed = gathered_sum(partial, "row")
     bias_t = own_half(jnp.broadcast_to(encoder_bias[:, None], (owned_cols, slot_count)))
     pre_picked = summed + pick_rows(bias_t, offs_t)
     latent_t = spread_rows(pre_picked, offs_t).astype(jnp.bfloat16)
@@ -123,7 +127,10 @@
         decoder_weight, got_error, (((1,), (1,)), ((), ())), preferred_element_type=jnp.float32
     )
     dlatent_part = pick_rows(own_half(dlatent_t), offs_t)
-    dlatent, loss_total = lax.psum((dlatent_part, loss_part), "row")
+    loss_row = jnp.zeros((1, slot_count), jnp.float32).at[0, :group_rows].set(loss_part)
+    reduced = gathered_sum(jnp.concatenate([dlatent_part, loss_row], axis=0), "row")
+    dlatent = reduced[:PER]
+    loss_total = reduced[PER, :group_rows]
     grad_t = spread_rows(dlatent, offs_t).astype(jnp.bfloat16)
     grad_wide_t = widen(grad_t)
     encoder_grad = lax.dot_general(

time: 352 us -> 346 us (0.983)
  blocking collectives: 143 us -> 137 us
    psum x2 -> x0, blocking collectives: 63.9 us -> none  [the longest x1 36.4 us: per_device(): summed = lax.psum(partial, 'row')]
    all_gather x0 -> x2, blocking collectives: none -> 58.2 us  [gathered_sum(): return jnp.sum(lax.all_gather(x, axis, axis=0), axis=0)]
where the time goes in v4:
time: 346 us
  waiting for transfers between devices  147 us (42%)
  blocking collectives  137 us (40%)
  starting transfers between devices  24 us (7%)
  matrix products  21.9 us (6%)
  other arithmetic  9.43 us (3%)
  local copies, waits for them, and re-layouts  5.42 us (2%)
    all_to_all x1, blocking collectives, per_device(): lax.all_to_all(decoded.reshape(owners, per_owner, feature_width), 'lat',...  78.8 us
    all_to_all x1, waiting for transfers between devices, per_device(): lax.all_to_all(out_error.reshape(owners, per_owner, feature_width), 'lat'...  72.4 us
    all_to_all x1, waiting for transfers between devices, per_device(): lax.all_to_all(outgoing.reshape(owners, per_owner, feature_width), 'lat',...  70.6 us
    all_gather x2, blocking collectives, gathered_sum(): return jnp.sum(lax.all_gather(x, axis, axis=0), axis=0)  58.2 us
    all_to_all x1, starting transfers between devices, per_device(): lax.all_to_all(out_offs, 'lat', split_axis=0, concat_axis=0, tiled=True)  10.6 us
    all_to_all x1, starting transfers between devices, per_device(): lax.all_to_all(outgoing.reshape(owners, per_owner, feature_width), 'lat',...  7.57 us
  transfers between devices with their start and end apart: 3, of which 3 were waited for; matrix products, arithmetic and copies ran while one was open for 2% of the time, Pallas kernels for 0%

profile of v4, /device:TPU:6, one launch (start us, length us, event | category | flops | bytes accessed | tf_op | source)
XLA Modules:
  0.0 345.6 jit_solution(7884437066441899299)
XLA Ops:
  0.7 0.9 copy.38
  2.8 0.9 fusion.3
  4.0 0.9 reshape.1018
  4.9 10.6 %all-to-all-start.1 = ((s32[64,1,192]{2,1,0:T(1,128)}), s32[64,1,192]{2,1,0:T(1,128)S(1)}, u32[]{:S(2)}, u32[]{:S(2)}) async-start(s32[64,1,192]{2,1,0:T(1,128)} %reshape.1018), calls=%async_computation.1 | async-start | bytes 131072 | tf_op jit(solution)/shard_map/all_to_all | solution.py:66
  15.7 1.0 fusion
  16.8 2.8 convolution_convert_fusion.2
  19.5 4.0 %all-to-all-done.1 = s32[64,1,192]{2,1,0:T(1,128)S(1)} async-done(((s32[64,1,192]{2,1,0:T(1,128)}), s32[64,1,192]{2,1,0:T(1,128)S(1)}, u32[]{:S(2)}, u32[]{:S(2)}) %all-to-all-start.1) | async-done | bytes 49184 | tf_op jit(solution)/shard_map/all_to_all | solution.py:66
  23.5 7.6 %all-to-all-start = ((bf16[64,24,1024]{2,1,0:T(8,128)(2,1)}), bf16[64,24,1024]{2,1,0:T(8,128)(2,1)}, u32[]{:S(2)}, u32[]{:S(2)}) async-start(bf16[64,24,1024]{2,1,0:T(8,128)(2,1)} %bitcast.53), calls=%async_computation | async-start | bytes 6291456 | tf_op jit(solution)/shard_map/all_to_all | solution.py:67
  34.3 70.6 %all-to-all-done = bf16[64,24,1024]{2,1,0:T(8,128)(2,1)} async-done(((bf16[64,24,1024]{2,1,0:T(8,128)(2,1)}), bf16[64,24,1024]{2,1,0:T(8,128)(2,1)}, u32[]{:S(2)}, u32[]{:S(2)}) %all-to-all-start) | async-done | bytes 3145760 | tf_op jit(solution)/shard_map/all_to_all | solution.py:67
  104.9 2.9 fusion.21
  108.2 1.5 select_reduce_fusion.1
  109.7 31.9 %all-gather = f32[64,1536]{1,0:T(8,128)S(1)} all-gather(f32[8,1536]{1,0:T(8,128)S(1)} %get-tuple-element.41), channel_id=2, replica_groups=mesh['lat'=64,'row'=8] {'row'}, dimensions={0}, use_global_device_ids=true | all-gather | bytes 442368 | tf_op jit(solution)/shard_map/all_gather | solution.py:37
  142.3 1.1 convolution_convert_fusion.1
  143.4 78.8 %all_to_all.20 = bf16[64,24,1024]{2,1,0:T(8,128)(2,1)S(1)} all-to-all(bf16[64,24,1024]{2,1,0:T(8,128)(2,1)S(1)} %bitcast.56), channel_id=1, replica_groups=mesh['lat'=64,'row'=8] {'lat'}, dimensions={0} | all-to-all | bytes 6291456 | tf_op jit(solution)/shard_map/all_to_all | solution.py:102
  222.2 0.9 multiply_reduce_fusion
  223.1 2.8 convolution_convert_fusion
  226.0 5.8 %all-to-all-start.3 = ((bf16[64,24,1024]{2,1,0:T(8,128)(2,1)}), bf16[64,24,1024]{2,1,0:T(8,128)(2,1)}, u32[]{:S(2)}, u32[]{:S(2)}) async-start(bf16[64,24,1024]{2,1,0:T(8,128)(2,1)} %bitcast.54), calls=%async_computation.3 | async-start | bytes 6291456 | tf_op jit(solution)/shard_map/all_to_all | solution.py:116
  233.1 72.4 %all-to-all-done.3 = bf16[64,24,1024]{2,1,0:T(8,128)(2,1)} async-done(((bf16[64,24,1024]{2,1,0:T(8,128)(2,1)}), bf16[64,24,1024]{2,1,0:T(8,128)(2,1)}, u32[]{:S(2)}, u32[]{:S(2)}) %all-to-all-start.3) | async-done | bytes 3145760 | tf_op jit(solution)/shard_map/all_to_all | solution.py:116
  305.4 2.9 fusion.22
  308.5 0.9 select_reduce_fusion
  309.5 26.3 %all-gather.2 = f32[8,9,1536]{2,1,0:T(8,128)S(1)} all-gather(f32[1,9,1536]{2,1,0:T(8,128)S(1)} %fusion.15), channel_id=3, replica_groups=mesh['lat'=64,'row'=8] {'row'}, dimensions={0}, use_global_device_ids=true | all-gather | bytes 497664 | tf_op jit(solution)/shard_map/all_gather | solution.py:37
  336.7 0.9 convert_reduce_fusion
  338.2 3.7 %convolution_convert_fusion.3 = bf16[256,1024]{1,0:T(8,128)(2,1)} fusion(bf16[256,1536]{1,0:T(8,128)(2,1)S(1)} %bitcast.62, bf16[1536,1024]{1,0:T(8,128)(2,1)} %bitcast.16), kind=kOutput, calls=%fused_computation.21 | convolution fusion | flops 805568512 | bytes 4456448 | tf_op jit(solution)/shard_map/dot_general | solution.py:123
  341.9 3.7 %convolution_convert_fusion.4 = bf16[1024,256]{1,0:T(8,128)(2,1)} fusion(bf16[1536,1024]{1,0:T(8,128)(2,1)} %bitcast.4, bf16[256,1536]{1,0:T(8,128)(2,1)S(1)} %bitcast.61), kind=kOutput, calls=%fused_computation.22 | convolution fusion | flops 805568512 | bytes 4456448 | tf_op jit(solution)/shard_map/dot_general | solution.py:136
  (65 shorter events, 8.8 us)
Async XLA Ops:
  0.6 141.7 %copy-start = (bf16[256,1024]{1,0:T(8,128)(2,1)S(1)}, bf16[256,1024]{1,0:T(8,128)(2,1)}, u32[]{:S(2)}) copy-start(bf16[256,1024]{1,0:T(8,128)(2,1)} %param.13) | copy-start | bytes 1572868
  0.6 1.9 copy-start.2
  1.5 14.2 %copy-start.3 = (s32[192,4]{0,1:T(4,128)S(1)}, s32[192,4]{0,1:T(4,128)}, u32[]{:S(2)}) copy-start(s32[192,4]{0,1:T(4,128)} %param.14) | copy-start | bytes 9220
  1.9 14.9 %copy-start.1 = (f32[192,1024]{1,0:T(8,128)S(1)}, f32[192,1024]{1,0:T(8,128)}, u32[]{:S(2)}) copy-start(f32[192,1024]{1,0:T(8,128)} %param.9) | copy-start | bytes 2359300
  1.9 14.9 %copy-start.4 = (f32[1024]{0:T(1024)S(1)}, f32[1024]{0:T(1024)}, u32[]{:S(2)}) copy-start(f32[1024]{0:T(1024)} %param.10) | copy-start | bytes 12292
  4.9 18.6 %all-to-all-start.1 = ((s32[64,1,192]{2,1,0:T(1,128)}), s32[64,1,192]{2,1,0:T(1,128)S(1)}, u32[]{:S(2)}, u32[]{:S(2)}) async-start(s32[64,1,192]{2,1,0:T(1,128)} %reshape.1018), calls=%async_computation.1 | async-start | bytes 131072 | tf_op jit(solution)/shard_map/all_to_all | solution.py:66
  23.5 81.3 %copy-start.6 = (bf16[1024,256]{1,0:T(8,128)(2,1)S(1)}, bf16[1024,256]{1,0:T(8,128)(2,1)}, u32[]{:S(2)}) copy-start(bf16[1024,256]{1,0:T(8,128)(2,1)} %param.11) | copy-start | bytes 1572868
  23.5 81.3 %all-to-all-start = ((bf16[64,24,1024]{2,1,0:T(8,128)(2,1)}), bf16[64,24,1024]{2,1,0:T(8,128)(2,1)}, u32[]{:S(2)}, u32[]{:S(2)}) async-start(bf16[64,24,1024]{2,1,0:T(8,128)(2,1)} %bitcast.53), calls=%async_computation | async-start | bytes 6291456 | tf_op jit(solution)/shard_map/all_to_all | solution.py:67
  104.9 2.9 copy-start.5
  226.0 79.5 %all-to-all-start.3 = ((bf16[64,24,1024]{2,1,0:T(8,128)(2,1)}), bf16[64,24,1024]{2,1,0:T(8,128)(2,1)}, u32[]{:S(2)}, u32[]{:S(2)}) async-start(bf16[64,24,1024]{2,1,0:T(8,128)(2,1)} %bitcast.54), calls=%async_computation.3 | async-start | bytes 6291456 | tf_op jit(solution)/shard_map/all_to_all | solution.py:116

commit v5 on v3

v5 whole, which is shorter than its diff:
```python
import jax
import jax.numpy as jnp
from jax import lax
from jax.sharding import PartitionSpec as P


D = 8192
BLK = 128
KB = 4
PER = 8
RANK_PARTS = (4, 8)


def slot_ranks(row_blocks, total_blocks):
    pair_blocks = row_blocks.reshape(-1)
    onehot = (pair_blocks[:, None] == jnp.arange(total_blocks, dtype=jnp.int32)[None, :]).astype(
        jnp.int32
    )
    before = jnp.cumsum(onehot, axis=0) - onehot
    return pair_blocks, jnp.sum(before * onehot, axis=1)


def pick_rows(values_t, offsets_t):
    lanes = jnp.arange(BLK, dtype=jnp.int32)
    hit = offsets_t[:, None, :] == lanes[None, :, None]
    return jnp.sum(jnp.where(hit, values_t[None, :, :], 0.0), axis=1)


def spread_rows(picked_t, offsets_t):
    lanes = jnp.arange(BLK, dtype=jnp.int32)[:, None]
    out = jnp.zeros((BLK, picked_t.shape[1]), picked_t.dtype)
    for j in range(PER):
        out = jnp.where(offsets_t[j : j + 1, :] == lanes, picked_t[j : j + 1, :], out)
    return out


def butterfly_sum(x, axis):
    size = lax.axis_size(axis)
    step = 1
    while step < size:
        other = lax.ppermute(x, axis, perm=[(i, i ^ step) for i in range(size)])
        x = x + other
        step *= 2
    return x


def exchange(x, owners):
    rows = x.shape[0]
    return lax.all_to_all(
        x.reshape((owners, rows // owners) + x.shape[1:]), "lat", split_axis=0, concat_axis=0, tiled=True
    ).reshape(x.shape)


def device_step(
    activations, center_bias, encoder_weight, encoder_bias, decoder_weight, row_blocks, pick_offsets
):
    group_rows, feature_width = activations.shape
    owners = lax.axis_size("lat")
    owned_blocks = encoder_bias.shape[0] // BLK
    owned_cols = owned_blocks * BLK
    total_blocks = owned_blocks * owners
    capacity = 2 * group_rows * KB // total_blocks
    slot_count = total_blocks * capacity
    per_owner = owned_blocks * capacity
    assert sum(RANK_PARTS) == capacity
    bases = [owned_blocks * sum(RANK_PARTS[:h]) for h in range(len(RANK_PARTS))]
    pair_blocks, rank = slot_ranks(row_blocks, total_blocks)
    owner_of, block_in = pair_blocks // owned_blocks, pair_blocks % owned_blocks
    second = rank >= RANK_PARTS[0]
    in_chunk = jnp.where(second, rank - RANK_PARTS[0], rank)
    chunk_len = jnp.where(second, RANK_PARTS[1], RANK_PARTS[0])
    chunk_base = jnp.where(second, bases[1], bases[0])
    target = owner_of * per_owner + chunk_base + block_in * chunk_len + in_chunk
    slots = jnp.arange(slot_count, dtype=jnp.int32)

    pair_hot = target[None, :] == slots[:, None]
    row_hot = jnp.any(pair_hot.reshape(slot_count, group_rows, KB), axis=2).astype(jnp.bfloat16)
    pair_hot = pair_hot.astype(jnp.bfloat16)
    row_hot_owner = row_hot.reshape(owners, per_owner, group_rows)

    centered = (activations - center_bias[None, :]).astype(jnp.bfloat16)
    offs_plus = (pick_offsets.reshape(-1, PER) + 1).astype(jnp.bfloat16)
    out_offs_t = lax.dot_general(
        offs_plus, pair_hot, (((0,), (1,)), ((), ())), preferred_element_type=jnp.float32
    ).astype(jnp.int32)
    out_offs = out_offs_t.reshape(PER, owners, per_owner).transpose(1, 0, 2)
    got_offs = lax.all_to_all(out_offs, "lat", split_axis=0, concat_axis=0, tiled=True)
    col_block = jnp.arange(owned_cols, dtype=jnp.int32) // BLK

    def own_half(full_t, slot_block):
        parts = full_t.reshape(owned_blocks, BLK, slot_block.shape[0])
        sel = jnp.arange(owned_blocks, dtype=jnp.int32)[:, None, None] == slot_block[None, None, :]
        return jnp.sum(jnp.where(sel, parts, 0.0), axis=0)

    def widen(narrow_t, slot_block):
        tiled = jnp.tile(narrow_t, (owned_blocks, 1))
        return jnp.where(col_block[:, None] == slot_block[None, :], tiled, jnp.zeros_like(tiled))

    got_rows, offs_t, latent_wide_t, blocks_of, rebuilt = [], [], [], [], None
    for h, part in enumerate(RANK_PARTS):
        width = owned_blocks * part
        chunk_slots = owners * width
        slot_block = (jnp.arange(chunk_slots, dtype=jnp.int32) // part) % owned_blocks
        hot_h = row_hot_owner[:, bases[h] : bases[h] + width].reshape(chunk_slots, group_rows)
        outgoing = jnp.dot(hot_h, centered, preferred_element_type=jnp.float32).astype(jnp.bfloat16)
        rows_h = exchange(outgoing, owners)
        offs_h = got_offs[:, :, bases[h] : bases[h] + width].transpose(1, 0, 2)
        offs_h = offs_h.reshape(PER, chunk_slots) - 1
        partial_t = lax.dot_general(
            encoder_weight, rows_h, (((0,), (1,)), ((), ())), preferred_element_type=jnp.float32
        )
        summed = butterfly_sum(pick_rows(own_half(partial_t, slot_block), offs_h), "row")
        bias_t = own_half(jnp.broadcast_to(encoder_bias[:, None], (owned_cols, chunk_slots)), slot_block)
        pre_picked = summed + pick_rows(bias_t, offs_h)
        latent_h = widen(spread_rows(pre_picked, offs_h).astype(jnp.bfloat16), slot_block)
        decoded = lax.dot_general(
            latent_h, decoder_weight, (((0,), (0,)), ((), ())), preferred_element_type=jnp.float32
        ).astype(jnp.bfloat16)
        returned = exchange(decoded, owners)
        term = lax.dot_general(
            hot_h, returned, (((0,), (0,)), ((), ())), preferred_element_type=jnp.float32
        )
        rebuilt = term if rebuilt is None else rebuilt + term
        got_rows.append(rows_h)
        offs_t.append(offs_h)
        latent_wide_t.append(latent_h)
        blocks_of.append(slot_block)

    recon_error = (center_bias[None, :] + rebuilt) - activations
    loss_part = jnp.sum(recon_error * recon_error, axis=1)
    error_b = recon_error.astype(jnp.bfloat16)
    out_error = jnp.dot(row_hot, error_b, preferred_element_type=jnp.float32).astype(jnp.bfloat16)
    got_error = exchange(out_error, owners).reshape(owners, per_owner, feature_width)
    errors = [
        got_error[:, bases[h] : bases[h] + owned_blocks * part].reshape(-1, feature_width)
        for h, part in enumerate(RANK_PARTS)
    ]

    decoder_grad = None
    dlatent_parts = []
    for h in range(len(RANK_PARTS)):
        term = lax.dot_general(
            latent_wide_t[h], errors[h], (((1,), (0,)), ((), ())), preferred_element_type=jnp.float32
        )
        decoder_grad = term if decoder_grad is None else decoder_grad + term
        dlatent_t = lax.dot_general(
            decoder_weight, errors[h], (((1,), (1,)), ((), ())), preferred_element_type=jnp.float32
        )
        dlatent_parts.append(pick_rows(own_half(dlatent_t, blocks_of[h]), offs_t[h]))
    decoder_grad = decoder_grad.astype(jnp.bfloat16)
    flat = jnp.concatenate([p.reshape(-1) for p in dlatent_parts] + [loss_part])
    reduced = butterfly_sum(flat, "row")
    loss_total = reduced[PER * slot_count :]

    encoder_grad, bias_grad = None, None
    start = 0
    for h in range(len(RANK_PARTS)):
        size = offs_t[h].size
        dl_h = reduced[start : start + size].reshape(offs_t[h].shape)
        start += size
        grad_h = widen(spread_rows(dl_h, offs_t[h]).astype(jnp.bfloat16), blocks_of[h])
        term = lax.dot_general(
            got_rows[h], grad_h, (((0,), (1,)), ((), ())), preferred_element_type=jnp.float32
        )
        bias_term = jnp.sum(grad_h.astype(jnp.float32), axis=1)
        encoder_grad = term if encoder_grad is None else encoder_grad + term
        bias_grad = bias_term if bias_grad is None else bias_grad + bias_term
    encoder_grad = encoder_grad.astype(jnp.bfloat16)
    row_loss = loss_total / D
    return (encoder_grad, decoder_grad, bias_grad, row_loss)


def solution(mesh):
    return jax.shard_map(
        device_step,
        mesh=mesh,
        in_specs=(
            P("lat", "row"),
            P("row"),
            P("row", "lat"),
            P("lat"),
            P("lat", "row"),
            P("lat", None),
            P("lat", None, None),
        ),
        out_specs=(P("row", "lat"), P("lat", "row"), P("lat"), P("lat")),
        check_vma=False,
    )
```

time: 341 us -> 355 us (1.041)
  waiting for transfers between devices: 164 us -> 102 us
  local copies, waits for them, and re-layouts: 5.42 us -> 36.3 us
  starting transfers between devices: 59.2 us -> 86.8 us
  other arithmetic: 9.42 us -> 18.6 us
  matrix products: 21.9 us -> 27.6 us
    all_to_all x3 -> x5, waiting for transfers between devices: 148 us -> 81.4 us  [the longest x4 76.7 us: exchange(): lax.all_to_all(x.reshape((owners, rows // owners) + x.shape[1:]), 'lat',...]
    eq x8 -> x16, local copies, waits for them, and re-layouts: 0.67 us -> 19.8 us  [spread_rows(): out = jnp.where(offsets_t[j:j + 1, :] == lanes, picked_t[j:j + 1, :], out)]
    all_to_all x3 -> x5, starting transfers between devices: 24 us -> 40.9 us  [the longest x4 30.3 us: exchange(): lax.all_to_all(x.reshape((owners, rows // owners) + x.shape[1:]), 'lat',...]
    ppermute x6 -> x9, starting transfers between devices: 35.2 us -> 45.9 us  [butterfly_sum(): other = lax.ppermute(x, axis, perm=[(i, i ^ step) for i in range(size)])]
    dot_general x9 -> x16, matrix products: 21.9 us -> 27.6 us  [the longest x2 8.05 us: device_step(): lax.dot_general(hot_h, returned, (((0,), (0,)), ((), ())), preferred_elem...]
    ppermute x6 -> x9, waiting for transfers between devices: 15.7 us -> 21 us  [butterfly_sum(): other = lax.ppermute(x, axis, perm=[(i, i ^ step) for i in range(size)])]
    unnamed x17 -> x93, local copies, waits for them, and re-layouts: 1.88 us -> 5.98 us
    sub x2 -> x4, local copies, waits for them, and re-layouts: 0.21 us -> 4.31 us  [device_step(): offs_h = offs_h.reshape(PER, chunk_slots) - 1]
  transfers between devices with their start and end apart: 9 -> 14, of which waited for: 9 -> 11; matrix products, arithmetic and copies ran while one was open for 2% -> 17% of each run, Pallas kernels for 0% -> 0%
where the time goes in v5:
time: 355 us; the launch traced here: 352 us
  waiting for transfers between devices  102 us (29%)
  starting transfers between devices  86.8 us (24%)
  blocking collectives  78.9 us (22%)
  local copies, waits for them, and re-layouts  36.3 us (10%)
  matrix products  27.6 us (8%)
  other arithmetic  18.6 us (5%)
    all_to_all x1, blocking collectives, exchange(): lax.all_to_all(x.reshape((owners, rows // owners) + x.shape[1:]), 'lat',...  78.9 us
    all_to_all x4, waiting for transfers between devices, exchange(): lax.all_to_all(x.reshape((owners, rows // owners) + x.shape[1:]), 'lat',...  76.7 us
    ppermute x9, starting transfers between devices, butterfly_sum(): other = lax.ppermute(x, axis, perm=[(i, i ^ step) for i in range(size)])  45.9 us
    all_to_all x4, starting transfers between devices, exchange(): lax.all_to_all(x.reshape((owners, rows // owners) + x.shape[1:]), 'lat',...  30.3 us
    ppermute x9, waiting for transfers between devices, butterfly_sum(): other = lax.ppermute(x, axis, perm=[(i, i ^ step) for i in range(size)])  21 us
    eq x16, local copies, waits for them, and re-layouts, spread_rows(): out = jnp.where(offsets_t[j:j + 1, :] == lanes, picked_t[j:j + 1, :], out)  19.8 us
    all_to_all x1, starting transfers between devices, device_step(): lax.all_to_all(out_offs, 'lat', split_axis=0, concat_axis=0, tiled=True)  10.6 us
    dot_general x2, matrix products, device_step(): lax.dot_general(hot_h, returned, (((0,), (0,)), ((), ())), preferred_elem...  8.05 us
  transfers between devices with their start and end apart: 14, of which 11 were waited for; matrix products, arithmetic and copies ran while one was open for 17% of the time, Pallas kernels for 0%

profile of v5, /device:TPU:6, one launch (start us, length us, event | category | flops | bytes accessed | tf_op | source)
XLA Modules:
  0.0 352.3 jit_solution(17265382552744150674)
XLA Ops:
  4.9 10.6 %all-to-all-start.1 = ((s32[64,1,192]{2,1,0:T(1,128)}), s32[64,1,192]{2,1,0:T(1,128)S(1)}, u32[]{:S(2)}, u32[]{:S(2)}) async-start(s32[64,1,192]{2,1,0:T(1,128)} %reshape.1905), calls=%async_computation.1 | async-start | bytes 131072 | tf_op jit(solution)/shard_map/all_to_all | solution.py:87
  18.9 4.7 %all-to-all-done.1 = s32[64,1,192]{2,1,0:T(1,128)S(1)} async-done(((s32[64,1,192]{2,1,0:T(1,128)}), s32[64,1,192]{2,1,0:T(1,128)S(1)}, u32[]{:S(2)}, u32[]{:S(2)}) %all-to-all-start.1) | async-done | bytes 49184 | tf_op jit(solution)/shard_map/all_to_all | solution.py:87
  23.5 6.6 %all-to-all-start = ((bf16[64,8,1024]{2,1,0:T(8,128)(2,1)}), bf16[64,8,1024]{2,1,0:T(8,128)(2,1)S(1)}, u32[]{:S(2)}, u32[]{:S(2)}) async-start(bf16[64,8,1024]{2,1,0:T(8,128)(2,1)} %fusion.6), calls=%async_computation | async-start | bytes 2097152 | tf_op jit(solution)/shard_map/all_to_all | solution.py:49
  32.2 26.8 %all-to-all-done = bf16[64,8,1024]{2,1,0:T(8,128)(2,1)S(1)} async-done(((bf16[64,8,1024]{2,1,0:T(8,128)(2,1)}), bf16[64,8,1024]{2,1,0:T(8,128)(2,1)S(1)}, u32[]{:S(2)}, u32[]{:S(2)}) %all-to-all-start) | async-done | bytes 1048608 | tf_op jit(solution)/shard_map/all_to_all | solution.py:49
  60.0 5.7 %all-to-all-start.3 = ((bf16[64,16,1024]{2,1,0:T(8,128)(2,1)}), bf16[64,16,1024]{2,1,0:T(8,128)(2,1)S(1)}, u32[]{:S(2)}, u32[]{:S(2)}) async-start(bf16[64,16,1024]{2,1,0:T(8,128)(2,1)} %bitcast.116), calls=%async_computation.3 | async-start | bytes 4194304 | tf_op jit(solution)/shard_map/all_to_all | solution.py:49
  76.4 4.3 %collective-permute-start = (f32[8,512]{1,0:T(8,128)S(1)}, f32[8,512]{1,0:T(8,128)S(1)}, u32[]{:S(2)}, u32[]{:S(2)}) collective-permute-start(f32[8,512]{1,0:T(8,128)S(1)} %get-tuple-element.22), channel_id=1, source_target_pairs={{0,1},{1,0},{2,3},{3,2},{4,5},{5,4},{6,7},{7,6},{8,9},{9,8},{10,11... | collective-permute-start | bytes 49160 | tf_op jit(solution)/shard_map/ppermute | solution.py:41
  82.4 6.1 %collective-permute-start.1 = (f32[8,512]{1,0:T(8,128)S(1)}, f32[8,512]{1,0:T(8,128)S(1)}, u32[]{:S(2)}, u32[]{:S(2)}) collective-permute-start(f32[8,512]{1,0:T(8,128)S(1)} %add.220), channel_id=1, source_target_pairs={{0,2},{1,3},{2,0},{3,1},{4,6},{5,7},{6,4},{7,5},{8,10},{9,11},{10,... | collective-permute-start | bytes 49160 | tf_op jit(solution)/shard_map/ppermute | solution.py:41
  91.0 9.1 %collective-permute-start.2 = (f32[8,512]{1,0:T(8,128)}, f32[8,512]{1,0:T(8,128)}, u32[]{:S(2)}, u32[]{:S(2)}) collective-permute-start(f32[8,512]{1,0:T(8,128)} %add.221), channel_id=1, source_target_pairs={{0,4},{1,5},{2,6},{3,7},{4,0},{5,1},{6,2},{7,3},{8,12},{9,13},{10,... | collective-permute-start | bytes 49160 | tf_op jit(solution)/shard_map/ppermute | solution.py:41
  113.8 3.2 all-to-all-done.3
  116.9 7.5 %all-to-all-start.2 = ((bf16[64,8,1024]{2,1,0:T(8,128)(2,1)}), bf16[64,8,1024]{2,1,0:T(8,128)(2,1)}, u32[]{:S(2)}, u32[]{:S(2)}) async-start(bf16[64,8,1024]{2,1,0:T(8,128)(2,1)} %fusion.7), calls=%async_computation.2 | async-start | bytes 2097152 | tf_op jit(solution)/shard_map/all_to_all | solution.py:49
  132.4 3.4 collective-permute-start.3
  138.2 4.7 %collective-permute-start.4 = (f32[8,1024]{1,0:T(8,128)S(1)}, f32[8,1024]{1,0:T(8,128)S(1)}, u32[]{:S(2)}, u32[]{:S(2)}) collective-permute-start(f32[8,1024]{1,0:T(8,128)S(1)} %add.225), channel_id=1, source_target_pairs={{0,2},{1,3},{2,0},{3,1},{4,6},{5,7},{6,4},{7,5},{8,10},{9,11},{10,... | collective-permute-start | bytes 98312 | tf_op jit(solution)/shard_map/ppermute | solution.py:41
  145.9 8.8 %collective-permute-start.5 = (f32[8,1024]{1,0:T(8,128)}, f32[8,1024]{1,0:T(8,128)}, u32[]{:S(2)}, u32[]{:S(2)}) collective-permute-start(f32[8,1024]{1,0:T(8,128)} %add.226), channel_id=1, source_target_pairs={{0,4},{1,5},{2,6},{3,7},{4,0},{5,1},{6,2},{7,3},{8,12},{9,13},{10,... | collective-permute-start | bytes 98312 | tf_op jit(solution)/shard_map/ppermute | solution.py:41
  170.1 2.8 convolution_convert_fusion.1
  172.9 10.5 %all-to-all-start.4 = ((bf16[64,16,1024]{2,1,0:T(8,128)(2,1)}), bf16[64,16,1024]{2,1,0:T(8,128)(2,1)}, u32[]{:S(2)}, u32[]{:S(2)}) async-start(bf16[64,16,1024]{2,1,0:T(8,128)(2,1)} %bitcast.117), calls=%async_computation.4 | async-start | bytes 4194304 | tf_op jit(solution)/shard_map/all_to_all | solution.py:49
  184.3 3.5 convolution_bitcast_fusion
  187.8 46.8 %all-to-all-done.4 = bf16[64,16,1024]{2,1,0:T(8,128)(2,1)} async-done(((bf16[64,16,1024]{2,1,0:T(8,128)(2,1)}), bf16[64,16,1024]{2,1,0:T(8,128)(2,1)}, u32[]{:S(2)}, u32[]{:S(2)}) %all-to-all-start.4) | async-done | bytes 2097184 | tf_op jit(solution)/shard_map/all_to_all | solution.py:49
  234.6 4.6 %multiply_reduce_fusion = (f32[192]{0:T(256)S(1)}, bf16[192,1024]{1,0:T(8,128)(2,1)S(1)}) fusion(f32[192,1024]{1,0:T(8,128)S(1)} %copy-done.3, f32[192,1024]{1,0:T(8,128)} %convolution_bitcast_fusion, bf16[64,16,1024]{2,1,0:T(8,128)(2,1)} %all-to-all-done.4, pred[64,16,192]{2,1,0:T(8,128)(4,1)} %copy-done.13, f32[1024]{0:T(1024)} %param.8), kind=kOutput, calls=%fused_computation.47 | convolution fusion | flops 403832640 | bytes 4264704 | tf_op jit(solution)/shard_map/dot_general | solution.py:120
  240.3 78.9 %all_to_all.30 = bf16[64,24,1024]{2,1,0:T(8,128)(2,1)S(1)} all-to-all(bf16[64,24,1024]{2,1,0:T(8,128)(2,1)S(1)} %bitcast.115), channel_id=1, replica_groups=mesh['lat'=64,'row'=8] {'lat'}, dimensions={0} | all-to-all | bytes 6291456 | tf_op jit(solution)/shard_map/all_to_all | solution.py:49
  322.1 3.4 collective-permute-start.6
  325.5 2.6 collective-permute-done.6
  328.2 4.3 %collective-permute-start.7 = (f32[12480]{0:T(1024)S(1)}, f32[12480]{0:T(1024)S(1)}, u32[]{:S(2)}, u32[]{:S(2)}) collective-permute-start(f32[12480]{0:T(1024)S(1)} %fusion.70), channel_id=1, source_target_pairs={{0,2},{1,3},{2,0},{3,1},{4,6},{5,7},{6,4},{7,5},{8,10},{9,11},{10,... | collective-permute-start | bytes 149768 | tf_op jit(solution)/shard_map/ppermute | solution.py:41
  332.5 2.6 collective-permute-done.7
  337.1 8.5 %collective-permute-done.8 = f32[12480]{0:T(1024)S(1)} collective-permute-done((f32[12480]{0:T(1024)S(1)}, f32[12480]{0:T(1024)S(1)}, u32[]{:S(2)}, u32[]{:S(2)}) %collective-permute-start.8) | collective-permute-done | bytes 49952 | tf_op jit(solution)/shard_map/ppermute | solution.py:41
  (202 shorter events, 80.7 us)
Async XLA Ops:
  0.6 110.9 %copy-start = (bf16[256,1024]{1,0:T(8,128)(2,1)S(1)}, bf16[256,1024]{1,0:T(8,128)(2,1)}, u32[]{:S(2)}) copy-start(bf16[256,1024]{1,0:T(8,128)(2,1)} %param.11) | copy-start | bytes 1572868
  4.9 18.6 %all-to-all-start.1 = ((s32[64,1,192]{2,1,0:T(1,128)}), s32[64,1,192]{2,1,0:T(1,128)S(1)}, u32[]{:S(2)}, u32[]{:S(2)}) async-start(s32[64,1,192]{2,1,0:T(1,128)} %reshape.1905), calls=%async_computation.1 | async-start | bytes 131072 | tf_op jit(solution)/shard_map/all_to_all | solution.py:87
  23.5 35.5 %all-to-all-start = ((bf16[64,8,1024]{2,1,0:T(8,128)(2,1)}), bf16[64,8,1024]{2,1,0:T(8,128)(2,1)S(1)}, u32[]{:S(2)}, u32[]{:S(2)}) async-start(bf16[64,8,1024]{2,1,0:T(8,128)(2,1)} %fusion.6), calls=%async_computation | async-start | bytes 2097152 | tf_op jit(solution)/shard_map/all_to_all | solution.py:49
  30.2 28.8 %copy-start.13 = (pred[64,16,192]{2,1,0:T(8,128)(4,1)}, pred[64,16,192]{2,1,0:T(8,128)(4,1)S(1)}, u32[]{:S(2)}) copy-start(pred[64,16,192]{2,1,0:T(8,128)(4,1)S(1)} %slice.313) | copy-start | bytes 589828
  60.0 57.0 %all-to-all-start.3 = ((bf16[64,16,1024]{2,1,0:T(8,128)(2,1)}), bf16[64,16,1024]{2,1,0:T(8,128)(2,1)S(1)}, u32[]{:S(2)}, u32[]{:S(2)}) async-start(bf16[64,16,1024]{2,1,0:T(8,128)(2,1)} %bitcast.116), calls=%async_computation.3 | async-start | bytes 4194304 | tf_op jit(solution)/shard_map/all_to_all | solution.py:49
  72.6 27.5 %copy-start.9 = (s32[8,64,8]{2,0,1:T(8,128)S(1)}, s32[8,64,8]{2,0,1:T(8,128)}, u32[]{:S(2)}) copy-start(s32[8,64,8]{2,0,1:T(8,128)} %copy-done.8) | copy-start | bytes 49156
  76.4 6.0 %collective-permute-start = (f32[8,512]{1,0:T(8,128)S(1)}, f32[8,512]{1,0:T(8,128)S(1)}, u32[]{:S(2)}, u32[]{:S(2)}) collective-permute-start(f32[8,512]{1,0:T(8,128)S(1)} %get-tuple-element.22), channel_id=1, source_target_pairs={{0,1},{1,0},{2,3},{3,2},{4,5},{5,4},{6,7},{7,6},{8,9},{9,8},{10,11... | collective-permute-start | bytes 49160 | tf_op jit(solution)/shard_map/ppermute | solution.py:41
  82.4 8.0 %collective-permute-start.1 = (f32[8,512]{1,0:T(8,128)S(1)}, f32[8,512]{1,0:T(8,128)S(1)}, u32[]{:S(2)}, u32[]{:S(2)}) collective-permute-start(f32[8,512]{1,0:T(8,128)S(1)} %add.220), channel_id=1, source_target_pairs={{0,2},{1,3},{2,0},{3,1},{4,6},{5,7},{6,4},{7,5},{8,10},{9,11},{10,... | collective-permute-start | bytes 49160 | tf_op jit(solution)/shard_map/ppermute | solution.py:41
  91.0 18.9 %collective-permute-start.2 = (f32[8,512]{1,0:T(8,128)}, f32[8,512]{1,0:T(8,128)}, u32[]{:S(2)}, u32[]{:S(2)}) collective-permute-start(f32[8,512]{1,0:T(8,128)} %add.221), channel_id=1, source_target_pairs={{0,4},{1,5},{2,6},{3,7},{4,0},{5,1},{6,2},{7,3},{8,12},{9,13},{10,... | collective-permute-start | bytes 49160 | tf_op jit(solution)/shard_map/ppermute | solution.py:41
  116.9 56.0 %all-to-all-start.2 = ((bf16[64,8,1024]{2,1,0:T(8,128)(2,1)}), bf16[64,8,1024]{2,1,0:T(8,128)(2,1)}, u32[]{:S(2)}, u32[]{:S(2)}) async-start(bf16[64,8,1024]{2,1,0:T(8,128)(2,1)} %fusion.7), calls=%async_computation.2 | async-start | bytes 2097152 | tf_op jit(solution)/shard_map/all_to_all | solution.py:49
  132.4 5.8 %collective-permute-start.3 = (f32[8,1024]{1,0:T(8,128)S(1)}, f32[8,1024]{1,0:T(8,128)S(1)}, u32[]{:S(2)}, u32[]{:S(2)}) collective-permute-start(f32[8,1024]{1,0:T(8,128)S(1)} %get-tuple-element.20), channel_id=1, source_target_pairs={{0,1},{1,0},{2,3},{3,2},{4,5},{5,4},{6,7},{7,6},{8,9},{9,8},{10,11... | collective-permute-start | bytes 98312 | tf_op jit(solution)/shard_map/ppermute | solution.py:41
  138.2 7.0 %collective-permute-start.4 = (f32[8,1024]{1,0:T(8,128)S(1)}, f32[8,1024]{1,0:T(8,128)S(1)}, u32[]{:S(2)}, u32[]{:S(2)}) collective-permute-start(f32[8,1024]{1,0:T(8,128)S(1)} %add.225), channel_id=1, source_target_pairs={{0,2},{1,3},{2,0},{3,1},{4,6},{5,7},{6,4},{7,5},{8,10},{9,11},{10,... | collective-permute-start | bytes 98312 | tf_op jit(solution)/shard_map/ppermute | solution.py:41
  145.9 21.6 %collective-permute-start.5 = (f32[8,1024]{1,0:T(8,128)}, f32[8,1024]{1,0:T(8,128)}, u32[]{:S(2)}, u32[]{:S(2)}) collective-permute-start(f32[8,1024]{1,0:T(8,128)} %add.226), channel_id=1, source_target_pairs={{0,4},{1,5},{2,6},{3,7},{4,0},{5,1},{6,2},{7,3},{8,12},{9,13},{10,... | collective-permute-start | bytes 98312 | tf_op jit(solution)/shard_map/ppermute | solution.py:41
  172.9 61.7 %all-to-all-start.4 = ((bf16[64,16,1024]{2,1,0:T(8,128)(2,1)}), bf16[64,16,1024]{2,1,0:T(8,128)(2,1)}, u32[]{:S(2)}, u32[]{:S(2)}) async-start(bf16[64,16,1024]{2,1,0:T(8,128)(2,1)} %bitcast.117), calls=%async_computation.4 | async-start | bytes 4194304 | tf_op jit(solution)/shard_map/all_to_all | solution.py:49
  321.5 25.1 %copy-start.31 = (s32[512]{0:T(512)S(1)}, s32[512]{0:T(512)}, u32[]{:S(2)}) copy-start(s32[512]{0:T(512)} %eq.796) | copy-start | bytes 6148
  321.5 25.1 %copy-start.32 = (s32[512]{0:T(512)S(1)}, s32[512]{0:T(512)}, u32[]{:S(2)}) copy-start(s32[512]{0:T(512)} %eq.809) | copy-start | bytes 6148
  321.5 25.1 %copy-start.33 = (s32[512]{0:T(512)S(1)}, s32[512]{0:T(512)}, u32[]{:S(2)}) copy-start(s32[512]{0:T(512)} %eq.813) | copy-start | bytes 6148
  321.5 25.1 %copy-start.34 = (s32[512]{0:T(512)S(1)}, s32[512]{0:T(512)}, u32[]{:S(2)}) copy-start(s32[512]{0:T(512)} %eq.817) | copy-start | bytes 6148
  321.5 25.1 %copy-start.35 = (s32[512]{0:T(512)S(1)}, s32[512]{0:T(512)}, u32[]{:S(2)}) copy-start(s32[512]{0:T(512)} %eq.821) | copy-start | bytes 6148
  321.5 25.1 %copy-start.36 = (s32[512]{0:T(512)S(1)}, s32[512]{0:T(512)}, u32[]{:S(2)}) copy-start(s32[512]{0:T(512)} %eq.825) | copy-start | bytes 6148
  321.5 25.2 %copy-start.19 = (s32[512]{0:T(512)S(1)}, s32[512]{0:T(512)}, u32[]{:S(2)}) copy-start(s32[512]{0:T(512)} %copy-done.18) | copy-start | bytes 6148
  322.1 6.0 %collective-permute-start.6 = (f32[12480]{0:T(1024)S(1)}, f32[12480]{0:T(1024)S(1)}, u32[]{:S(2)}, u32[]{:S(2)}) collective-permute-start(f32[12480]{0:T(1024)S(1)} %pad_maximum_fusion), channel_id=1, source_target_pairs={{0,1},{1,0},{2,3},{3,2},{4,5},{5,4},{6,7},{7,6},{8,9},{9,8},{10,11... | collective-permute-start | bytes 149768 | tf_op jit(solution)/shard_map/ppermute | solution.py:41
  328.2 6.9 %collective-permute-start.7 = (f32[12480]{0:T(1024)S(1)}, f32[12480]{0:T(1024)S(1)}, u32[]{:S(2)}, u32[]{:S(2)}) collective-permute-start(f32[12480]{0:T(1024)S(1)} %fusion.70), channel_id=1, source_target_pairs={{0,2},{1,3},{2,0},{3,1},{4,6},{5,7},{6,4},{7,5},{8,10},{9,11},{10,... | collective-permute-start | bytes 149768 | tf_op jit(solution)/shard_map/ppermute | solution.py:41
  335.1 10.5 %collective-permute-start.8 = (f32[12480]{0:T(1024)S(1)}, f32[12480]{0:T(1024)S(1)}, u32[]{:S(2)}, u32[]{:S(2)}) collective-permute-start(f32[12480]{0:T(1024)S(1)} %add.232), channel_id=1, source_target_pairs={{0,4},{1,5},{2,6},{3,7},{4,0},{5,1},{6,2},{7,3},{8,12},{9,13},{10,... | collective-permute-start | bytes 149768 | tf_op jit(solution)/shard_map/ppermute | solution.py:41
  (34 other events, 418.5 us)

commit v6 on v3

--- a/solution.py
+++ b/solution.py
@@ -64,21 +64,19 @@
     centered = (activations - center_bias[None, :]).astype(jnp.bfloat16)
     outgoing = jnp.dot(row_hot, centered, preferred_element_type=jnp.float32).astype(jnp.bfloat16)
     offs_plus = (pick_offsets.reshape(-1, PER) + 1).astype(jnp.bfloat16)
-    out_offs_t = lax.dot_general(
-        offs_plus, pair_hot, (((0,), (1,)), ((), ())), preferred_element_type=jnp.float32
-    ).astype(jnp.int32)
-    out_offs = out_offs_t.reshape(PER, owners, per_owner).transpose(1, 0, 2)
-
-    got_offs = lax.all_to_all(out_offs, "lat", split_axis=0, concat_axis=0, tiled=True)
-    got_rows = lax.all_to_all(
-        outgoing.reshape(owners, per_owner, feature_width),
+    out_offs = jnp.dot(pair_hot, offs_plus, preferred_element_type=jnp.float32).astype(jnp.bfloat16)
+    payload = jnp.concatenate(
+        [outgoing, out_offs, jnp.zeros((slot_count, BLK - PER), jnp.bfloat16)], axis=1
+    )
+    got = lax.all_to_all(
+        payload.reshape(owners, per_owner, feature_width + BLK),
         "lat",
         split_axis=0,
         concat_axis=0,
         tiled=True,
-    )
-    got_rows = got_rows.reshape(slot_count, feature_width)
-    offs_t = got_offs.transpose(1, 0, 2).reshape(PER, slot_count) - 1
+    ).reshape(slot_count, feature_width + BLK)
+    got_rows = got[:, :feature_width]
+    offs_t = got[:, feature_width : feature_width + PER].astype(jnp.int32).T - 1
 
     slot_block = (slots // capacity) % owned_blocks
     col_block = jnp.arange(owned_cols, dtype=jnp.int32) // BLK

time: 341 us -> 342 us (level)
  starting transfers between devices: 59.2 us -> 50.7 us
  local copies, waits for them, and re-layouts: 5.42 us -> 11.3 us
    all_to_all x2 -> x1, starting transfers between devices: 18.2 us -> 10.8 us  [per_device(): lax.all_to_all(payload.reshape(owners, per_owner, feature_width + BLK), '...]
    all_to_all x2 -> x1, waiting for transfers between devices: 76 us -> 82.1 us  [per_device(): lax.all_to_all(payload.reshape(owners, per_owner, feature_width + BLK), '...]
    concatenate x0 -> x2, local copies, waits for them, and re-layouts: none -> 5.87 us  [per_device(): jnp.concatenate([outgoing, out_offs, jnp.zeros((slot_count, BLK - PER), j...]
    ppermute x6, waiting for transfers between devices: 15.7 us -> 11.5 us  [butterfly_sum(): other = lax.ppermute(x, axis, perm=[(i, i ^ step) for i in range(size)])]
  transfers between devices with their start and end apart: 9 -> 8, of which waited for: 9 -> 6; matrix products, arithmetic and copies ran while one was open for 2% -> 2% of each run, Pallas kernels for 0% -> 0%
where the time goes in v6:
time: 342 us; the launch traced here: 341 us
  waiting for transfers between devices  166 us (49%)
  blocking collectives  79.3 us (23%)
  starting transfers between devices  50.7 us (15%)
  matrix products  20.3 us (6%)
  other arithmetic  12.5 us (4%)
  local copies, waits for them, and re-layouts  11.3 us (3%)
    all_to_all x1, waiting for transfers between devices, per_device(): lax.all_to_all(payload.reshape(owners, per_owner, feature_width + BLK), '...  82.1 us
    all_to_all x1, blocking collectives, per_device(): lax.all_to_all(decoded.reshape(owners, per_owner, feature_width), 'lat',...  79.3 us
    all_to_all x1, waiting for transfers between devices, per_device(): lax.all_to_all(out_error.reshape(owners, per_owner, feature_width), 'lat'...  72.4 us
    ppermute x6, starting transfers between devices, butterfly_sum(): other = lax.ppermute(x, axis, perm=[(i, i ^ step) for i in range(size)])  34.1 us
    ppermute x6, waiting for transfers between devices, butterfly_sum(): other = lax.ppermute(x, axis, perm=[(i, i ^ step) for i in range(size)])  11.5 us
    all_to_all x1, starting transfers between devices, per_device(): lax.all_to_all(payload.reshape(owners, per_owner, feature_width + BLK), '...  10.8 us
  transfers between devices with their start and end apart: 8, of which 6 were waited for; matrix products, arithmetic and copies ran while one was open for 2% of the time, Pallas kernels for 0%

profile of v6, /device:TPU:6, one launch (start us, length us, event | category | flops | bytes accessed | tf_op | source)
XLA Modules:
  0.0 341.2 jit_solution(10966293274827889757)
XLA Ops:
  6.1 2.9 maximum_maximum_fusion
  8.9 5.8 %copy.46 = bf16[1536,1152]{1,0:T(8,128)(2,1)} copy(bf16[1536,1152]{0,1:T(8,128)(2,1)} %maximum_maximum_fusion) | data formatting | bytes 7077888 | tf_op jit(solution)/shard_map/concatenate | solution.py:68
  14.7 10.8 %all-to-all-start = ((bf16[64,24,1152]{2,1,0:T(8,128)(2,1)}), bf16[64,24,1152]{2,1,0:T(8,128)(2,1)}, u32[]{:S(2)}, u32[]{:S(2)}) async-start(bf16[64,24,1152]{2,1,0:T(8,128)(2,1)} %bitcast.45), calls=%async_computation | async-start | bytes 7077888 | tf_op jit(solution)/shard_map/all_to_all | solution.py:71
  25.6 82.1 %all-to-all-done = bf16[64,24,1152]{2,1,0:T(8,128)(2,1)} async-done(((bf16[64,24,1152]{2,1,0:T(8,128)(2,1)}), bf16[64,24,1152]{2,1,0:T(8,128)(2,1)}, u32[]{:S(2)}, u32[]{:S(2)}) %all-to-all-start) | async-done | bytes 3538976 | tf_op jit(solution)/shard_map/all_to_all | solution.py:71
  108.8 3.0 fusion.4
  112.5 1.5 select_reduce_fusion.2
  114.0 4.1 %collective-permute-start = (f32[8,1536]{1,0:T(8,128)S(1)}, f32[8,1536]{1,0:T(8,128)S(1)}, u32[]{:S(2)}, u32[]{:S(2)}) collective-permute-start(f32[8,1536]{1,0:T(8,128)S(1)} %get-tuple-element.40), channel_id=1, source_target_pairs={{0,1},{1,0},{2,3},{3,2},{4,5},{5,4},{6,7},{7,6},{8,9},{9,8},{10,11... | collective-permute-start | bytes 147464 | tf_op jit(solution)/shard_map/ppermute | solution.py:40
  118.1 2.1 collective-permute-done
  120.2 6.1 %collective-permute-start.1 = (f32[8,1536]{1,0:T(8,128)S(1)}, f32[8,1536]{1,0:T(8,128)S(1)}, u32[]{:S(2)}, u32[]{:S(2)}) collective-permute-start(f32[8,1536]{1,0:T(8,128)S(1)} %add.99), channel_id=1, source_target_pairs={{0,2},{1,3},{2,0},{3,1},{4,6},{5,7},{6,4},{7,5},{8,10},{9,11},{10,... | collective-permute-start | bytes 147464 | tf_op jit(solution)/shard_map/ppermute | solution.py:40
  126.3 2.0 collective-permute-done.1
  128.4 9.5 %collective-permute-start.2 = (f32[8,1536]{1,0:T(8,128)S(1)}, f32[8,1536]{1,0:T(8,128)S(1)}, u32[]{:S(2)}, u32[]{:S(2)}) collective-permute-start(f32[8,1536]{1,0:T(8,128)S(1)} %add.100), channel_id=1, source_target_pairs={{0,4},{1,5},{2,6},{3,7},{4,0},{5,1},{6,2},{7,3},{8,12},{9,13},{10,... | collective-permute-start | bytes 147464 | tf_op jit(solution)/shard_map/ppermute | solution.py:40
  137.9 3.1 slice_reduce_fusion.7
  142.8 79.3 %all_to_all.15 = bf16[64,24,1024]{2,1,0:T(8,128)(2,1)S(1)} all-to-all(bf16[64,24,1024]{2,1,0:T(8,128)(2,1)S(1)} %bitcast.48), channel_id=1, replica_groups=mesh['lat'=64,'row'=8] {'lat'}, dimensions={0} | all-to-all | bytes 6291456 | tf_op jit(solution)/shard_map/all_to_all | solution.py:106
  223.0 2.8 convolution_convert_fusion
  225.9 5.8 %all-to-all-start.2 = ((bf16[64,24,1024]{2,1,0:T(8,128)(2,1)}), bf16[64,24,1024]{2,1,0:T(8,128)(2,1)}, u32[]{:S(2)}, u32[]{:S(2)}) async-start(bf16[64,24,1024]{2,1,0:T(8,128)(2,1)} %bitcast.46), calls=%async_computation.2 | async-start | bytes 6291456 | tf_op jit(solution)/shard_map/all_to_all | solution.py:120
  233.0 72.4 %all-to-all-done.2 = bf16[64,24,1024]{2,1,0:T(8,128)(2,1)} async-done(((bf16[64,24,1024]{2,1,0:T(8,128)(2,1)}), bf16[64,24,1024]{2,1,0:T(8,128)(2,1)}, u32[]{:S(2)}, u32[]{:S(2)}) %all-to-all-start.2) | async-done | bytes 3145760 | tf_op jit(solution)/shard_map/all_to_all | solution.py:120
  305.3 2.9 fusion.32
  309.4 3.2 collective-permute-start.3
  312.5 3.3 collective-permute-done.3
  315.9 4.1 %collective-permute-start.4 = (f32[9,1536]{1,0:T(8,128)S(1)}, f32[9,1536]{1,0:T(8,128)S(1)}, u32[]{:S(2)}, u32[]{:S(2)}) collective-permute-start(f32[9,1536]{1,0:T(8,128)S(1)} %fusion.31), channel_id=1, source_target_pairs={{0,2},{1,3},{2,0},{3,1},{4,6},{5,7},{6,4},{7,5},{8,10},{9,11},{10,... | collective-permute-start | bytes 165896 | tf_op jit(solution)/shard_map/ppermute | solution.py:40
  320.3 4.1 %collective-permute-done.4 = f32[9,1536]{1,0:T(8,128)S(1)} collective-permute-done((f32[9,1536]{1,0:T(8,128)S(1)}, f32[9,1536]{1,0:T(8,128)S(1)}, u32[]{:S(2)}, u32[]{:S(2)}) %collective-permute-start.4) | collective-permute-done | bytes 55328 | tf_op jit(solution)/shard_map/ppermute | solution.py:40
  324.4 7.1 %collective-permute-start.5 = (f32[9,1536]{1,0:T(8,128)S(1)}, f32[9,1536]{1,0:T(8,128)S(1)}, u32[]{:S(2)}, u32[]{:S(2)}) collective-permute-start(f32[9,1536]{1,0:T(8,128)S(1)} %add.105), channel_id=1, source_target_pairs={{0,4},{1,5},{2,6},{3,7},{4,0},{5,1},{6,2},{7,3},{8,12},{9,13},{10,... | collective-permute-start | bytes 165896 | tf_op jit(solution)/shard_map/ppermute | solution.py:40
  331.5 3.7 %convolution_convert_fusion.3 = bf16[256,1024]{1,0:T(8,128)(2,1)} fusion(bf16[256,1536]{1,0:T(8,128)(2,1)S(1)} %bitcast.53, bf16[1536,1024]{1,0:T(8,128)(2,1)} %bitcast.14), kind=kOutput, calls=%fused_computation.27 | convolution fusion | flops 805568512 | bytes 4456448 | tf_op jit(solution)/shard_map/dot_general | solution.py:127
  337.4 3.8 %fusion.8 = bf16[1024,256]{1,0:T(8,128)(2,1)} fusion(bf16[1536,1152]{1,0:T(8,128)(2,1)} %bitcast.5, bf16[256,1536]{1,0:T(8,128)(2,1)S(1)} %bitcast.51, s32[1536]{0:T(1024)S(1)} %add_select_fusion, s32[256]{0:T(256)S(1)} %and_select_fusion.1), kind=kOutput, calls=%fused_computation.26 | convolution fusion | flops 806354944 | bytes 4463616 | tf_op jit(solution)/shard_map/dot_general | solution.py:140
  (66 shorter events, 14.5 us)
Async XLA Ops:
  0.6 141.1 %copy-start = (bf16[256,1024]{1,0:T(8,128)(2,1)S(1)}, bf16[256,1024]{1,0:T(8,128)(2,1)}, u32[]{:S(2)}) copy-start(bf16[256,1024]{1,0:T(8,128)(2,1)} %param.13) | copy-start | bytes 1572868
  0.6 2.2 copy-start.4
  0.7 3.2 copy-start.3
  0.7 4.4 %copy-start.5 = (f32[1024]{0:T(1024)S(1)}, f32[1024]{0:T(1024)}, u32[]{:S(2)}) copy-start(f32[1024]{0:T(1024)} %param.10) | copy-start | bytes 12292
  0.7 4.4 %copy-start.1 = (f32[192,1024]{1,0:T(8,128)S(1)}, f32[192,1024]{1,0:T(8,128)}, u32[]{:S(2)}) copy-start(f32[192,1024]{1,0:T(8,128)} %param.9) | copy-start | bytes 2359300
  14.7 93.0 %all-to-all-start = ((bf16[64,24,1152]{2,1,0:T(8,128)(2,1)}), bf16[64,24,1152]{2,1,0:T(8,128)(2,1)}, u32[]{:S(2)}, u32[]{:S(2)}) async-start(bf16[64,24,1152]{2,1,0:T(8,128)(2,1)} %bitcast.45), calls=%async_computation | async-start | bytes 7077888 | tf_op jit(solution)/shard_map/all_to_all | solution.py:71
  108.8 3.3 copy-start.6
  114.0 6.2 %collective-permute-start = (f32[8,1536]{1,0:T(8,128)S(1)}, f32[8,1536]{1,0:T(8,128)S(1)}, u32[]{:S(2)}, u32[]{:S(2)}) collective-permute-start(f32[8,1536]{1,0:T(8,128)S(1)} %get-tuple-element.40), channel_id=1, source_target_pairs={{0,1},{1,0},{2,3},{3,2},{4,5},{5,4},{6,7},{7,6},{8,9},{9,8},{10,11... | collective-permute-start | bytes 147464 | tf_op jit(solution)/shard_map/ppermute | solution.py:40
  120.2 8.1 %collective-permute-start.1 = (f32[8,1536]{1,0:T(8,128)S(1)}, f32[8,1536]{1,0:T(8,128)S(1)}, u32[]{:S(2)}, u32[]{:S(2)}) collective-permute-start(f32[8,1536]{1,0:T(8,128)S(1)} %add.99), channel_id=1, source_target_pairs={{0,2},{1,3},{2,0},{3,1},{4,6},{5,7},{6,4},{7,5},{8,10},{9,11},{10,... | collective-permute-start | bytes 147464 | tf_op jit(solution)/shard_map/ppermute | solution.py:40
  128.4 12.6 %collective-permute-start.2 = (f32[8,1536]{1,0:T(8,128)S(1)}, f32[8,1536]{1,0:T(8,128)S(1)}, u32[]{:S(2)}, u32[]{:S(2)}) collective-permute-start(f32[8,1536]{1,0:T(8,128)S(1)} %add.100), channel_id=1, source_target_pairs={{0,4},{1,5},{2,6},{3,7},{4,0},{5,1},{6,2},{7,3},{8,12},{9,13},{10,... | collective-permute-start | bytes 147464 | tf_op jit(solution)/shard_map/ppermute | solution.py:40
  142.8 79.3 %copy-start.2 = (f32[192,1024]{1,0:T(8,128)S(1)}, f32[192,1024]{1,0:T(8,128)}, u32[]{:S(2)}) copy-start(f32[192,1024]{1,0:T(8,128)} %param.9) | copy-start | bytes 2359300
  225.9 79.5 %all-to-all-start.2 = ((bf16[64,24,1024]{2,1,0:T(8,128)(2,1)}), bf16[64,24,1024]{2,1,0:T(8,128)(2,1)}, u32[]{:S(2)}, u32[]{:S(2)}) async-start(bf16[64,24,1024]{2,1,0:T(8,128)(2,1)} %bitcast.46), calls=%async_computation.2 | async-start | bytes 6291456 | tf_op jit(solution)/shard_map/all_to_all | solution.py:120
  309.4 6.5 %collective-permute-start.3 = (f32[9,1536]{1,0:T(8,128)S(1)}, f32[9,1536]{1,0:T(8,128)S(1)}, u32[]{:S(2)}, u32[]{:S(2)}) collective-permute-start(f32[9,1536]{1,0:T(8,128)S(1)} %select_maximum_fusion), channel_id=1, source_target_pairs={{0,1},{1,0},{2,3},{3,2},{4,5},{5,4},{6,7},{7,6},{8,9},{9,8},{10,11... | collective-permute-start | bytes 165896 | tf_op jit(solution)/shard_map/ppermute | solution.py:40
  315.9 8.5 %collective-permute-start.4 = (f32[9,1536]{1,0:T(8,128)S(1)}, f32[9,1536]{1,0:T(8,128)S(1)}, u32[]{:S(2)}, u32[]{:S(2)}) collective-permute-start(f32[9,1536]{1,0:T(8,128)S(1)} %fusion.31), channel_id=1, source_target_pairs={{0,2},{1,3},{2,0},{3,1},{4,6},{5,7},{6,4},{7,5},{8,10},{9,11},{10,... | collective-permute-start | bytes 165896 | tf_op jit(solution)/shard_map/ppermute | solution.py:40
  324.4 10.9 %collective-permute-start.5 = (f32[9,1536]{1,0:T(8,128)S(1)}, f32[9,1536]{1,0:T(8,128)S(1)}, u32[]{:S(2)}, u32[]{:S(2)}) collective-permute-start(f32[9,1536]{1,0:T(8,128)S(1)} %add.105), channel_id=1, source_target_pairs={{0,4},{1,5},{2,6},{3,7},{4,0},{5,1},{6,2},{7,3},{8,12},{9,13},{10,... | collective-permute-start | bytes 165896 | tf_op jit(solution)/shard_map/ppermute | solution.py:40

commit v7 on v6

--- a/solution.py
+++ b/solution.py
@@ -62,12 +62,16 @@
     pair_hot = pair_hot.astype(jnp.bfloat16)
 
     centered = (activations - center_bias[None, :]).astype(jnp.bfloat16)
-    outgoing = jnp.dot(row_hot, centered, preferred_element_type=jnp.float32).astype(jnp.bfloat16)
     offs_plus = (pick_offsets.reshape(-1, PER) + 1).astype(jnp.bfloat16)
-    out_offs = jnp.dot(pair_hot, offs_plus, preferred_element_type=jnp.float32).astype(jnp.bfloat16)
-    payload = jnp.concatenate(
-        [outgoing, out_offs, jnp.zeros((slot_count, BLK - PER), jnp.bfloat16)], axis=1
+    pair_data = jnp.concatenate(
+        [
+            jnp.repeat(centered, KB, axis=0),
+            offs_plus,
+            jnp.zeros((group_rows * KB, BLK - PER), jnp.bfloat16),
+        ],
+        axis=1,
     )
+    payload = jnp.dot(pair_hot, pair_data, preferred_element_type=jnp.float32).astype(jnp.bfloat16)
     got = lax.all_to_all(
         payload.reshape(owners, per_owner, feature_width + BLK),
         "lat",

time: 342 us -> 347 us (1.015)
  blocking collectives: 79.3 us -> 0 us
  waiting for transfers between devices: 166 us -> 237 us
  starting transfers between devices: 50.7 us -> 58.8 us
  matrix products: 20.3 us -> 28.1 us
    all_to_all x1 -> x0, blocking collectives: 79.3 us -> none  [per_device(): lax.all_to_all(decoded.reshape(owners, per_owner, feature_width), 'lat',...]
    all_to_all x0 -> x1, waiting for transfers between devices: none -> 72.4 us  [per_device(): lax.all_to_all(decoded.reshape(owners, per_owner, feature_width), 'lat',...]
    all_to_all x0 -> x1, starting transfers between devices: none -> 5.91 us  [per_device(): lax.all_to_all(decoded.reshape(owners, per_owner, feature_width), 'lat',...]
    dot_general x2 -> x1, matrix products: 1.96 us -> 6.28 us  [per_device(): jnp.dot(pair_hot, pair_data, preferred_element_type=jnp.float32)]
    concatenate x2 -> x1, local copies, waits for them, and re-layouts: 5.87 us -> 2.03 us  [per_device(): jnp.concatenate([jnp.repeat(centered, KB, axis=0), offs_plus, jnp.zeros((...]
  transfers between devices with their start and end apart: 8 -> 9, of which waited for: 6 -> 7; matrix products, arithmetic and copies ran while one was open for 2% -> 3% of each run, Pallas kernels for 0% -> 0%
where the time goes in v7:
time: 347 us; the launch traced here: 346 us
  waiting for transfers between devices  237 us (68%)
  starting transfers between devices  58.8 us (17%)
  matrix products  28.1 us (8%)
  local copies, waits for them, and re-layouts  11.5 us (3%)
  other arithmetic  9.72 us (3%)
    all_to_all x1, waiting for transfers between devices, per_device(): lax.all_to_all(payload.reshape(owners, per_owner, feature_width + BLK), '...  82.1 us
    all_to_all x1, waiting for transfers between devices, per_device(): lax.all_to_all(out_error.reshape(owners, per_owner, feature_width), 'lat'...  72.5 us
    all_to_all x1, waiting for transfers between devices, per_device(): lax.all_to_all(decoded.reshape(owners, per_owner, feature_width), 'lat',...  72.4 us
    ppermute x6, starting transfers between devices, butterfly_sum(): other = lax.ppermute(x, axis, perm=[(i, i ^ step) for i in range(size)])  36.3 us
    all_to_all x1, starting transfers between devices, per_device(): lax.all_to_all(payload.reshape(owners, per_owner, feature_width + BLK), '...  11 us
    ppermute x6, waiting for transfers between devices, butterfly_sum(): other = lax.ppermute(x, axis, perm=[(i, i ^ step) for i in range(size)])  9.56 us
  transfers between devices with their start and end apart: 9, of which 7 were waited for; matrix products, arithmetic and copies ran while one was open for 3% of the time, Pallas kernels for 0%

profile of v7, /device:TPU:6, one launch (start us, length us, event | category | flops | bytes accessed | tf_op | source)
XLA Modules:
  0.0 345.7 jit_solution(17649998557050454719)
XLA Ops:
  4.3 2.4 reshape.875
  8.9 6.3 %convolution_convert_fusion = bf16[1536,1152]{1,0:T(8,128)(2,1)} fusion(bf16[768,1152]{1,0:T(8,128)(2,1)} %concatenate.8, s32[768]{0:T(1024)S(1)} %multiply_add_fusion.1), kind=kOutput, calls=%fused_computation | convolution fusion | flops 2720858112 | bytes 5311488 | tf_op jit(solution)/shard_map/dot_general | solution.py:74
  15.2 11.0 %all-to-all-start = ((bf16[64,24,1152]{2,1,0:T(8,128)(2,1)}), bf16[64,24,1152]{2,1,0:T(8,128)(2,1)}, u32[]{:S(2)}, u32[]{:S(2)}) async-start(bf16[64,24,1152]{2,1,0:T(8,128)(2,1)} %bitcast.45), calls=%async_computation | async-start | bytes 7077888 | tf_op jit(solution)/shard_map/all_to_all | solution.py:75
  26.2 82.1 %all-to-all-done = bf16[64,24,1152]{2,1,0:T(8,128)(2,1)} async-done(((bf16[64,24,1152]{2,1,0:T(8,128)(2,1)}), bf16[64,24,1152]{2,1,0:T(8,128)(2,1)}, u32[]{:S(2)}, u32[]{:S(2)}) %all-to-all-start) | async-done | bytes 3538976 | tf_op jit(solution)/shard_map/all_to_all | solution.py:75
  109.5 2.9 fusion.3
  114.5 4.1 %collective-permute-start = (f32[8,1536]{1,0:T(8,128)S(1)}, f32[8,1536]{1,0:T(8,128)S(1)}, u32[]{:S(2)}, u32[]{:S(2)}) collective-permute-start(f32[8,1536]{1,0:T(8,128)S(1)} %get-tuple-element.40), channel_id=1, source_target_pairs={{0,1},{1,0},{2,3},{3,2},{4,5},{5,4},{6,7},{7,6},{8,9},{9,8},{10,11... | collective-permute-start | bytes 147464 | tf_op jit(solution)/shard_map/ppermute | solution.py:40
  120.7 6.1 %collective-permute-start.1 = (f32[8,1536]{1,0:T(8,128)S(1)}, f32[8,1536]{1,0:T(8,128)S(1)}, u32[]{:S(2)}, u32[]{:S(2)}) collective-permute-start(f32[8,1536]{1,0:T(8,128)S(1)} %add.99), channel_id=1, source_target_pairs={{0,2},{1,3},{2,0},{3,1},{4,6},{5,7},{6,4},{7,5},{8,10},{9,11},{10,... | collective-permute-start | bytes 147464 | tf_op jit(solution)/shard_map/ppermute | solution.py:40
  128.9 9.5 %collective-permute-start.2 = (f32[8,1536]{1,0:T(8,128)S(1)}, f32[8,1536]{1,0:T(8,128)S(1)}, u32[]{:S(2)}, u32[]{:S(2)}) collective-permute-start(f32[8,1536]{1,0:T(8,128)S(1)} %add.100), channel_id=1, source_target_pairs={{0,4},{1,5},{2,6},{3,7},{4,0},{5,1},{6,2},{7,3},{8,12},{9,13},{10,... | collective-permute-start | bytes 147464 | tf_op jit(solution)/shard_map/ppermute | solution.py:40
  138.4 3.1 slice_reduce_fusion.7
  142.2 2.8 convolution_convert_fusion.2
  145.1 5.9 %all-to-all-start.1 = ((bf16[64,24,1024]{2,1,0:T(8,128)(2,1)}), bf16[64,24,1024]{2,1,0:T(8,128)(2,1)}, u32[]{:S(2)}, u32[]{:S(2)}) async-start(bf16[64,24,1024]{2,1,0:T(8,128)(2,1)} %bitcast.46), calls=%async_computation.1 | async-start | bytes 6291456 | tf_op jit(solution)/shard_map/all_to_all | solution.py:110
  152.2 72.4 %all-to-all-done.1 = bf16[64,24,1024]{2,1,0:T(8,128)(2,1)} async-done(((bf16[64,24,1024]{2,1,0:T(8,128)(2,1)}), bf16[64,24,1024]{2,1,0:T(8,128)(2,1)}, u32[]{:S(2)}, u32[]{:S(2)}) %all-to-all-start.1) | async-done | bytes 3145760 | tf_op jit(solution)/shard_map/all_to_all | solution.py:110
  224.7 2.8 multiply_reduce_fusion
  227.5 2.8 convolution_convert_fusion.1
  230.3 5.6 %all-to-all-start.2 = ((bf16[64,24,1024]{2,1,0:T(8,128)(2,1)}), bf16[64,24,1024]{2,1,0:T(8,128)(2,1)}, u32[]{:S(2)}, u32[]{:S(2)}) async-start(bf16[64,24,1024]{2,1,0:T(8,128)(2,1)} %bitcast.44), calls=%async_computation.2 | async-start | bytes 6291456 | tf_op jit(solution)/shard_map/all_to_all | solution.py:124
  237.1 72.5 %all-to-all-done.2 = bf16[64,24,1024]{2,1,0:T(8,128)(2,1)} async-done(((bf16[64,24,1024]{2,1,0:T(8,128)(2,1)}), bf16[64,24,1024]{2,1,0:T(8,128)(2,1)}, u32[]{:S(2)}, u32[]{:S(2)}) %all-to-all-start.2) | async-done | bytes 3145760 | tf_op jit(solution)/shard_map/all_to_all | solution.py:124
  309.6 2.9 fusion.29
  313.6 3.4 collective-permute-start.3
  317.0 3.1 collective-permute-done.3
  320.1 4.8 %collective-permute-start.4 = (f32[9,1536]{1,0:T(8,128)S(1)}, f32[9,1536]{1,0:T(8,128)S(1)}, u32[]{:S(2)}, u32[]{:S(2)}) collective-permute-start(f32[9,1536]{1,0:T(8,128)S(1)} %fusion.28), channel_id=1, source_target_pairs={{0,2},{1,3},{2,0},{3,1},{4,6},{5,7},{6,4},{7,5},{8,10},{9,11},{10,... | collective-permute-start | bytes 165896 | tf_op jit(solution)/shard_map/ppermute | solution.py:40
  325.2 2.3 collective-permute-done.4
  327.6 8.4 %collective-permute-start.5 = (f32[9,1536]{1,0:T(8,128)S(1)}, f32[9,1536]{1,0:T(8,128)S(1)}, u32[]{:S(2)}, u32[]{:S(2)}) collective-permute-start(f32[9,1536]{1,0:T(8,128)S(1)} %add.105), channel_id=1, source_target_pairs={{0,4},{1,5},{2,6},{3,7},{4,0},{5,1},{6,2},{7,3},{8,12},{9,13},{10,... | collective-permute-start | bytes 165896 | tf_op jit(solution)/shard_map/ppermute | solution.py:40
  336.0 3.7 %convolution_convert_fusion.3 = bf16[256,1024]{1,0:T(8,128)(2,1)} fusion(bf16[256,1536]{1,0:T(8,128)(2,1)S(1)} %bitcast.52, bf16[1536,1024]{1,0:T(8,128)(2,1)} %bitcast.14), kind=kOutput, calls=%fused_computation.24 | convolution fusion | flops 805568512 | bytes 4456448 | tf_op jit(solution)/shard_map/dot_general | solution.py:131
  341.9 3.8 %fusion.6 = bf16[1024,256]{1,0:T(8,128)(2,1)} fusion(bf16[1536,1152]{1,0:T(8,128)(2,1)} %bitcast.5, bf16[256,1536]{1,0:T(8,128)(2,1)S(1)} %bitcast.50, s32[1536]{0:T(1024)S(1)} %add_select_fusion, s32[256]{0:T(256)S(1)} %and_select_fusion.1), kind=kOutput, calls=%fused_computation.23 | convolution fusion | flops 806354944 | bytes 4463616 | tf_op jit(solution)/shard_map/dot_general | solution.py:144
  (69 shorter events, 19.8 us)
Async XLA Ops:
  0.6 141.6 %copy-start = (bf16[256,1024]{1,0:T(8,128)(2,1)S(1)}, bf16[256,1024]{1,0:T(8,128)(2,1)}, u32[]{:S(2)}) copy-start(bf16[256,1024]{1,0:T(8,128)(2,1)} %param.13) | copy-start | bytes 1572868
  0.6 1.9 copy-start.5
  0.7 1.9 copy-start.1
  2.6 4.1 %copy-start.3 = (s32[192,4,8]{0,2,1:T(8,128)S(1)}, s32[192,4,8]{0,2,1:T(8,128)}, u32[]{:S(2)}) copy-start(s32[192,4,8]{0,2,1:T(8,128)} %param.15) | copy-start | bytes 73732
  15.2 94.3 %copy-start.7 = (bf16[1024,256]{1,0:T(8,128)(2,1)S(1)}, bf16[1024,256]{1,0:T(8,128)(2,1)}, u32[]{:S(2)}) copy-start(bf16[1024,256]{1,0:T(8,128)(2,1)} %param.11) | copy-start | bytes 1572868
  15.2 93.1 %all-to-all-start = ((bf16[64,24,1152]{2,1,0:T(8,128)(2,1)}), bf16[64,24,1152]{2,1,0:T(8,128)(2,1)}, u32[]{:S(2)}, u32[]{:S(2)}) async-start(bf16[64,24,1152]{2,1,0:T(8,128)(2,1)} %bitcast.45), calls=%async_computation | async-start | bytes 7077888 | tf_op jit(solution)/shard_map/all_to_all | solution.py:75
  109.5 3.2 copy-start.6
  114.5 6.2 %collective-permute-start = (f32[8,1536]{1,0:T(8,128)S(1)}, f32[8,1536]{1,0:T(8,128)S(1)}, u32[]{:S(2)}, u32[]{:S(2)}) collective-permute-start(f32[8,1536]{1,0:T(8,128)S(1)} %get-tuple-element.40), channel_id=1, source_target_pairs={{0,1},{1,0},{2,3},{3,2},{4,5},{5,4},{6,7},{7,6},{8,9},{9,8},{10,11... | collective-permute-start | bytes 147464 | tf_op jit(solution)/shard_map/ppermute | solution.py:40
  120.7 8.1 %collective-permute-start.1 = (f32[8,1536]{1,0:T(8,128)S(1)}, f32[8,1536]{1,0:T(8,128)S(1)}, u32[]{:S(2)}, u32[]{:S(2)}) collective-permute-start(f32[8,1536]{1,0:T(8,128)S(1)} %add.99), channel_id=1, source_target_pairs={{0,2},{1,3},{2,0},{3,1},{4,6},{5,7},{6,4},{7,5},{8,10},{9,11},{10,... | collective-permute-start | bytes 147464 | tf_op jit(solution)/shard_map/ppermute | solution.py:40
  128.9 12.6 %collective-permute-start.2 = (f32[8,1536]{1,0:T(8,128)S(1)}, f32[8,1536]{1,0:T(8,128)S(1)}, u32[]{:S(2)}, u32[]{:S(2)}) collective-permute-start(f32[8,1536]{1,0:T(8,128)S(1)} %add.100), channel_id=1, source_target_pairs={{0,4},{1,5},{2,6},{3,7},{4,0},{5,1},{6,2},{7,3},{8,12},{9,13},{10,... | collective-permute-start | bytes 147464 | tf_op jit(solution)/shard_map/ppermute | solution.py:40
  145.1 6.1 %copy-start.4 = (s32[192,4]{0,1:T(4,128)S(1)}, s32[192,4]{0,1:T(4,128)}, u32[]{:S(2)}) copy-start(s32[192,4]{0,1:T(4,128)} %param.14) | copy-start | bytes 9220
  145.1 79.6 %copy-start.2 = (f32[192,1024]{1,0:T(8,128)S(1)}, f32[192,1024]{1,0:T(8,128)}, u32[]{:S(2)}) copy-start(f32[192,1024]{1,0:T(8,128)} %param.9) | copy-start | bytes 2359300
  145.1 79.6 %all-to-all-start.1 = ((bf16[64,24,1024]{2,1,0:T(8,128)(2,1)}), bf16[64,24,1024]{2,1,0:T(8,128)(2,1)}, u32[]{:S(2)}, u32[]{:S(2)}) async-start(bf16[64,24,1024]{2,1,0:T(8,128)(2,1)} %bitcast.46), calls=%async_computation.1 | async-start | bytes 6291456 | tf_op jit(solution)/shard_map/all_to_all | solution.py:110
  230.3 79.3 %all-to-all-start.2 = ((bf16[64,24,1024]{2,1,0:T(8,128)(2,1)}), bf16[64,24,1024]{2,1,0:T(8,128)(2,1)}, u32[]{:S(2)}, u32[]{:S(2)}) async-start(bf16[64,24,1024]{2,1,0:T(8,128)(2,1)} %bitcast.44), calls=%async_computation.2 | async-start | bytes 6291456 | tf_op jit(solution)/shard_map/all_to_all | solution.py:124
  313.6 6.5 %collective-permute-start.3 = (f32[9,1536]{1,0:T(8,128)S(1)}, f32[9,1536]{1,0:T(8,128)S(1)}, u32[]{:S(2)}, u32[]{:S(2)}) collective-permute-start(f32[9,1536]{1,0:T(8,128)S(1)} %select_maximum_fusion), channel_id=1, source_target_pairs={{0,1},{1,0},{2,3},{3,2},{4,5},{5,4},{6,7},{7,6},{8,9},{9,8},{10,11... | collective-permute-start | bytes 165896 | tf_op jit(solution)/shard_map/ppermute | solution.py:40
  320.1 7.4 %collective-permute-start.4 = (f32[9,1536]{1,0:T(8,128)S(1)}, f32[9,1536]{1,0:T(8,128)S(1)}, u32[]{:S(2)}, u32[]{:S(2)}) collective-permute-start(f32[9,1536]{1,0:T(8,128)S(1)} %fusion.28), channel_id=1, source_target_pairs={{0,2},{1,3},{2,0},{3,1},{4,6},{5,7},{6,4},{7,5},{8,10},{9,11},{10,... | collective-permute-start | bytes 165896 | tf_op jit(solution)/shard_map/ppermute | solution.py:40
  327.6 12.2 %collective-permute-start.5 = (f32[9,1536]{1,0:T(8,128)S(1)}, f32[9,1536]{1,0:T(8,128)S(1)}, u32[]{:S(2)}, u32[]{:S(2)}) collective-permute-start(f32[9,1536]{1,0:T(8,128)S(1)} %add.105), channel_id=1, source_target_pairs={{0,4},{1,5},{2,6},{3,7},{4,0},{5,1},{6,2},{7,3},{8,12},{9,13},{10,... | collective-permute-start | bytes 165896 | tf_op jit(solution)/shard_map/ppermute | solution.py:40

commit v8 on v3

--- a/solution.py
+++ b/solution.py
@@ -69,7 +69,6 @@
     ).astype(jnp.int32)
     out_offs = out_offs_t.reshape(PER, owners, per_owner).transpose(1, 0, 2)
 
-    got_offs = lax.all_to_all(out_offs, "lat", split_axis=0, concat_axis=0, tiled=True)
     got_rows = lax.all_to_all(
         outgoing.reshape(owners, per_owner, feature_width),
         "lat",
@@ -78,6 +77,8 @@
         tiled=True,
     )
     got_rows = got_rows.reshape(slot_count, feature_width)
+    after_rows = (got_rows[0, 0] * 0).astype(jnp.int32)
+    got_offs = lax.all_to_all(out_offs + after_rows, "lat", split_axis=0, concat_axis=0, tiled=True)
     offs_t = got_offs.transpose(1, 0, 2).reshape(PER, slot_count) - 1
 
     slot_block = (slots // capacity) % owned_blocks

time: 341 us -> 343 us (level)
    all_to_all x1, starting transfers between devices: 10.6 us -> 5.41 us  [per_device(): lax.all_to_all(out_offs + after_rows, 'lat', split_axis=0, concat_axis=0,...]
where the time goes in v8:
time: 343 us; the launch traced here: 342 us
  waiting for transfers between devices  164 us (48%)
  blocking collectives  79.7 us (23%)
  starting transfers between devices  59.4 us (17%)
  matrix products  21.9 us (6%)
  other arithmetic  9.41 us (3%)
  local copies, waits for them, and re-layouts  6.66 us (2%)
    all_to_all x1, blocking collectives, per_device(): lax.all_to_all(decoded.reshape(owners, per_owner, feature_width), 'lat',...  79.7 us
    all_to_all x1, waiting for transfers between devices, per_device(): lax.all_to_all(outgoing.reshape(owners, per_owner, feature_width), 'lat',...  73.5 us
    all_to_all x1, waiting for transfers between devices, per_device(): lax.all_to_all(out_error.reshape(owners, per_owner, feature_width), 'lat'...  72.4 us
    ppermute x6, starting transfers between devices, butterfly_sum(): other = lax.ppermute(x, axis, perm=[(i, i ^ step) for i in range(size)])  37.2 us
    ppermute x6, waiting for transfers between devices, butterfly_sum(): other = lax.ppermute(x, axis, perm=[(i, i ^ step) for i in range(size)])  13.1 us
    all_to_all x1, starting transfers between devices, per_device(): lax.all_to_all(outgoing.reshape(owners, per_owner, feature_width), 'lat',...  10.9 us
  transfers between devices with their start and end apart: 9, of which 9 were waited for; matrix products, arithmetic and copies ran while one was open for 2% of the time, Pallas kernels for 0%

profile of v8, /device:TPU:6, one launch (start us, length us, event | category | flops | bytes accessed | tf_op | source)
XLA Modules:
  0.0 342.5 jit_solution(15944963788989495935)
XLA Ops:
  3.8 2.8 convolution_convert_fusion.2
  6.6 10.9 %all-to-all-start = ((bf16[64,24,1024]{2,1,0:T(8,128)(2,1)}), bf16[64,24,1024]{2,1,0:T(8,128)(2,1)}, u32[]{:S(2)}, u32[]{:S(2)}) async-start(bf16[64,24,1024]{2,1,0:T(8,128)(2,1)} %bitcast.51), calls=%async_computation | async-start | bytes 6291456 | tf_op jit(solution)/shard_map/all_to_all | solution.py:72
  17.8 73.5 %all-to-all-done = bf16[64,24,1024]{2,1,0:T(8,128)(2,1)} async-done(((bf16[64,24,1024]{2,1,0:T(8,128)(2,1)}), bf16[64,24,1024]{2,1,0:T(8,128)(2,1)}, u32[]{:S(2)}, u32[]{:S(2)}) %all-to-all-start) | async-done | bytes 3145760 | tf_op jit(solution)/shard_map/all_to_all | solution.py:72
  95.3 5.4 %all-to-all-start.1 = ((s32[64,1,192]{2,1,0:T(1,128)}), s32[64,1,192]{2,1,0:T(1,128)S(1)}, u32[]{:S(2)}, u32[]{:S(2)}) async-start(s32[64,1,192]{2,1,0:T(1,128)} %reshape.1017), calls=%async_computation.1 | async-start | bytes 131072 | tf_op jit(solution)/shard_map/all_to_all | solution.py:81
  100.8 2.9 fusion.22
  104.1 4.7 %all-to-all-done.1 = s32[64,1,192]{2,1,0:T(1,128)S(1)} async-done(((s32[64,1,192]{2,1,0:T(1,128)}), s32[64,1,192]{2,1,0:T(1,128)S(1)}, u32[]{:S(2)}, u32[]{:S(2)}) %all-to-all-start.1) | async-done | bytes 49184 | tf_op jit(solution)/shard_map/all_to_all | solution.py:81
  112.0 4.1 %collective-permute-start = (f32[8,1536]{1,0:T(8,128)S(1)}, f32[8,1536]{1,0:T(8,128)S(1)}, u32[]{:S(2)}, u32[]{:S(2)}) collective-permute-start(f32[8,1536]{1,0:T(8,128)S(1)} %get-tuple-element.40), channel_id=1, source_target_pairs={{0,1},{1,0},{2,3},{3,2},{4,5},{5,4},{6,7},{7,6},{8,9},{9,8},{10,11... | collective-permute-start | bytes 147464 | tf_op jit(solution)/shard_map/ppermute | solution.py:40
  116.2 2.1 collective-permute-done
  118.2 6.1 %collective-permute-start.1 = (f32[8,1536]{1,0:T(8,128)S(1)}, f32[8,1536]{1,0:T(8,128)S(1)}, u32[]{:S(2)}, u32[]{:S(2)}) collective-permute-start(f32[8,1536]{1,0:T(8,128)S(1)} %add.120), channel_id=1, source_target_pairs={{0,2},{1,3},{2,0},{3,1},{4,6},{5,7},{6,4},{7,5},{8,10},{9,11},{10,... | collective-permute-start | bytes 147464 | tf_op jit(solution)/shard_map/ppermute | solution.py:40
  124.4 2.3 collective-permute-done.1
  126.7 9.2 %collective-permute-start.2 = (f32[8,1536]{1,0:T(8,128)S(1)}, f32[8,1536]{1,0:T(8,128)S(1)}, u32[]{:S(2)}, u32[]{:S(2)}) collective-permute-start(f32[8,1536]{1,0:T(8,128)S(1)} %add.121), channel_id=1, source_target_pairs={{0,4},{1,5},{2,6},{3,7},{4,0},{5,1},{6,2},{7,3},{8,12},{9,13},{10,... | collective-permute-start | bytes 147464 | tf_op jit(solution)/shard_map/ppermute | solution.py:40
  139.6 79.7 %all_to_all.20 = bf16[64,24,1024]{2,1,0:T(8,128)(2,1)S(1)} all-to-all(bf16[64,24,1024]{2,1,0:T(8,128)(2,1)S(1)} %bitcast.54), channel_id=1, replica_groups=mesh['lat'=64,'row'=8] {'lat'}, dimensions={0} | all-to-all | bytes 6291456 | tf_op jit(solution)/shard_map/all_to_all | solution.py:109
  220.2 2.8 convolution_convert_fusion
  223.0 5.8 %all-to-all-start.3 = ((bf16[64,24,1024]{2,1,0:T(8,128)(2,1)}), bf16[64,24,1024]{2,1,0:T(8,128)(2,1)}, u32[]{:S(2)}, u32[]{:S(2)}) async-start(bf16[64,24,1024]{2,1,0:T(8,128)(2,1)} %bitcast.52), calls=%async_computation.3 | async-start | bytes 6291456 | tf_op jit(solution)/shard_map/all_to_all | solution.py:123
  230.1 72.4 %all-to-all-done.3 = bf16[64,24,1024]{2,1,0:T(8,128)(2,1)} async-done(((bf16[64,24,1024]{2,1,0:T(8,128)(2,1)}), bf16[64,24,1024]{2,1,0:T(8,128)(2,1)}, u32[]{:S(2)}, u32[]{:S(2)}) %all-to-all-start.3) | async-done | bytes 3145760 | tf_op jit(solution)/shard_map/all_to_all | solution.py:123
  302.5 2.9 fusion.23
  306.6 3.5 %collective-permute-start.3 = (f32[9,1536]{1,0:T(8,128)S(1)}, f32[9,1536]{1,0:T(8,128)S(1)}, u32[]{:S(2)}, u32[]{:S(2)}) collective-permute-start(f32[9,1536]{1,0:T(8,128)S(1)} %select_maximum_fusion), channel_id=1, source_target_pairs={{0,1},{1,0},{2,3},{3,2},{4,5},{5,4},{6,7},{7,6},{8,9},{9,8},{10,11... | collective-permute-start | bytes 165896 | tf_op jit(solution)/shard_map/ppermute | solution.py:40
  310.0 3.1 collective-permute-done.3
  313.1 4.9 %collective-permute-start.4 = (f32[9,1536]{1,0:T(8,128)S(1)}, f32[9,1536]{1,0:T(8,128)S(1)}, u32[]{:S(2)}, u32[]{:S(2)}) collective-permute-start(f32[9,1536]{1,0:T(8,128)S(1)} %fusion.21), channel_id=1, source_target_pairs={{0,2},{1,3},{2,0},{3,1},{4,6},{5,7},{6,4},{7,5},{8,10},{9,11},{10,... | collective-permute-start | bytes 165896 | tf_op jit(solution)/shard_map/ppermute | solution.py:40
  317.9 2.6 collective-permute-done.4
  320.5 9.4 %collective-permute-start.5 = (f32[9,1536]{1,0:T(8,128)S(1)}, f32[9,1536]{1,0:T(8,128)S(1)}, u32[]{:S(2)}, u32[]{:S(2)}) collective-permute-start(f32[9,1536]{1,0:T(8,128)S(1)} %add.126), channel_id=1, source_target_pairs={{0,4},{1,5},{2,6},{3,7},{4,0},{5,1},{6,2},{7,3},{8,12},{9,13},{10,... | collective-permute-start | bytes 165896 | tf_op jit(solution)/shard_map/ppermute | solution.py:40
  330.0 2.6 collective-permute-done.5
  335.0 3.7 %convolution_convert_fusion.3 = bf16[256,1024]{1,0:T(8,128)(2,1)} fusion(bf16[256,1536]{1,0:T(8,128)(2,1)S(1)} %bitcast.60, bf16[1536,1024]{1,0:T(8,128)(2,1)} %bitcast.16), kind=kOutput, calls=%fused_computation.22 | convolution fusion | flops 805568512 | bytes 4456448 | tf_op jit(solution)/shard_map/dot_general | solution.py:130
  338.7 3.7 %convolution_convert_fusion.4 = bf16[1024,256]{1,0:T(8,128)(2,1)} fusion(bf16[1536,1024]{1,0:T(8,128)(2,1)} %bitcast.4, bf16[256,1536]{1,0:T(8,128)(2,1)S(1)} %bitcast.59), kind=kOutput, calls=%fused_computation.23 | convolution fusion | flops 805568512 | bytes 4456448 | tf_op jit(solution)/shard_map/dot_general | solution.py:143
  (81 shorter events, 19.5 us)
Async XLA Ops:
  0.6 137.8 %copy-start = (bf16[256,1024]{1,0:T(8,128)(2,1)S(1)}, bf16[256,1024]{1,0:T(8,128)(2,1)}, u32[]{:S(2)}) copy-start(bf16[256,1024]{1,0:T(8,128)(2,1)} %param.13) | copy-start | bytes 1572868
  0.6 2.1 copy-start.4
  0.7 3.2 copy-start.5
  0.7 3.2 copy-start.1
  6.6 11.0 %copy-start.3 = (s32[192,4,8]{0,2,1:T(8,128)S(1)}, s32[192,4,8]{0,2,1:T(8,128)}, u32[]{:S(2)}) copy-start(s32[192,4,8]{0,2,1:T(8,128)} %param.15) | copy-start | bytes 73732
  6.6 94.1 %copy-start.7 = (bf16[1024,256]{1,0:T(8,128)(2,1)S(1)}, bf16[1024,256]{1,0:T(8,128)(2,1)}, u32[]{:S(2)}) copy-start(bf16[1024,256]{1,0:T(8,128)(2,1)} %param.11) | copy-start | bytes 1572868
  6.6 84.7 %all-to-all-start = ((bf16[64,24,1024]{2,1,0:T(8,128)(2,1)}), bf16[64,24,1024]{2,1,0:T(8,128)(2,1)}, u32[]{:S(2)}, u32[]{:S(2)}) async-start(bf16[64,24,1024]{2,1,0:T(8,128)(2,1)} %bitcast.51), calls=%async_computation | async-start | bytes 6291456 | tf_op jit(solution)/shard_map/all_to_all | solution.py:72
  95.3 13.4 %all-to-all-start.1 = ((s32[64,1,192]{2,1,0:T(1,128)}), s32[64,1,192]{2,1,0:T(1,128)S(1)}, u32[]{:S(2)}, u32[]{:S(2)}) async-start(s32[64,1,192]{2,1,0:T(1,128)} %reshape.1017), calls=%async_computation.1 | async-start | bytes 131072 | tf_op jit(solution)/shard_map/all_to_all | solution.py:81
  100.8 2.9 copy-start.6
  112.0 6.2 %collective-permute-start = (f32[8,1536]{1,0:T(8,128)S(1)}, f32[8,1536]{1,0:T(8,128)S(1)}, u32[]{:S(2)}, u32[]{:S(2)}) collective-permute-start(f32[8,1536]{1,0:T(8,128)S(1)} %get-tuple-element.40), channel_id=1, source_target_pairs={{0,1},{1,0},{2,3},{3,2},{4,5},{5,4},{6,7},{7,6},{8,9},{9,8},{10,11... | collective-permute-start | bytes 147464 | tf_op jit(solution)/shard_map/ppermute | solution.py:40
  118.2 8.4 %collective-permute-start.1 = (f32[8,1536]{1,0:T(8,128)S(1)}, f32[8,1536]{1,0:T(8,128)S(1)}, u32[]{:S(2)}, u32[]{:S(2)}) collective-permute-start(f32[8,1536]{1,0:T(8,128)S(1)} %add.120), channel_id=1, source_target_pairs={{0,2},{1,3},{2,0},{3,1},{4,6},{5,7},{6,4},{7,5},{8,10},{9,11},{10,... | collective-permute-start | bytes 147464 | tf_op jit(solution)/shard_map/ppermute | solution.py:40
  126.7 11.1 %collective-permute-start.2 = (f32[8,1536]{1,0:T(8,128)S(1)}, f32[8,1536]{1,0:T(8,128)S(1)}, u32[]{:S(2)}, u32[]{:S(2)}) collective-permute-start(f32[8,1536]{1,0:T(8,128)S(1)} %add.121), channel_id=1, source_target_pairs={{0,4},{1,5},{2,6},{3,7},{4,0},{5,1},{6,2},{7,3},{8,12},{9,13},{10,... | collective-permute-start | bytes 147464 | tf_op jit(solution)/shard_map/ppermute | solution.py:40
  139.6 79.7 %copy-start.2 = (f32[192,1024]{1,0:T(8,128)S(1)}, f32[192,1024]{1,0:T(8,128)}, u32[]{:S(2)}) copy-start(f32[192,1024]{1,0:T(8,128)} %param.9) | copy-start | bytes 2359300
  223.0 79.5 %all-to-all-start.3 = ((bf16[64,24,1024]{2,1,0:T(8,128)(2,1)}), bf16[64,24,1024]{2,1,0:T(8,128)(2,1)}, u32[]{:S(2)}, u32[]{:S(2)}) async-start(bf16[64,24,1024]{2,1,0:T(8,128)(2,1)} %bitcast.52), calls=%async_computation.3 | async-start | bytes 6291456 | tf_op jit(solution)/shard_map/all_to_all | solution.py:123
  306.6 6.5 %collective-permute-start.3 = (f32[9,1536]{1,0:T(8,128)S(1)}, f32[9,1536]{1,0:T(8,128)S(1)}, u32[]{:S(2)}, u32[]{:S(2)}) collective-permute-start(f32[9,1536]{1,0:T(8,128)S(1)} %select_maximum_fusion), channel_id=1, source_target_pairs={{0,1},{1,0},{2,3},{3,2},{4,5},{5,4},{6,7},{7,6},{8,9},{9,8},{10,11... | collective-permute-start | bytes 165896 | tf_op jit(solution)/shard_map/ppermute | solution.py:40
  313.1 7.4 %collective-permute-start.4 = (f32[9,1536]{1,0:T(8,128)S(1)}, f32[9,1536]{1,0:T(8,128)S(1)}, u32[]{:S(2)}, u32[]{:S(2)}) collective-permute-start(f32[9,1536]{1,0:T(8,128)S(1)} %fusion.21), channel_id=1, source_target_pairs={{0,2},{1,3},{2,0},{3,1},{4,6},{5,7},{6,4},{7,5},{8,10},{9,11},{10,... | collective-permute-start | bytes 165896 | tf_op jit(solution)/shard_map/ppermute | solution.py:40
  320.5 12.1 %collective-permute-start.5 = (f32[9,1536]{1,0:T(8,128)S(1)}, f32[9,1536]{1,0:T(8,128)S(1)}, u32[]{:S(2)}, u32[]{:S(2)}) collective-permute-start(f32[9,1536]{1,0:T(8,128)S(1)} %add.126), channel_id=1, source_target_pairs={{0,4},{1,5},{2,6},{3,7},{4,0},{5,1},{6,2},{7,3},{8,12},{9,13},{10,... | collective-permute-start | bytes 165896 | tf_op jit(solution)/shard_map/ppermute | solution.py:40

commit v9 on v3

--- a/solution.py
+++ b/solution.py
@@ -35,11 +35,11 @@
 
 def butterfly_sum(x, axis):
     size = lax.axis_size(axis)
-    step = 1
-    while step < size:
+    step = size // 2
+    while step >= 1:
         other = lax.ppermute(x, axis, perm=[(i, i ^ step) for i in range(size)])
         x = x + other
-        step *= 2
+        step //= 2
     return x
 
 

time: 341 us -> 341 us (level)
  no operation moved by 1% of the time
where the time goes in v9:
time: 341 us; the launch traced here: 340 us
  waiting for transfers between devices  164 us (48%)
  blocking collectives  79.9 us (23%)
  starting transfers between devices  58.8 us (17%)
  matrix products  21.9 us (6%)
  other arithmetic  9.42 us (3%)
  local copies, waits for them, and re-layouts  5.42 us (2%)
    all_to_all x1, blocking collectives, per_device(): lax.all_to_all(decoded.reshape(owners, per_owner, feature_width), 'lat',...  79.9 us
    all_to_all x1, waiting for transfers between devices, per_device(): lax.all_to_all(out_error.reshape(owners, per_owner, feature_width), 'lat'...  72.4 us
    all_to_all x1, waiting for transfers between devices, per_device(): lax.all_to_all(outgoing.reshape(owners, per_owner, feature_width), 'lat',...  72 us
    ppermute x6, starting transfers between devices, butterfly_sum(): other = lax.ppermute(x, axis, perm=[(i, i ^ step) for i in range(size)])  34.8 us
    ppermute x6, waiting for transfers between devices, butterfly_sum(): other = lax.ppermute(x, axis, perm=[(i, i ^ step) for i in range(size)])  15.4 us
    all_to_all x1, starting transfers between devices, per_device(): lax.all_to_all(out_offs, 'lat', split_axis=0, concat_axis=0, tiled=True)  10.6 us
    all_to_all x1, starting transfers between devices, per_device(): lax.all_to_all(outgoing.reshape(owners, per_owner, feature_width), 'lat',...  7.57 us
  transfers between devices with their start and end apart: 9, of which 9 were waited for; matrix products, arithmetic and copies ran while one was open for 2% of the time, Pallas kernels for 0%

profile of v9, /device:TPU:6, one launch (start us, length us, event | category | flops | bytes accessed | tf_op | source)
XLA Modules:
  0.0 340.2 jit_solution(898332312151608398)
XLA Ops:
  4.9 10.6 %all-to-all-start.1 = ((s32[64,1,192]{2,1,0:T(1,128)}), s32[64,1,192]{2,1,0:T(1,128)S(1)}, u32[]{:S(2)}, u32[]{:S(2)}) async-start(s32[64,1,192]{2,1,0:T(1,128)} %reshape.1013), calls=%async_computation.1 | async-start | bytes 131072 | tf_op jit(solution)/shard_map/all_to_all | solution.py:72
  16.8 2.8 convolution_convert_fusion.2
  19.5 4.0 %all-to-all-done.1 = s32[64,1,192]{2,1,0:T(1,128)S(1)} async-done(((s32[64,1,192]{2,1,0:T(1,128)}), s32[64,1,192]{2,1,0:T(1,128)S(1)}, u32[]{:S(2)}, u32[]{:S(2)}) %all-to-all-start.1) | async-done | bytes 49184 | tf_op jit(solution)/shard_map/all_to_all | solution.py:72
  23.5 7.6 %all-to-all-start = ((bf16[64,24,1024]{2,1,0:T(8,128)(2,1)}), bf16[64,24,1024]{2,1,0:T(8,128)(2,1)}, u32[]{:S(2)}, u32[]{:S(2)}) async-start(bf16[64,24,1024]{2,1,0:T(8,128)(2,1)} %bitcast.49), calls=%async_computation | async-start | bytes 6291456 | tf_op jit(solution)/shard_map/all_to_all | solution.py:73
  32.9 72.0 %all-to-all-done = bf16[64,24,1024]{2,1,0:T(8,128)(2,1)} async-done(((bf16[64,24,1024]{2,1,0:T(8,128)(2,1)}), bf16[64,24,1024]{2,1,0:T(8,128)(2,1)}, u32[]{:S(2)}, u32[]{:S(2)}) %all-to-all-start) | async-done | bytes 3145760 | tf_op jit(solution)/shard_map/all_to_all | solution.py:73
  104.9 2.9 fusion.21
  109.7 10.9 %collective-permute-start = (f32[8,1536]{1,0:T(8,128)S(1)}, f32[8,1536]{1,0:T(8,128)S(1)}, u32[]{:S(2)}, u32[]{:S(2)}) collective-permute-start(f32[8,1536]{1,0:T(8,128)S(1)} %get-tuple-element.40), channel_id=1, source_target_pairs={{0,4},{1,5},{2,6},{3,7},{4,0},{5,1},{6,2},{7,3},{8,12},{9,13},{10,... | collective-permute-start | bytes 147464 | tf_op jit(solution)/shard_map/ppermute | solution.py:40
  120.6 2.1 collective-permute-done
  122.8 4.8 %collective-permute-start.1 = (f32[8,1536]{1,0:T(8,128)S(1)}, f32[8,1536]{1,0:T(8,128)S(1)}, u32[]{:S(2)}, u32[]{:S(2)}) collective-permute-start(f32[8,1536]{1,0:T(8,128)S(1)} %add.104), channel_id=1, source_target_pairs={{0,2},{1,3},{2,0},{3,1},{4,6},{5,7},{6,4},{7,5},{8,10},{9,11},{10,... | collective-permute-start | bytes 147464 | tf_op jit(solution)/shard_map/ppermute | solution.py:40
  127.6 2.0 collective-permute-done.1
  129.7 3.6 %collective-permute-start.2 = (f32[8,1536]{1,0:T(8,128)S(1)}, f32[8,1536]{1,0:T(8,128)S(1)}, u32[]{:S(2)}, u32[]{:S(2)}) collective-permute-start(f32[8,1536]{1,0:T(8,128)S(1)} %add.105), channel_id=1, source_target_pairs={{0,1},{1,0},{2,3},{3,2},{4,5},{5,4},{6,7},{7,6},{8,9},{9,8},{10,11... | collective-permute-start | bytes 147464 | tf_op jit(solution)/shard_map/ppermute | solution.py:40
  137.4 79.9 %all_to_all.20 = bf16[64,24,1024]{2,1,0:T(8,128)(2,1)S(1)} all-to-all(bf16[64,24,1024]{2,1,0:T(8,128)(2,1)S(1)} %bitcast.52), channel_id=1, replica_groups=mesh['lat'=64,'row'=8] {'lat'}, dimensions={0} | all-to-all | bytes 6291456 | tf_op jit(solution)/shard_map/all_to_all | solution.py:108
  218.3 2.8 convolution_convert_fusion
  221.1 5.8 %all-to-all-start.3 = ((bf16[64,24,1024]{2,1,0:T(8,128)(2,1)}), bf16[64,24,1024]{2,1,0:T(8,128)(2,1)}, u32[]{:S(2)}, u32[]{:S(2)}) async-start(bf16[64,24,1024]{2,1,0:T(8,128)(2,1)} %bitcast.50), calls=%async_computation.3 | async-start | bytes 6291456 | tf_op jit(solution)/shard_map/all_to_all | solution.py:122
  228.2 72.4 %all-to-all-done.3 = bf16[64,24,1024]{2,1,0:T(8,128)(2,1)} async-done(((bf16[64,24,1024]{2,1,0:T(8,128)(2,1)}), bf16[64,24,1024]{2,1,0:T(8,128)(2,1)}, u32[]{:S(2)}, u32[]{:S(2)}) %all-to-all-start.3) | async-done | bytes 3145760 | tf_op jit(solution)/shard_map/all_to_all | solution.py:122
  300.6 2.9 fusion.22
  304.6 8.1 %collective-permute-start.3 = (f32[9,1536]{1,0:T(8,128)S(1)}, f32[9,1536]{1,0:T(8,128)S(1)}, u32[]{:S(2)}, u32[]{:S(2)}) collective-permute-start(f32[9,1536]{1,0:T(8,128)S(1)} %select_maximum_fusion), channel_id=1, source_target_pairs={{0,4},{1,5},{2,6},{3,7},{4,0},{5,1},{6,2},{7,3},{8,12},{9,13},{10,... | collective-permute-start | bytes 165896 | tf_op jit(solution)/shard_map/ppermute | solution.py:40
  312.7 2.7 collective-permute-done.3
  315.4 4.9 %collective-permute-start.4 = (f32[9,1536]{1,0:T(8,128)S(1)}, f32[9,1536]{1,0:T(8,128)S(1)}, u32[]{:S(2)}, u32[]{:S(2)}) collective-permute-start(f32[9,1536]{1,0:T(8,128)S(1)} %fusion.20), channel_id=1, source_target_pairs={{0,2},{1,3},{2,0},{3,1},{4,6},{5,7},{6,4},{7,5},{8,10},{9,11},{10,... | collective-permute-start | bytes 165896 | tf_op jit(solution)/shard_map/ppermute | solution.py:40
  320.3 3.6 %collective-permute-done.4 = f32[9,1536]{1,0:T(8,128)S(1)} collective-permute-done((f32[9,1536]{1,0:T(8,128)S(1)}, f32[9,1536]{1,0:T(8,128)S(1)}, u32[]{:S(2)}, u32[]{:S(2)}) %collective-permute-start.4) | collective-permute-done | bytes 55328 | tf_op jit(solution)/shard_map/ppermute | solution.py:40
  323.9 2.6 collective-permute-start.5
  326.5 3.9 %collective-permute-done.5 = f32[9,1536]{1,0:T(8,128)S(1)} collective-permute-done((f32[9,1536]{1,0:T(8,128)S(1)}, f32[9,1536]{1,0:T(8,128)S(1)}, u32[]{:S(2)}, u32[]{:S(2)}) %collective-permute-start.5) | collective-permute-done | bytes 55328 | tf_op jit(solution)/shard_map/ppermute | solution.py:40
  332.8 3.7 %convolution_convert_fusion.3 = bf16[256,1024]{1,0:T(8,128)(2,1)} fusion(bf16[256,1536]{1,0:T(8,128)(2,1)S(1)} %bitcast.58, bf16[1536,1024]{1,0:T(8,128)(2,1)} %bitcast.15), kind=kOutput, calls=%fused_computation.21 | convolution fusion | flops 805568512 | bytes 4456448 | tf_op jit(solution)/shard_map/dot_general | solution.py:129
  336.5 3.7 %convolution_convert_fusion.4 = bf16[1024,256]{1,0:T(8,128)(2,1)} fusion(bf16[1536,1024]{1,0:T(8,128)(2,1)} %bitcast.4, bf16[256,1536]{1,0:T(8,128)(2,1)S(1)} %bitcast.57), kind=kOutput, calls=%fused_computation.22 | convolution fusion | flops 805568512 | bytes 4456448 | tf_op jit(solution)/shard_map/dot_general | solution.py:142
  (78 shorter events, 18.8 us)
Async XLA Ops:
  0.6 135.7 %copy-start = (bf16[256,1024]{1,0:T(8,128)(2,1)S(1)}, bf16[256,1024]{1,0:T(8,128)(2,1)}, u32[]{:S(2)}) copy-start(bf16[256,1024]{1,0:T(8,128)(2,1)} %param.13) | copy-start | bytes 1572868
  0.6 1.9 copy-start.2
  1.5 14.2 %copy-start.3 = (s32[192,4]{0,1:T(4,128)S(1)}, s32[192,4]{0,1:T(4,128)}, u32[]{:S(2)}) copy-start(s32[192,4]{0,1:T(4,128)} %param.14) | copy-start | bytes 9220
  1.9 14.9 %copy-start.1 = (f32[192,1024]{1,0:T(8,128)S(1)}, f32[192,1024]{1,0:T(8,128)}, u32[]{:S(2)}) copy-start(f32[192,1024]{1,0:T(8,128)} %param.9) | copy-start | bytes 2359300
  1.9 14.9 %copy-start.4 = (f32[1024]{0:T(1024)S(1)}, f32[1024]{0:T(1024)}, u32[]{:S(2)}) copy-start(f32[1024]{0:T(1024)} %param.10) | copy-start | bytes 12292
  4.9 18.6 %all-to-all-start.1 = ((s32[64,1,192]{2,1,0:T(1,128)}), s32[64,1,192]{2,1,0:T(1,128)S(1)}, u32[]{:S(2)}, u32[]{:S(2)}) async-start(s32[64,1,192]{2,1,0:T(1,128)} %reshape.1013), calls=%async_computation.1 | async-start | bytes 131072 | tf_op jit(solution)/shard_map/all_to_all | solution.py:72
  23.5 81.3 %copy-start.6 = (bf16[1024,256]{1,0:T(8,128)(2,1)S(1)}, bf16[1024,256]{1,0:T(8,128)(2,1)}, u32[]{:S(2)}) copy-start(bf16[1024,256]{1,0:T(8,128)(2,1)} %param.11) | copy-start | bytes 1572868
  23.5 81.3 %all-to-all-start = ((bf16[64,24,1024]{2,1,0:T(8,128)(2,1)}), bf16[64,24,1024]{2,1,0:T(8,128)(2,1)}, u32[]{:S(2)}, u32[]{:S(2)}) async-start(bf16[64,24,1024]{2,1,0:T(8,128)(2,1)} %bitcast.49), calls=%async_computation | async-start | bytes 6291456 | tf_op jit(solution)/shard_map/all_to_all | solution.py:73
  104.9 2.9 copy-start.5
  109.7 13.0 %collective-permute-start = (f32[8,1536]{1,0:T(8,128)S(1)}, f32[8,1536]{1,0:T(8,128)S(1)}, u32[]{:S(2)}, u32[]{:S(2)}) collective-permute-start(f32[8,1536]{1,0:T(8,128)S(1)} %get-tuple-element.40), channel_id=1, source_target_pairs={{0,4},{1,5},{2,6},{3,7},{4,0},{5,1},{6,2},{7,3},{8,12},{9,13},{10,... | collective-permute-start | bytes 147464 | tf_op jit(solution)/shard_map/ppermute | solution.py:40
  122.8 6.9 %collective-permute-start.1 = (f32[8,1536]{1,0:T(8,128)S(1)}, f32[8,1536]{1,0:T(8,128)S(1)}, u32[]{:S(2)}, u32[]{:S(2)}) collective-permute-start(f32[8,1536]{1,0:T(8,128)S(1)} %add.104), channel_id=1, source_target_pairs={{0,2},{1,3},{2,0},{3,1},{4,6},{5,7},{6,4},{7,5},{8,10},{9,11},{10,... | collective-permute-start | bytes 147464 | tf_op jit(solution)/shard_map/ppermute | solution.py:40
  129.7 6.0 %collective-permute-start.2 = (f32[8,1536]{1,0:T(8,128)S(1)}, f32[8,1536]{1,0:T(8,128)S(1)}, u32[]{:S(2)}, u32[]{:S(2)}) collective-permute-start(f32[8,1536]{1,0:T(8,128)S(1)} %add.105), channel_id=1, source_target_pairs={{0,1},{1,0},{2,3},{3,2},{4,5},{5,4},{6,7},{7,6},{8,9},{9,8},{10,11... | collective-permute-start | bytes 147464 | tf_op jit(solution)/shard_map/ppermute | solution.py:40
  221.1 79.5 %all-to-all-start.3 = ((bf16[64,24,1024]{2,1,0:T(8,128)(2,1)}), bf16[64,24,1024]{2,1,0:T(8,128)(2,1)}, u32[]{:S(2)}, u32[]{:S(2)}) async-start(bf16[64,24,1024]{2,1,0:T(8,128)(2,1)} %bitcast.50), calls=%async_computation.3 | async-start | bytes 6291456 | tf_op jit(solution)/shard_map/all_to_all | solution.py:122
  304.6 10.8 %collective-permute-start.3 = (f32[9,1536]{1,0:T(8,128)S(1)}, f32[9,1536]{1,0:T(8,128)S(1)}, u32[]{:S(2)}, u32[]{:S(2)}) collective-permute-start(f32[9,1536]{1,0:T(8,128)S(1)} %select_maximum_fusion), channel_id=1, source_target_pairs={{0,4},{1,5},{2,6},{3,7},{4,0},{5,1},{6,2},{7,3},{8,12},{9,13},{10,... | collective-permute-start | bytes 165896 | tf_op jit(solution)/shard_map/ppermute | solution.py:40
  315.4 8.5 %collective-permute-start.4 = (f32[9,1536]{1,0:T(8,128)S(1)}, f32[9,1536]{1,0:T(8,128)S(1)}, u32[]{:S(2)}, u32[]{:S(2)}) collective-permute-start(f32[9,1536]{1,0:T(8,128)S(1)} %fusion.20), channel_id=1, source_target_pairs={{0,2},{1,3},{2,0},{3,1},{4,6},{5,7},{6,4},{7,5},{8,10},{9,11},{10,... | collective-permute-start | bytes 165896 | tf_op jit(solution)/shard_map/ppermute | solution.py:40
  323.9 6.5 %collective-permute-start.5 = (f32[9,1536]{1,0:T(8,128)S(1)}, f32[9,1536]{1,0:T(8,128)S(1)}, u32[]{:S(2)}, u32[]{:S(2)}) collective-permute-start(f32[9,1536]{1,0:T(8,128)S(1)} %add.110), channel_id=1, source_target_pairs={{0,1},{1,0},{2,3},{3,2},{4,5},{5,4},{6,7},{7,6},{8,9},{9,8},{10,11... | collective-permute-start | bytes 165896 | tf_op jit(solution)/shard_map/ppermute | solution.py:40

commit v10 on v3

--- a/solution.py
+++ b/solution.py
@@ -2,6 +2,7 @@
 import jax.numpy as jnp
 from jax import lax
 from jax.sharding import PartitionSpec as P
+
 
 D = 8192
 BLK = 128
@@ -43,7 +44,7 @@
     return x
 
 
-def per_device(
+def device_step(
     activations, center_bias, encoder_weight, encoder_bias, decoder_weight, row_blocks, pick_offsets
 ):
     group_rows, feature_width = activations.shape
@@ -101,7 +102,7 @@
     bias_t = own_half(jnp.broadcast_to(encoder_bias[:, None], (owned_cols, slot_count)))
     pre_picked = summed + pick_rows(bias_t, offs_t)
     latent_t = spread_rows(pre_picked, offs_t).astype(jnp.bfloat16)
-    latent_wide_t = widen(latent_t)
+    latent_wide_t = lax.optimization_barrier(widen(latent_t))
     decoded = lax.dot_general(
         latent_wide_t, decoder_weight, (((0,), (0,)), ((), ())), preferred_element_type=jnp.float32
     ).astype(jnp.bfloat16)
@@ -149,7 +150,7 @@
 
 def solution(mesh):
     return jax.shard_map(
-        per_device,
+        device_step,
         mesh=mesh,
         in_specs=(
             P("lat", "row"),

time: 341 us -> 338 us (level)
  transfers between devices with their start and end apart: 9 -> 9, of which waited for: 9 -> 8; matrix products, arithmetic and copies ran while one was open for 2% -> 4% of each run, Pallas kernels for 0% -> 0%
where the time goes in v10:
time: 338 us; the launch traced here: 337 us
  waiting for transfers between devices  161 us (48%)
  blocking collectives  78.9 us (23%)
  starting transfers between devices  59.2 us (18%)
  matrix products  21.7 us (6%)
  other arithmetic  9.63 us (3%)
  local copies, waits for them, and re-layouts  5.37 us (2%)
    all_to_all x1, blocking collectives, device_step(): lax.all_to_all(decoded.reshape(owners, per_owner, feature_width), 'lat',...  78.9 us
    all_to_all x1, waiting for transfers between devices, device_step(): lax.all_to_all(out_error.reshape(owners, per_owner, feature_width), 'lat'...  72.4 us
    all_to_all x1, waiting for transfers between devices, device_step(): lax.all_to_all(outgoing.reshape(owners, per_owner, feature_width), 'lat',...  72 us
    ppermute x6, starting transfers between devices, butterfly_sum(): other = lax.ppermute(x, axis, perm=[(i, i ^ step) for i in range(size)])  35.2 us
    ppermute x6, waiting for transfers between devices, butterfly_sum(): other = lax.ppermute(x, axis, perm=[(i, i ^ step) for i in range(size)])  12.6 us
    all_to_all x1, starting transfers between devices, device_step(): lax.all_to_all(out_offs, 'lat', split_axis=0, concat_axis=0, tiled=True)  10.6 us
    all_to_all x1, starting transfers between devices, device_step(): lax.all_to_all(outgoing.reshape(owners, per_owner, feature_width), 'lat',...  7.57 us
  transfers between devices with their start and end apart: 9, of which 8 were waited for; matrix products, arithmetic and copies ran while one was open for 4% of the time, Pallas kernels for 0%

profile of v10, /device:TPU:6, one launch (start us, length us, event | category | flops | bytes accessed | tf_op | source)
XLA Modules:
  0.0 336.9 jit_solution(12224190296622507550)
XLA Ops:
  4.9 10.6 %all-to-all-start.1 = ((s32[64,1,192]{2,1,0:T(1,128)}), s32[64,1,192]{2,1,0:T(1,128)S(1)}, u32[]{:S(2)}, u32[]{:S(2)}) async-start(s32[64,1,192]{2,1,0:T(1,128)} %reshape.962), calls=%async_computation.1 | async-start | bytes 131072 | tf_op jit(solution)/shard_map/all_to_all | solution.py:73
  16.8 2.8 convolution_convert_fusion.2
  19.5 4.0 %all-to-all-done.1 = s32[64,1,192]{2,1,0:T(1,128)S(1)} async-done(((s32[64,1,192]{2,1,0:T(1,128)}), s32[64,1,192]{2,1,0:T(1,128)S(1)}, u32[]{:S(2)}, u32[]{:S(2)}) %all-to-all-start.1) | async-done | bytes 49184 | tf_op jit(solution)/shard_map/all_to_all | solution.py:73
  23.5 7.6 %all-to-all-start = ((bf16[64,24,1024]{2,1,0:T(8,128)(2,1)}), bf16[64,24,1024]{2,1,0:T(8,128)(2,1)}, u32[]{:S(2)}, u32[]{:S(2)}) async-start(bf16[64,24,1024]{2,1,0:T(8,128)(2,1)} %bitcast.51), calls=%async_computation | async-start | bytes 6291456 | tf_op jit(solution)/shard_map/all_to_all | solution.py:74
  32.9 72.0 %all-to-all-done = bf16[64,24,1024]{2,1,0:T(8,128)(2,1)} async-done(((bf16[64,24,1024]{2,1,0:T(8,128)(2,1)}), bf16[64,24,1024]{2,1,0:T(8,128)(2,1)}, u32[]{:S(2)}, u32[]{:S(2)}) %all-to-all-start) | async-done | bytes 3145760 | tf_op jit(solution)/shard_map/all_to_all | solution.py:74
  104.9 2.9 fusion.17
  108.2 1.5 select_reduce_fusion.2
  109.7 4.3 %collective-permute-start = (f32[8,1536]{1,0:T(8,128)S(1)}, f32[8,1536]{1,0:T(8,128)S(1)}, u32[]{:S(2)}, u32[]{:S(2)}) collective-permute-start(f32[8,1536]{1,0:T(8,128)S(1)} %get-tuple-element.40), channel_id=1, source_target_pairs={{0,1},{1,0},{2,3},{3,2},{4,5},{5,4},{6,7},{7,6},{8,9},{9,8},{10,11... | collective-permute-start | bytes 147464 | tf_op jit(solution)/shard_map/ppermute | solution.py:41
  114.0 2.1 collective-permute-done
  116.1 6.1 %collective-permute-start.1 = (f32[8,1536]{1,0:T(8,128)S(1)}, f32[8,1536]{1,0:T(8,128)S(1)}, u32[]{:S(2)}, u32[]{:S(2)}) collective-permute-start(f32[8,1536]{1,0:T(8,128)S(1)} %add.102), channel_id=1, source_target_pairs={{0,2},{1,3},{2,0},{3,1},{4,6},{5,7},{6,4},{7,5},{8,10},{9,11},{10,... | collective-permute-start | bytes 147464 | tf_op jit(solution)/shard_map/ppermute | solution.py:41
  122.2 2.0 collective-permute-done.1
  124.2 9.5 %collective-permute-start.2 = (f32[8,1536]{1,0:T(8,128)S(1)}, f32[8,1536]{1,0:T(8,128)S(1)}, u32[]{:S(2)}, u32[]{:S(2)}) collective-permute-start(f32[8,1536]{1,0:T(8,128)S(1)} %add.103), channel_id=1, source_target_pairs={{0,4},{1,5},{2,6},{3,7},{4,0},{5,1},{6,2},{7,3},{8,12},{9,13},{10,... | collective-permute-start | bytes 147464 | tf_op jit(solution)/shard_map/ppermute | solution.py:41
  137.9 78.9 %all_to_all.20 = bf16[64,24,1024]{2,1,0:T(8,128)(2,1)S(1)} all-to-all(bf16[64,24,1024]{2,1,0:T(8,128)(2,1)S(1)} %bitcast.50), channel_id=1, replica_groups=mesh['lat'=64,'row'=8] {'lat'}, dimensions={0} | all-to-all | bytes 6291456 | tf_op jit(solution)/shard_map/all_to_all | solution.py:109
  217.8 2.8 convolution_convert_fusion
  220.6 5.8 %all-to-all-start.3 = ((bf16[64,24,1024]{2,1,0:T(8,128)(2,1)}), bf16[64,24,1024]{2,1,0:T(8,128)(2,1)}, u32[]{:S(2)}, u32[]{:S(2)}) async-start(bf16[64,24,1024]{2,1,0:T(8,128)(2,1)} %bitcast.52), calls=%async_computation.3 | async-start | bytes 6291456 | tf_op jit(solution)/shard_map/all_to_all | solution.py:123
  227.7 72.4 %all-to-all-done.3 = bf16[64,24,1024]{2,1,0:T(8,128)(2,1)} async-done(((bf16[64,24,1024]{2,1,0:T(8,128)(2,1)}), bf16[64,24,1024]{2,1,0:T(8,128)(2,1)}, u32[]{:S(2)}, u32[]{:S(2)}) %all-to-all-start.3) | async-done | bytes 3145760 | tf_op jit(solution)/shard_map/all_to_all | solution.py:123
  300.1 2.9 fusion.18
  304.1 2.9 collective-permute-start.3
  307.1 3.6 %collective-permute-done.3 = f32[9,1536]{1,0:T(8,128)S(1)} collective-permute-done((f32[9,1536]{1,0:T(8,128)S(1)}, f32[9,1536]{1,0:T(8,128)S(1)}, u32[]{:S(2)}, u32[]{:S(2)}) %collective-permute-start.3) | collective-permute-done | bytes 55328 | tf_op jit(solution)/shard_map/ppermute | solution.py:41
  310.7 4.4 %collective-permute-start.4 = (f32[9,1536]{1,0:T(8,128)S(1)}, f32[9,1536]{1,0:T(8,128)S(1)}, u32[]{:S(2)}, u32[]{:S(2)}) collective-permute-start(f32[9,1536]{1,0:T(8,128)S(1)} %fusion.16), channel_id=1, source_target_pairs={{0,2},{1,3},{2,0},{3,1},{4,6},{5,7},{6,4},{7,5},{8,10},{9,11},{10,... | collective-permute-start | bytes 165896 | tf_op jit(solution)/shard_map/ppermute | solution.py:41
  315.1 4.0 %collective-permute-done.4 = f32[9,1536]{1,0:T(8,128)S(1)} collective-permute-done((f32[9,1536]{1,0:T(8,128)S(1)}, f32[9,1536]{1,0:T(8,128)S(1)}, u32[]{:S(2)}, u32[]{:S(2)}) %collective-permute-start.4) | collective-permute-done | bytes 55328 | tf_op jit(solution)/shard_map/ppermute | solution.py:41
  319.1 8.0 %collective-permute-start.5 = (f32[9,1536]{1,0:T(8,128)S(1)}, f32[9,1536]{1,0:T(8,128)S(1)}, u32[]{:S(2)}, u32[]{:S(2)}) collective-permute-start(f32[9,1536]{1,0:T(8,128)S(1)} %add.108), channel_id=1, source_target_pairs={{0,4},{1,5},{2,6},{3,7},{4,0},{5,1},{6,2},{7,3},{8,12},{9,13},{10,... | collective-permute-start | bytes 165896 | tf_op jit(solution)/shard_map/ppermute | solution.py:41
  327.1 3.7 %convolution_convert_fusion.3 = bf16[256,1024]{1,0:T(8,128)(2,1)} fusion(bf16[256,1536]{1,0:T(8,128)(2,1)S(1)} %compare_select_fusion.1, bf16[1536,1024]{1,0:T(8,128)(2,1)} %bitcast.15), kind=kOutput, calls=%fused_computation.20 | convolution fusion | flops 805568512 | bytes 4456448 | tf_op jit(solution)/shard_map/dot_general | solution.py:130
  333.1 3.7 %convolution_convert_fusion.4 = bf16[1024,256]{1,0:T(8,128)(2,1)} fusion(bf16[1536,1024]{1,0:T(8,128)(2,1)} %bitcast.4, bf16[256,1536]{1,0:T(8,128)(2,1)S(1)} %bitcast.57), kind=kOutput, calls=%fused_computation.21 | convolution fusion | flops 805568512 | bytes 4456448 | tf_op jit(solution)/shard_map/dot_general | solution.py:143
  (78 shorter events, 17.2 us)
Async XLA Ops:
  0.6 136.3 %copy-start = (bf16[256,1024]{1,0:T(8,128)(2,1)S(1)}, bf16[256,1024]{1,0:T(8,128)(2,1)}, u32[]{:S(2)}) copy-start(bf16[256,1024]{1,0:T(8,128)(2,1)} %param.13) | copy-start | bytes 1572868
  0.6 1.9 copy-start.2
  1.5 14.2 %copy-start.3 = (s32[192,4]{0,1:T(4,128)S(1)}, s32[192,4]{0,1:T(4,128)}, u32[]{:S(2)}) copy-start(s32[192,4]{0,1:T(4,128)} %param.14) | copy-start | bytes 9220
  1.9 14.9 %copy-start.1 = (f32[192,1024]{1,0:T(8,128)S(1)}, f32[192,1024]{1,0:T(8,128)}, u32[]{:S(2)}) copy-start(f32[192,1024]{1,0:T(8,128)} %param.9) | copy-start | bytes 2359300
  1.9 14.9 %copy-start.4 = (f32[1024]{0:T(1024)S(1)}, f32[1024]{0:T(1024)}, u32[]{:S(2)}) copy-start(f32[1024]{0:T(1024)} %param.10) | copy-start | bytes 12292
  4.9 18.6 %all-to-all-start.1 = ((s32[64,1,192]{2,1,0:T(1,128)}), s32[64,1,192]{2,1,0:T(1,128)S(1)}, u32[]{:S(2)}, u32[]{:S(2)}) async-start(s32[64,1,192]{2,1,0:T(1,128)} %reshape.962), calls=%async_computation.1 | async-start | bytes 131072 | tf_op jit(solution)/shard_map/all_to_all | solution.py:73
  23.5 81.3 %copy-start.6 = (bf16[1024,256]{1,0:T(8,128)(2,1)S(1)}, bf16[1024,256]{1,0:T(8,128)(2,1)}, u32[]{:S(2)}) copy-start(bf16[1024,256]{1,0:T(8,128)(2,1)} %param.11) | copy-start | bytes 1572868
  23.5 81.3 %all-to-all-start = ((bf16[64,24,1024]{2,1,0:T(8,128)(2,1)}), bf16[64,24,1024]{2,1,0:T(8,128)(2,1)}, u32[]{:S(2)}, u32[]{:S(2)}) async-start(bf16[64,24,1024]{2,1,0:T(8,128)(2,1)} %bitcast.51), calls=%async_computation | async-start | bytes 6291456 | tf_op jit(solution)/shard_map/all_to_all | solution.py:74
  104.9 2.9 copy-start.5
  109.7 6.3 %collective-permute-start = (f32[8,1536]{1,0:T(8,128)S(1)}, f32[8,1536]{1,0:T(8,128)S(1)}, u32[]{:S(2)}, u32[]{:S(2)}) collective-permute-start(f32[8,1536]{1,0:T(8,128)S(1)} %get-tuple-element.40), channel_id=1, source_target_pairs={{0,1},{1,0},{2,3},{3,2},{4,5},{5,4},{6,7},{7,6},{8,9},{9,8},{10,11... | collective-permute-start | bytes 147464 | tf_op jit(solution)/shard_map/ppermute | solution.py:41
  116.1 8.1 %collective-permute-start.1 = (f32[8,1536]{1,0:T(8,128)S(1)}, f32[8,1536]{1,0:T(8,128)S(1)}, u32[]{:S(2)}, u32[]{:S(2)}) collective-permute-start(f32[8,1536]{1,0:T(8,128)S(1)} %add.102), channel_id=1, source_target_pairs={{0,2},{1,3},{2,0},{3,1},{4,6},{5,7},{6,4},{7,5},{8,10},{9,11},{10,... | collective-permute-start | bytes 147464 | tf_op jit(solution)/shard_map/ppermute | solution.py:41
  124.2 11.8 %collective-permute-start.2 = (f32[8,1536]{1,0:T(8,128)S(1)}, f32[8,1536]{1,0:T(8,128)S(1)}, u32[]{:S(2)}, u32[]{:S(2)}) collective-permute-start(f32[8,1536]{1,0:T(8,128)S(1)} %add.103), channel_id=1, source_target_pairs={{0,4},{1,5},{2,6},{3,7},{4,0},{5,1},{6,2},{7,3},{8,12},{9,13},{10,... | collective-permute-start | bytes 147464 | tf_op jit(solution)/shard_map/ppermute | solution.py:41
  220.6 79.5 %all-to-all-start.3 = ((bf16[64,24,1024]{2,1,0:T(8,128)(2,1)}), bf16[64,24,1024]{2,1,0:T(8,128)(2,1)}, u32[]{:S(2)}, u32[]{:S(2)}) async-start(bf16[64,24,1024]{2,1,0:T(8,128)(2,1)} %bitcast.52), calls=%async_computation.3 | async-start | bytes 6291456 | tf_op jit(solution)/shard_map/all_to_all | solution.py:123
  304.1 6.5 %collective-permute-start.3 = (f32[9,1536]{1,0:T(8,128)S(1)}, f32[9,1536]{1,0:T(8,128)S(1)}, u32[]{:S(2)}, u32[]{:S(2)}) collective-permute-start(f32[9,1536]{1,0:T(8,128)S(1)} %select_maximum_fusion), channel_id=1, source_target_pairs={{0,1},{1,0},{2,3},{3,2},{4,5},{5,4},{6,7},{7,6},{8,9},{9,8},{10,11... | collective-permute-start | bytes 165896 | tf_op jit(solution)/shard_map/ppermute | solution.py:41
  310.7 8.5 %collective-permute-start.4 = (f32[9,1536]{1,0:T(8,128)S(1)}, f32[9,1536]{1,0:T(8,128)S(1)}, u32[]{:S(2)}, u32[]{:S(2)}) collective-permute-start(f32[9,1536]{1,0:T(8,128)S(1)} %fusion.16), channel_id=1, source_target_pairs={{0,2},{1,3},{2,0},{3,1},{4,6},{5,7},{6,4},{7,5},{8,10},{9,11},{10,... | collective-permute-start | bytes 165896 | tf_op jit(solution)/shard_map/ppermute | solution.py:41
  319.1 11.7 %collective-permute-start.5 = (f32[9,1536]{1,0:T(8,128)S(1)}, f32[9,1536]{1,0:T(8,128)S(1)}, u32[]{:S(2)}, u32[]{:S(2)}) collective-permute-start(f32[9,1536]{1,0:T(8,128)S(1)} %add.108), channel_id=1, source_target_pairs={{0,4},{1,5},{2,6},{3,7},{4,0},{5,1},{6,2},{7,3},{8,12},{9,13},{10,... | collective-permute-start | bytes 165896 | tf_op jit(solution)/shard_map/ppermute | solution.py:41

commit v11 on v10

--- a/solution.py
+++ b/solution.py
@@ -127,9 +127,18 @@
         concat_axis=0,
         tiled=True,
     ).reshape(slot_count, feature_width)
-    decoder_grad = lax.dot_general(
-        latent_wide_t, got_error, (((1,), (0,)), ((), ())), preferred_element_type=jnp.float32
-    ).astype(jnp.bfloat16)
+    halves = []
+    half = feature_width // 2
+    for lo in (0, half):
+        halves.append(
+            lax.dot_general(
+                latent_wide_t,
+                got_error[:, lo : lo + half],
+                (((1,), (0,)), ((), ())),
+                preferred_element_type=jnp.float32,
+            ).astype(jnp.bfloat16)
+        )
+    decoder_grad = jnp.concatenate(halves, axis=1)
     dlatent_t = lax.dot_general(
         decoder_weight, got_error, (((1,), (1,)), ((), ())), preferred_element_type=jnp.float32
     )

time: 338 us -> 337 us (level)
  transfers between devices with their start and end apart: 9 -> 9, of which waited for: 8 -> 9; matrix products, arithmetic and copies ran while one was open for 4% -> 4% of each run, Pallas kernels for 0% -> 0%
where the time goes in v11:
time: 337 us; the launch traced here: 336 us
  waiting for transfers between devices  159 us (47%)
  blocking collectives  78.9 us (23%)
  starting transfers between devices  59.2 us (18%)
  matrix products  22 us (7%)
  other arithmetic  10.5 us (3%)
  local copies, waits for them, and re-layouts  5.37 us (2%)
    all_to_all x1, blocking collectives, device_step(): lax.all_to_all(decoded.reshape(owners, per_owner, feature_width), 'lat',...  78.9 us
    all_to_all x1, waiting for transfers between devices, device_step(): lax.all_to_all(out_error.reshape(owners, per_owner, feature_width), 'lat'...  72.4 us
    all_to_all x1, waiting for transfers between devices, device_step(): lax.all_to_all(outgoing.reshape(owners, per_owner, feature_width), 'lat',...  72 us
    ppermute x6, starting transfers between devices, butterfly_sum(): other = lax.ppermute(x, axis, perm=[(i, i ^ step) for i in range(size)])  35.2 us
    ppermute x6, waiting for transfers between devices, butterfly_sum(): other = lax.ppermute(x, axis, perm=[(i, i ^ step) for i in range(size)])  10.8 us
    all_to_all x1, starting transfers between devices, device_step(): lax.all_to_all(out_offs, 'lat', split_axis=0, concat_axis=0, tiled=True)  10.6 us
    all_to_all x1, starting transfers between devices, device_step(): lax.all_to_all(outgoing.reshape(owners, per_owner, feature_width), 'lat',...  7.57 us
  transfers between devices with their start and end apart: 9, of which 9 were waited for; matrix products, arithmetic and copies ran while one was open for 4% of the time, Pallas kernels for 0%

profile of v11, /device:TPU:6, one launch (start us, length us, event | category | flops | bytes accessed | tf_op | source)
XLA Modules:
  0.0 336.3 jit_solution(13715129893228703027)
XLA Ops:
  4.9 10.6 %all-to-all-start.1 = ((s32[64,1,192]{2,1,0:T(1,128)}), s32[64,1,192]{2,1,0:T(1,128)S(1)}, u32[]{:S(2)}, u32[]{:S(2)}) async-start(s32[64,1,192]{2,1,0:T(1,128)} %reshape.962), calls=%async_computation.1 | async-start | bytes 131072 | tf_op jit(solution)/shard_map/all_to_all | solution.py:73
  16.8 2.8 convolution_convert_fusion.2
  19.5 4.0 %all-to-all-done.1 = s32[64,1,192]{2,1,0:T(1,128)S(1)} async-done(((s32[64,1,192]{2,1,0:T(1,128)}), s32[64,1,192]{2,1,0:T(1,128)S(1)}, u32[]{:S(2)}, u32[]{:S(2)}) %all-to-all-start.1) | async-done | bytes 49184 | tf_op jit(solution)/shard_map/all_to_all | solution.py:73
  23.5 7.6 %all-to-all-start = ((bf16[64,24,1024]{2,1,0:T(8,128)(2,1)}), bf16[64,24,1024]{2,1,0:T(8,128)(2,1)}, u32[]{:S(2)}, u32[]{:S(2)}) async-start(bf16[64,24,1024]{2,1,0:T(8,128)(2,1)} %bitcast.51), calls=%async_computation | async-start | bytes 6291456 | tf_op jit(solution)/shard_map/all_to_all | solution.py:74
  32.9 72.0 %all-to-all-done = bf16[64,24,1024]{2,1,0:T(8,128)(2,1)} async-done(((bf16[64,24,1024]{2,1,0:T(8,128)(2,1)}), bf16[64,24,1024]{2,1,0:T(8,128)(2,1)}, u32[]{:S(2)}, u32[]{:S(2)}) %all-to-all-start) | async-done | bytes 3145760 | tf_op jit(solution)/shard_map/all_to_all | solution.py:74
  104.9 2.9 fusion.27
  109.7 4.3 %collective-permute-start = (f32[8,1536]{1,0:T(8,128)S(1)}, f32[8,1536]{1,0:T(8,128)S(1)}, u32[]{:S(2)}, u32[]{:S(2)}) collective-permute-start(f32[8,1536]{1,0:T(8,128)S(1)} %get-tuple-element.40), channel_id=1, source_target_pairs={{0,1},{1,0},{2,3},{3,2},{4,5},{5,4},{6,7},{7,6},{8,9},{9,8},{10,11... | collective-permute-start | bytes 147464 | tf_op jit(solution)/shard_map/ppermute | solution.py:41
  114.0 2.1 collective-permute-done
  116.1 6.1 %collective-permute-start.1 = (f32[8,1536]{1,0:T(8,128)S(1)}, f32[8,1536]{1,0:T(8,128)S(1)}, u32[]{:S(2)}, u32[]{:S(2)}) collective-permute-start(f32[8,1536]{1,0:T(8,128)S(1)} %add.102), channel_id=1, source_target_pairs={{0,2},{1,3},{2,0},{3,1},{4,6},{5,7},{6,4},{7,5},{8,10},{9,11},{10,... | collective-permute-start | bytes 147464 | tf_op jit(solution)/shard_map/ppermute | solution.py:41
  122.2 2.0 collective-permute-done.1
  124.2 9.5 %collective-permute-start.2 = (f32[8,1536]{1,0:T(8,128)S(1)}, f32[8,1536]{1,0:T(8,128)S(1)}, u32[]{:S(2)}, u32[]{:S(2)}) collective-permute-start(f32[8,1536]{1,0:T(8,128)S(1)} %add.103), channel_id=1, source_target_pairs={{0,4},{1,5},{2,6},{3,7},{4,0},{5,1},{6,2},{7,3},{8,12},{9,13},{10,... | collective-permute-start | bytes 147464 | tf_op jit(solution)/shard_map/ppermute | solution.py:41
  137.9 78.9 %all_to_all.20 = bf16[64,24,1024]{2,1,0:T(8,128)(2,1)S(1)} all-to-all(bf16[64,24,1024]{2,1,0:T(8,128)(2,1)S(1)} %bitcast.50), channel_id=1, replica_groups=mesh['lat'=64,'row'=8] {'lat'}, dimensions={0} | all-to-all | bytes 6291456 | tf_op jit(solution)/shard_map/all_to_all | solution.py:109
  217.8 2.8 convolution_convert_fusion
  220.6 5.8 %all-to-all-start.3 = ((bf16[64,24,1024]{2,1,0:T(8,128)(2,1)}), bf16[64,24,1024]{2,1,0:T(8,128)(2,1)}, u32[]{:S(2)}, u32[]{:S(2)}) async-start(bf16[64,24,1024]{2,1,0:T(8,128)(2,1)} %bitcast.52), calls=%async_computation.3 | async-start | bytes 6291456 | tf_op jit(solution)/shard_map/all_to_all | solution.py:123
  227.7 72.4 %all-to-all-done.3 = bf16[64,24,1024]{2,1,0:T(8,128)(2,1)} async-done(((bf16[64,24,1024]{2,1,0:T(8,128)(2,1)}), bf16[64,24,1024]{2,1,0:T(8,128)(2,1)}, u32[]{:S(2)}, u32[]{:S(2)}) %all-to-all-start.3) | async-done | bytes 3145760 | tf_op jit(solution)/shard_map/all_to_all | solution.py:123
  300.1 2.9 fusion.28
  304.1 2.9 collective-permute-start.3
  307.1 2.0 fusion.9
  310.7 4.4 %collective-permute-start.4 = (f32[9,1536]{1,0:T(8,128)S(1)}, f32[9,1536]{1,0:T(8,128)S(1)}, u32[]{:S(2)}, u32[]{:S(2)}) collective-permute-start(f32[9,1536]{1,0:T(8,128)S(1)} %fusion.26), channel_id=1, source_target_pairs={{0,2},{1,3},{2,0},{3,1},{4,6},{5,7},{6,4},{7,5},{8,10},{9,11},{10,... | collective-permute-start | bytes 165896 | tf_op jit(solution)/shard_map/ppermute | solution.py:41
  315.1 2.0 fusion.12
  317.1 2.1 collective-permute-done.4
  319.1 8.0 %collective-permute-start.5 = (f32[9,1536]{1,0:T(8,128)S(1)}, f32[9,1536]{1,0:T(8,128)S(1)}, u32[]{:S(2)}, u32[]{:S(2)}) collective-permute-start(f32[9,1536]{1,0:T(8,128)S(1)} %add.108), channel_id=1, source_target_pairs={{0,4},{1,5},{2,6},{3,7},{4,0},{5,1},{6,2},{7,3},{8,12},{9,13},{10,... | collective-permute-start | bytes 165896 | tf_op jit(solution)/shard_map/ppermute | solution.py:41
  328.0 2.2 collective-permute-done.5
  332.5 3.7 %convolution_convert_fusion.3 = bf16[1024,256]{1,0:T(8,128)(2,1)} fusion(bf16[1536,1024]{1,0:T(8,128)(2,1)} %bitcast.4, bf16[256,1536]{1,0:T(8,128)(2,1)S(1)} %bitcast.57), kind=kOutput, calls=%fused_computation.24 | convolution fusion | flops 805568512 | bytes 4456448 | tf_op jit(solution)/shard_map/dot_general | solution.py:152
  (80 shorter events, 21.2 us)
Async XLA Ops:
  0.6 136.3 %copy-start = (bf16[256,1024]{1,0:T(8,128)(2,1)S(1)}, bf16[256,1024]{1,0:T(8,128)(2,1)}, u32[]{:S(2)}) copy-start(bf16[256,1024]{1,0:T(8,128)(2,1)} %param.13) | copy-start | bytes 1572868
  0.6 1.9 copy-start.2
  1.5 14.2 %copy-start.3 = (s32[192,4]{0,1:T(4,128)S(1)}, s32[192,4]{0,1:T(4,128)}, u32[]{:S(2)}) copy-start(s32[192,4]{0,1:T(4,128)} %param.14) | copy-start | bytes 9220
  1.9 14.9 %copy-start.1 = (f32[192,1024]{1,0:T(8,128)S(1)}, f32[192,1024]{1,0:T(8,128)}, u32[]{:S(2)}) copy-start(f32[192,1024]{1,0:T(8,128)} %param.9) | copy-start | bytes 2359300
  1.9 14.9 %copy-start.4 = (f32[1024]{0:T(1024)S(1)}, f32[1024]{0:T(1024)}, u32[]{:S(2)}) copy-start(f32[1024]{0:T(1024)} %param.10) | copy-start | bytes 12292
  4.9 18.6 %all-to-all-start.1 = ((s32[64,1,192]{2,1,0:T(1,128)}), s32[64,1,192]{2,1,0:T(1,128)S(1)}, u32[]{:S(2)}, u32[]{:S(2)}) async-start(s32[64,1,192]{2,1,0:T(1,128)} %reshape.962), calls=%async_computation.1 | async-start | bytes 131072 | tf_op jit(solution)/shard_map/all_to_all | solution.py:73
  23.5 81.3 %copy-start.6 = (bf16[1024,256]{1,0:T(8,128)(2,1)S(1)}, bf16[1024,256]{1,0:T(8,128)(2,1)}, u32[]{:S(2)}) copy-start(bf16[1024,256]{1,0:T(8,128)(2,1)} %param.11) | copy-start | bytes 1572868
  23.5 81.3 %all-to-all-start = ((bf16[64,24,1024]{2,1,0:T(8,128)(2,1)}), bf16[64,24,1024]{2,1,0:T(8,128)(2,1)}, u32[]{:S(2)}, u32[]{:S(2)}) async-start(bf16[64,24,1024]{2,1,0:T(8,128)(2,1)} %bitcast.51), calls=%async_computation | async-start | bytes 6291456 | tf_op jit(solution)/shard_map/all_to_all | solution.py:74
  104.9 2.9 copy-start.5
  109.7 6.3 %collective-permute-start = (f32[8,1536]{1,0:T(8,128)S(1)}, f32[8,1536]{1,0:T(8,128)S(1)}, u32[]{:S(2)}, u32[]{:S(2)}) collective-permute-start(f32[8,1536]{1,0:T(8,128)S(1)} %get-tuple-element.40), channel_id=1, source_target_pairs={{0,1},{1,0},{2,3},{3,2},{4,5},{5,4},{6,7},{7,6},{8,9},{9,8},{10,11... | collective-permute-start | bytes 147464 | tf_op jit(solution)/shard_map/ppermute | solution.py:41
  116.1 8.1 %collective-permute-start.1 = (f32[8,1536]{1,0:T(8,128)S(1)}, f32[8,1536]{1,0:T(8,128)S(1)}, u32[]{:S(2)}, u32[]{:S(2)}) collective-permute-start(f32[8,1536]{1,0:T(8,128)S(1)} %add.102), channel_id=1, source_target_pairs={{0,2},{1,3},{2,0},{3,1},{4,6},{5,7},{6,4},{7,5},{8,10},{9,11},{10,... | collective-permute-start | bytes 147464 | tf_op jit(solution)/shard_map/ppermute | solution.py:41
  124.2 11.8 %collective-permute-start.2 = (f32[8,1536]{1,0:T(8,128)S(1)}, f32[8,1536]{1,0:T(8,128)S(1)}, u32[]{:S(2)}, u32[]{:S(2)}) collective-permute-start(f32[8,1536]{1,0:T(8,128)S(1)} %add.103), channel_id=1, source_target_pairs={{0,4},{1,5},{2,6},{3,7},{4,0},{5,1},{6,2},{7,3},{8,12},{9,13},{10,... | collective-permute-start | bytes 147464 | tf_op jit(solution)/shard_map/ppermute | solution.py:41
  220.6 79.5 %all-to-all-start.3 = ((bf16[64,24,1024]{2,1,0:T(8,128)(2,1)}), bf16[64,24,1024]{2,1,0:T(8,128)(2,1)}, u32[]{:S(2)}, u32[]{:S(2)}) async-start(bf16[64,24,1024]{2,1,0:T(8,128)(2,1)} %bitcast.52), calls=%async_computation.3 | async-start | bytes 6291456 | tf_op jit(solution)/shard_map/all_to_all | solution.py:123
  304.1 6.5 %collective-permute-start.3 = (f32[9,1536]{1,0:T(8,128)S(1)}, f32[9,1536]{1,0:T(8,128)S(1)}, u32[]{:S(2)}, u32[]{:S(2)}) collective-permute-start(f32[9,1536]{1,0:T(8,128)S(1)} %select_maximum_fusion), channel_id=1, source_target_pairs={{0,1},{1,0},{2,3},{3,2},{4,5},{5,4},{6,7},{7,6},{8,9},{9,8},{10,11... | collective-permute-start | bytes 165896 | tf_op jit(solution)/shard_map/ppermute | solution.py:41
  310.7 8.5 %collective-permute-start.4 = (f32[9,1536]{1,0:T(8,128)S(1)}, f32[9,1536]{1,0:T(8,128)S(1)}, u32[]{:S(2)}, u32[]{:S(2)}) collective-permute-start(f32[9,1536]{1,0:T(8,128)S(1)} %fusion.26), channel_id=1, source_target_pairs={{0,2},{1,3},{2,0},{3,1},{4,6},{5,7},{6,4},{7,5},{8,10},{9,11},{10,... | collective-permute-start | bytes 165896 | tf_op jit(solution)/shard_map/ppermute | solution.py:41
  319.1 11.1 %collective-permute-start.5 = (f32[9,1536]{1,0:T(8,128)S(1)}, f32[9,1536]{1,0:T(8,128)S(1)}, u32[]{:S(2)}, u32[]{:S(2)}) collective-permute-start(f32[9,1536]{1,0:T(8,128)S(1)} %add.108), channel_id=1, source_target_pairs={{0,4},{1,5},{2,6},{3,7},{4,0},{5,1},{6,2},{7,3},{8,12},{9,13},{10,... | collective-permute-start | bytes 165896 | tf_op jit(solution)/shard_map/ppermute | solution.py:41
